TPU v7x, 32 devices: a whole 2x2x4 slice. The times are simulated.
32 devices in a mesh: tensor: 4 (over y, x), context: 2 (over core), dp: 4 (over z).
Axes of the slice: x: 2, y: 2, z: 4, core: 2. Of those that a mesh axis runs over, the one named last changes fastest.
Arguments:
- q_pre: bfloat16 [4, 2, 128, 2048], P('dp', 'context', None, 'tensor'), may hold values from -6 to 6
- k_pre: bfloat16 [4, 2, 128, 256], P('dp', 'context'), may hold values from -6 to 6
- values: bfloat16 [4, 2, 128, 256], P('dp', 'context'), may hold values from -6 to 6
- cotangent: bfloat16 [4, 2, 128, 4096], P('dp', 'context', 'tensor'), may hold values from -6 to 6
- out_weight: bfloat16 [2048, 4096], P('tensor'), may hold values from -0.125 to 0.125
- q_gain: float32 [128], replicated, may hold values from 0.5 to 6
- k_gain: float32 [128], replicated, may hold values from 0.5 to 6
- block_position: int32 [4, 2], P('dp'), may hold values from 0 to 1, each once within a row
Outputs:
- d_queries: bfloat16 [4, 2, 128, 2048], P('dp', 'context', None, 'tensor')
- d_keys: bfloat16 [4, 2, 128, 256], P('dp', 'context', None, 'tensor')
- d_values: bfloat16 [4, 2, 128, 256], P('dp', 'context', None, 'tensor')
- d_q_gain: float32 [128], replicated
- d_k_gain: float32 [128], replicated
Inputs may be any that keep to these rules, and one draw needn't show every extreme that they name: Each row of block_position is a permutation of the 2 blocks.
All inputs are finite; a program needn't handle non-finite values.
Results may differ from a plain program's by a relative error of at most 0.007.
The roundings to bfloat16 on the way count: a program that leaves them out, or rounds other values in their place, can miss the bound.
Values may be sent and summed in bfloat16 or wider, within the bound.
No kernel may reach another device: no remote copies, remote signals or barrier semaphores. Data moves between devices by JAX's collectives and lax.ppermute only.
A program may use at most 64 MiB of HBM per device.

v0:
```python
import math

import jax
import jax.numpy as jnp
from jax import lax
from jax.sharding import PartitionSpec as P

EPS = 1e-06


def from_partner(value, axis, bit):
    mask = 2**bit
    pairs = [(source, source ^ mask) for source in range(lax.axis_size(axis))]
    return lax.ppermute(value, axis, pairs)


def normalize(rows_in):
    inverse = lax.rsqrt(jnp.mean(rows_in * rows_in, axis=-1, keepdims=True) + EPS)
    return (rows_in * inverse, inverse)


def norm_backward(grad_norm, unit_rows, inverse, gain):
    scaled = grad_norm * gain
    return inverse * (scaled - unit_rows * jnp.mean(scaled * unit_rows, axis=-1, keepdims=True))


def softmax_rows(scores, visible):
    scores = jnp.where(visible[None], scores, -jnp.inf)
    row_max = jnp.max(scores, axis=-1, keepdims=True)
    exponent = jnp.exp(scores - row_max)
    return exponent / jnp.sum(exponent, axis=-1, keepdims=True)


def dense_block(query_norm, grad_attn, key_norm, value_rows, visible, score_scale):
    scores = (
        jnp.einsum("qhd,kd->hqk", query_norm, key_norm, preferred_element_type=jnp.float32)
        * score_scale
    )
    probabilities = softmax_rows(scores, visible)
    grad_prob = jnp.einsum("qhd,kd->hqk", grad_attn, value_rows, preferred_element_type=jnp.float32)
    row_delta = jnp.sum(probabilities * grad_prob, axis=-1, keepdims=True)
    grad_score = (probabilities * (grad_prob - row_delta) * score_scale).astype(jnp.bfloat16)
    prob_low = probabilities.astype(jnp.bfloat16)
    grad_query = jnp.einsum("hqk,kd->qhd", grad_score, key_norm, preferred_element_type=jnp.float32)
    grad_key = jnp.einsum("hqk,qhd->kd", grad_score, query_norm, preferred_element_type=jnp.float32)
    grad_value = jnp.einsum("hqk,qhd->kd", prob_low, grad_attn, preferred_element_type=jnp.float32)
    return (grad_query, grad_key, grad_value)


def shards(q_pre, k_pre, values, cotangent, out_weight, q_gain, k_gain, block_position):
    tensor_pos = lax.axis_index("tensor")
    context_pos = lax.axis_index("context")
    shard_count = lax.axis_size("context")
    seq_local = q_pre.shape[0]
    block_rows = q_pre.shape[2]
    head_size = q_gain.shape[0]
    head_count = q_pre.shape[3] // head_size
    kv_column = tensor_pos // 2 * head_size
    own_keys = lax.dynamic_slice_in_dim(k_pre[:, 0], kv_column, head_size, 2)
    own_values = lax.dynamic_slice_in_dim(values[:, 0], kv_column, head_size, 2)
    all_keys, all_values = (
        lax.all_gather(own_keys, "context", axis=1, tiled=True),
        lax.all_gather(own_values, "context", axis=1, tiled=True),
    )
    product = lax.dot_general(
        lax.all_gather(cotangent[:, 0], "tensor", axis=1, tiled=True),
        out_weight,
        (((2,), (1,)), ((), ())),
        preferred_element_type=jnp.float32,
    )
    grad_attn_all = product.astype(jnp.bfloat16)
    grad_attn_all = grad_attn_all.reshape(seq_local, block_rows, head_count, head_size)
    offsets = jnp.arange(block_rows, dtype=jnp.int32)
    score_scale = 1.0 / math.sqrt(head_size)
    block_order = block_position[0]
    own_block = jnp.sum(jnp.where(jnp.arange(shard_count) == context_pos, block_order, 0))
    query_positions = own_block * block_rows + offsets
    key_positions = (block_order[:, None] * block_rows + offsets[None, :]).reshape(
        shard_count * block_rows
    )
    visible = key_positions[None, :] <= query_positions[:, None]
    query_unit, query_inverse = normalize(
        q_pre[0, 0].reshape(block_rows, head_count, head_size).astype(jnp.float32)
    )
    query_norm = (query_unit * q_gain).astype(jnp.bfloat16)
    key_unit, key_inverse = normalize(all_keys[0].astype(jnp.float32))
    key_norm = (key_unit * k_gain).astype(jnp.bfloat16)
    value_seq = all_values[0]
    grad_attn = grad_attn_all[0]
    query_grads = []
    key_total = jnp.zeros((shard_count * block_rows, head_size), jnp.float32)
    value_total = jnp.zeros((shard_count * block_rows, head_size), jnp.float32)
    for start_head in range(0, head_count, 2):
        pair_query = query_norm[:, start_head : start_head + 2]
        pair_grad = grad_attn[:, start_head : start_head + 2]
        grad_query, grad_key, grad_value = dense_block(
            pair_query, pair_grad, key_norm, value_seq, visible, score_scale
        )
        query_grads.append(grad_query)
        key_total = key_total + grad_key
        value_total = value_total + grad_value
    grad_qn = jnp.concatenate(query_grads, axis=1)
    d_query_list = [norm_backward(grad_qn, query_unit, query_inverse, q_gain).astype(jnp.bfloat16)]
    gain_query_part = jnp.sum(grad_qn * query_unit, axis=(0, 1))
    partial_list = [jnp.concatenate([key_total, value_total], axis=1)]
    partials = jnp.stack(partial_list, axis=0)
    own_sums = lax.psum_scatter(partials, "context", scatter_dimension=1, tiled=True)
    block_totals = own_sums + from_partner(own_sums.astype(jnp.bfloat16), "tensor", 0).astype(
        own_sums.dtype
    )
    own_unit, own_inverse = normalize(own_keys.astype(jnp.float32))
    grad_kn = block_totals[:, :, :head_size]
    d_key_full = norm_backward(grad_kn, own_unit, own_inverse, k_gain)
    gain_key_part = 0.5 * jnp.sum(grad_kn * own_unit, axis=(0, 1))
    half_size = head_size // 2
    half_start = tensor_pos % 2 * half_size
    d_key_half = lax.dynamic_slice_in_dim(d_key_full, half_start, half_size, 2).astype(jnp.bfloat16)
    d_value_half = lax.dynamic_slice_in_dim(
        block_totals[:, :, head_size:], half_start, half_size, 2
    ).astype(jnp.bfloat16)
    gain_query, gain_key = lax.psum((gain_query_part, gain_key_part), ("tensor", "context", "dp"))
    d_query = jnp.stack(d_query_list, axis=0)
    return (
        d_query.reshape(seq_local, 1, block_rows, head_count * head_size),
        d_key_half.reshape(seq_local, 1, block_rows, half_size),
        d_value_half.reshape(seq_local, 1, block_rows, half_size),
        gain_query,
        gain_key,
    )


def solution(mesh):
    placed = (
        P("dp", "context", None, "tensor"),
        P("dp", "context", None, None),
        P("dp", "context", None, None),
        P("dp", "context", "tensor", None),
        P("tensor", None),
        P(),
        P(),
        P("dp", None),
    )
    return jax.shard_map(
        shards,
        mesh=mesh,
        in_specs=placed,
        out_specs=(
            P("dp", "context", None, "tensor"),
            P("dp", "context", None, "tensor"),
            P("dp", "context", None, "tensor"),
            P(),
            P(),
        ),
        check_vma=False,
    )
```

profile of v0, /device:TPU:0, one launch (start us, length us, event | category | flops | bytes accessed | tf_op | source)
XLA Modules:
  0.0 109.1 jit_solution(12924287295462070317)
XLA Ops:
  7.2 0.7 all-gather.5.cloned.1.call-update
  8.0 1.0 copy.53
  9.3 2.0 %all-gather = bf16[1,1,256,128]{2,3,1,0:T(8,128)(2,1)S(1)} all-gather(bf16[1,1,128,128]{2,3,1,0:T(8,128)(2,1)S(1)} %copy.91), channel_id=2, replica_groups=mesh['tensor'=4,'context'=2,'dp'=4] {'context'}, dimensions={2}, use_global_device_ids=true | all-gather | bytes 98304 | tf_op jit(solution)/shard_map/all_gather | solution.py:62
  11.4 1.3 %bitcast_multiply_fusion = (s32[2]{0:T(128)S(1)}, s32[]{:T(128)}) fusion(s32[1,2]{1,0:T(1,128)} %param.15, s32[]{:T(128)S(6)} %axis_index.28), kind=kLoop, calls=%fused_computation.96 | loop fusion | flops 7 | bytes 24 | tf_op jit(solution)/shard_map/mul | solution.py:78
  13.5 0.8 constant_dynamic-slice_fusion
  14.2 1.8 %all-gather.1 = bf16[1,1,256,128]{3,2,1,0:T(8,128)(2,1)S(1)} all-gather(bf16[1,1,128,128]{3,2,1,0:T(8,128)(2,1)S(1)} %constant_dynamic-slice_fusion), channel_id=3, replica_groups=mesh['tensor'=4,'context'=2,'dp'=4] {'context'}, dimensions={2}, use_global_device_ids=true | all-gather | bytes 98304 | tf_op jit(solution)/shard_map/all_gather | solution.py:63
  16.1 0.7 broadcast_bitcast_fusion
  16.9 0.8 multiply_convert_fusion.1
  17.7 1.0 fusion.95
  18.7 1.0 fusion.100
  19.7 19.4 %all-gather.5.cloned.1.call-done = bf16[1,1,128,4096]{3,2,1,0:T(8,128)(2,1)} async-done(((bf16[1,1,32,4096]{3,2,1,0:T(8,128)(2,1)}), bf16[1,1,128,4096]{3,2,1,0:T(8,128)(2,1)}) %all-gather.5.cloned.1.call-update) | async-done | bytes 1048592 | tf_op jit(solution)/shard_map/all_gather | solution.py:66
  39.1 4.0 %convolution_convert_fusion = bf16[128,512]{1,0:T(8,128)(2,1)S(1)} fusion(bf16[512,4096]{1,0:T(8,128)(2,1)} %param.12, bf16[1,1,128,4096]{3,2,1,0:T(8,128)(2,1)} %all-gather.5.cloned.1.call-done), kind=kOutput, calls=%fused_computation.24 | convolution fusion | flops 536936448 | bytes 5373952 | tf_op jit(solution)/shard_map/dot_general | solution.py:65
  43.3 0.2 convolution_bitcast_fusion
  43.5 0.2 convolution_bitcast_fusion.2
  43.7 0.3 convolution_bitcast_fusion.4
  44.0 0.3 convolution_bitcast_fusion.6
  44.3 0.2 convolution_bitcast_fusion.1
  44.5 0.3 convolution_bitcast_fusion.7
  44.8 0.3 fusion.20
  45.0 0.6 fusion.21
  45.6 0.7 maximum_bitcast_fusion
  46.4 0.2 pad_maximum_fusion
  46.8 0.3 multiply_reduce_fusion.2
  47.1 0.8 copy.74
  47.8 6.4 %reduce-scatter.2.cloned.1.call-done = f32[1,128,256]{1,2,0:T(8,128)} async-done(((f32[1,256,256]{1,2,0:T(8,128)}), f32[1,128,256]{1,2,0:T(8,128)}) %reduce-scatter.2.cloned.1.call-update) | async-done | bytes 131088 | tf_op jit(solution)/shard_map/reduce_scatter | solution.py:107
  54.2 0.9 convert_element_type.95
  55.2 1.7 %collective-permute-start = (bf16[1,128,256]{1,2,0:T(8,128)(2,1)S(1)}, bf16[1,128,256]{1,2,0:T(8,128)(2,1)S(1)}, u32[]{:S(2)}, u32[]{:S(2)}) collective-permute-start(bf16[1,128,256]{1,2,0:T(8,128)(2,1)S(1)} %convert_element_type.95), channel_id=1, source_target_pairs={{0,8},{8,0},{16,24},{24,16},{1,9},{9,1},{17,25},{25,17},{2,10},{10... | collective-permute-start | bytes 196616 | tf_op jit(solution)/shard_map/ppermute | solution.py:14
  56.8 2.6 %collective-permute-done = bf16[1,128,256]{1,2,0:T(8,128)(2,1)S(1)} collective-permute-done((bf16[1,128,256]{1,2,0:T(8,128)(2,1)S(1)}, bf16[1,128,256]{1,2,0:T(8,128)(2,1)S(1)}, u32[]{:S(2)}, u32[]{:S(2)}) %collective-permute-start) | collective-permute-done | bytes 65568 | tf_op jit(solution)/shard_map/ppermute | solution.py:14
  59.4 0.9 convert_add_fusion
  60.5 40.5 %all-reduce = (f32[128]{0:T(128)}, f32[128]{0:T(128)}) all-reduce(f32[128]{0:T(128)S(1)} %bitcast_reduce_fusion, f32[128]{0:T(128)S(1)} %broadcast_multiply_fusion.1), channel_id=1, replica_groups=mesh['tensor'=4,'context'=2,'dp'=4] {'tensor','context','dp'}, use_global_device_ids=true, to_apply=%region_15.16 | all-reduce | flops 256 | bytes 2048 | tf_op jit(solution)/shard_map/psum | solution.py:121
  101.0 0.6 fusion.54
  101.6 0.6 fusion.55
  (32 shorter events, 1.1 us)
Async XLA Ops:
  7.2 2.0 %copy-start = (bf16[1,1,128,256]{3,2,1,0:T(8,128)(2,1)S(1)}, bf16[1,1,128,256]{3,2,1,0:T(8,128)(2,1)}, u32[]{:S(2)}) copy-start(bf16[1,1,128,256]{3,2,1,0:T(8,128)(2,1)} %param.9) | copy-start | bytes 196612
  7.2 31.9 %all-gather.5.cloned.1.call-start = ((), (), s32[]{:S(2)}) async-start(), calls=%async_computation.2 | async-start | bytes 1310720 | tf_op jit(solution)/shard_map/all_gather | solution.py:66
  7.9 46.3 %reduce-scatter.2.cloned.1.call-start = ((), (), s32[]{:S(2)}) async-start(), calls=%async_computation.1 | async-start | bytes 393216 | tf_op jit(solution)/shard_map/reduce_scatter | solution.py:107
  19.7 24.2 %copy-start.2 = (f32[128]{0:T(128)S(1)}, f32[128]{0:T(128)}, u32[]{:S(2)}) copy-start(f32[128]{0:T(128)} %param.14) | copy-start | bytes 1540
  43.5 2.9 %copy-start.1 = (f32[128]{0:T(128)S(1)}, f32[128]{0:T(128)}, u32[]{:S(2)}) copy-start(f32[128]{0:T(128)} %param.13) | copy-start | bytes 1540
  55.2 4.3 %collective-permute-start = (bf16[1,128,256]{1,2,0:T(8,128)(2,1)S(1)}, bf16[1,128,256]{1,2,0:T(8,128)(2,1)S(1)}, u32[]{:S(2)}, u32[]{:S(2)}) collective-permute-start(bf16[1,128,256]{1,2,0:T(8,128)(2,1)S(1)} %convert_element_type.95), channel_id=1, source_target_pairs={{0,8},{8,0},{16,24},{24,16},{1,9},{9,1},{17,25},{25,17},{2,10},{10... | collective-permute-start | bytes 196616 | tf_op jit(solution)/shard_map/ppermute | solution.py:14
Sparse Core Ops, SparseCore 0:
  9.8 29.2 all-gather.4
  46.5 7.7 reduce-scatter.1
where the time goes:
time: 109 us
  blocking collectives  44.3 us (41%)
  waiting for transfers between devices  29.1 us (27%)
  between operations  14.9 us (14%)
  matrix products  8.39 us (8%)
  other arithmetic  6.22 us (6%)
  local copies, waits for them, and re-layouts  4.4 us (4%)
  starting transfers between devices  1.74 us (2%)
    psum x1, blocking collectives, shards(): lax.psum((gain_query_part, gain_key_part), ('tensor', 'context', 'dp'))  40.5 us
    all_gather x1, waiting for transfers between devices, shards(): lax.all_gather(cotangent[:, 0], 'tensor', axis=1, tiled=True)  19.4 us
    reduce_scatter x1, waiting for transfers between devices, shards(): lax.psum_scatter(partials, 'context', scatter_dimension=1, tiled=True)  6.4 us
    dot_general x1, matrix products, shards(): lax.dot_general(lax.all_gather(cotangent[:, 0], 'tensor', axis=1, tiled=T...  4.04 us
    ppermute x1, waiting for transfers between devices, from_partner(): return lax.ppermute(value, axis, pairs)  2.61 us
  transfers between devices with their start and end apart: 3, of which 3 were waited for; matrix products, arithmetic and copies ran while one was open for 8% of the time, Pallas kernels for 0%

commit v1 on v0

v1 whole, which is shorter than its diff:
```python
import math

import jax
import jax.numpy as jnp
from jax import lax
from jax.sharding import PartitionSpec as P

EPS = 1e-06


def xor_permute(value, axis, mask):
    size = lax.axis_size(axis)
    return lax.ppermute(value, axis, [(source, source ^ mask) for source in range(size)])


def normalize(rows_in):
    inverse = lax.rsqrt(jnp.mean(rows_in * rows_in, axis=-1, keepdims=True) + EPS)
    return (rows_in * inverse, inverse)


def norm_backward(grad_norm, unit_rows, inverse, gain):
    scaled = grad_norm * gain
    return inverse * (scaled - unit_rows * jnp.mean(scaled * unit_rows, axis=-1, keepdims=True))


def shards(q_pre, k_pre, values, cotangent, out_weight, q_gain, k_gain, block_position):
    tensor_count = lax.axis_size("tensor")
    context_count = lax.axis_size("context")
    dp_count = lax.axis_size("dp")
    for size in (tensor_count, context_count, dp_count):
        assert size & (size - 1) == 0
    tensor_pos = lax.axis_index("tensor")
    context_pos = lax.axis_index("context")
    head_size = q_gain.shape[0]
    block_rows = q_pre.shape[2]
    head_count = q_pre.shape[3] // head_size
    kv_count = k_pre.shape[3] // head_size
    per_kv = tensor_count // kv_count
    half_size = head_size // per_kv
    kv_column = tensor_pos // per_kv * head_size
    score_scale = 1.0 / math.sqrt(head_size)

    own_kv = jnp.concatenate(
        [
            lax.dynamic_slice_in_dim(k_pre[0, 0], kv_column, head_size, 1),
            lax.dynamic_slice_in_dim(values[0, 0], kv_column, head_size, 1),
        ],
        axis=1,
    )
    kv_slots = [own_kv] + [xor_permute(own_kv, "context", k) for k in range(1, context_count)]

    cot_own = cotangent[0, 0]
    cot_pieces = [cot_own] + [xor_permute(cot_own, "tensor", m) for m in range(1, tensor_count)]
    piece_rows = cot_own.shape[0]
    product = lax.dot_general(
        jnp.stack(cot_pieces, axis=0),
        out_weight,
        (((2,), (1,)), ((), ())),
        preferred_element_type=jnp.float32,
    ).astype(jnp.bfloat16)
    order = tensor_pos ^ jnp.arange(tensor_count, dtype=jnp.int32)
    grad_attn = jnp.take(product, order, axis=0).reshape(block_rows, head_count, head_size)

    offsets = jnp.arange(block_rows, dtype=jnp.int32)
    block_order = block_position[0]
    slot_blocks = jnp.take(block_order, context_pos ^ jnp.arange(context_count, dtype=jnp.int32))
    query_positions = slot_blocks[0] * block_rows + offsets
    key_positions = (slot_blocks[:, None] * block_rows + offsets[None, :]).reshape(-1)
    visible = key_positions[None, :] <= query_positions[:, None]

    query_unit, query_inverse = normalize(
        q_pre[0, 0].reshape(block_rows, head_count, head_size).astype(jnp.float32)
    )
    query_norm = (query_unit * q_gain).astype(jnp.bfloat16)
    kv_all = jnp.concatenate(kv_slots, axis=0)
    key_unit, key_inverse = normalize(kv_all[:, :head_size].astype(jnp.float32))
    key_norm = (key_unit * k_gain).astype(jnp.bfloat16)
    value_rows = kv_all[:, head_size:]

    scores = (
        jnp.einsum("qhd,kd->hqk", query_norm, key_norm, preferred_element_type=jnp.float32)
        * score_scale
    )
    scores = jnp.where(visible[None], scores, -jnp.inf)
    row_max = jnp.max(scores, axis=-1, keepdims=True)
    exponent = jnp.exp(scores - row_max)
    probs = exponent / jnp.sum(exponent, axis=-1, keepdims=True)
    grad_prob = jnp.einsum("qhd,kd->hqk", grad_attn, value_rows, preferred_element_type=jnp.float32)
    row_delta = jnp.sum(probs * grad_prob, axis=-1, keepdims=True)
    grad_score = (probs * (grad_prob - row_delta) * score_scale).astype(jnp.bfloat16)
    prob_low = probs.astype(jnp.bfloat16)
    grad_qn = jnp.einsum("hqk,kd->qhd", grad_score, key_norm, preferred_element_type=jnp.float32)
    key_part = jnp.einsum("hqk,qhd->kd", grad_score, query_norm, preferred_element_type=jnp.float32)
    value_part = jnp.einsum("hqk,qhd->kd", prob_low, grad_attn, preferred_element_type=jnp.float32)

    d_query = norm_backward(grad_qn, query_unit, query_inverse, q_gain).astype(jnp.bfloat16)
    gain_query_part = jnp.sum(grad_qn * query_unit, axis=(0, 1))
    gain_key_part = jnp.sum(key_part * key_unit, axis=0)

    gains = jnp.stack([gain_query_part, gain_key_part], axis=0)
    for axis, size in (("context", context_count), ("tensor", tensor_count), ("dp", dp_count)):
        bit = 1
        while bit < size:
            gains = gains + xor_permute(gains, axis, bit)
            bit *= 2

    key_slots = key_part.reshape(context_count, block_rows, head_size)
    value_slots = value_part.reshape(context_count, block_rows, head_size)
    half_index = tensor_pos % per_kv
    key_total = key_slots[0]
    value_total = lax.dynamic_slice_in_dim(value_slots[0], half_index * half_size, half_size, 1)
    group_size = tensor_count * context_count
    for m in range(per_kv):
        for k in range(context_count):
            if m == 0 and k == 0:
                continue
            target_half = (tensor_pos ^ m) % per_kv
            term = jnp.concatenate(
                [
                    key_slots[k],
                    lax.dynamic_slice_in_dim(value_slots[k], target_half * half_size, half_size, 1),
                ],
                axis=1,
            )
            pairs = []
            for source in range(group_size):
                st, sc = divmod(source, context_count)
                pairs.append((source, (st ^ m) * context_count + (sc ^ k)))
            arrived = lax.ppermute(term, ("tensor", "context"), pairs)
            key_total = key_total + arrived[:, :head_size]
            value_total = value_total + arrived[:, head_size:]

    own_unit = key_unit[:block_rows]
    own_inverse = key_inverse[:block_rows]
    d_key_full = norm_backward(key_total, own_unit, own_inverse, k_gain)
    d_key_half = lax.dynamic_slice_in_dim(d_key_full, half_index * half_size, half_size, 1)
    return (
        d_query.reshape(1, 1, block_rows, head_count * head_size),
        d_key_half.astype(jnp.bfloat16).reshape(1, 1, block_rows, half_size),
        value_total.astype(jnp.bfloat16).reshape(1, 1, block_rows, half_size),
        gains[0],
        gains[1],
    )


def solution(mesh):
    placed = (
        P("dp", "context", None, "tensor"),
        P("dp", "context", None, None),
        P("dp", "context", None, None),
        P("dp", "context", "tensor", None),
        P("tensor", None),
        P(),
        P(),
        P("dp", None),
    )
    return jax.shard_map(
        shards,
        mesh=mesh,
        in_specs=placed,
        out_specs=(
            P("dp", "context", None, "tensor"),
            P("dp", "context", None, "tensor"),
            P("dp", "context", None, "tensor"),
            P(),
            P(),
        ),
        check_vma=False,
    )
```

time: 109 us -> 44.7 us (0.41)
  blocking collectives: 44.3 us -> 0 us
  between operations: 14.9 us -> 1.01 us
  waiting for transfers between devices: 29.1 us -> 16.7 us
  starting transfers between devices: 1.74 us -> 13.5 us
  other arithmetic: 6.22 us -> 0.92 us
  matrix products: 8.39 us -> 6.08 us
  local copies, waits for them, and re-layouts: 4.4 us -> 6.22 us
    psum x1 -> x0, blocking collectives: 40.5 us -> none  [shards(): lax.psum((gain_query_part, gain_key_part), ('tensor', 'context', 'dp'))]
    all_gather x1 -> x0, waiting for transfers between devices: 19.4 us -> none  [shards(): lax.all_gather(cotangent[:, 0], 'tensor', axis=1, tiled=True)]
    ppermute x1 -> x12, waiting for transfers between devices: 2.61 us -> 16.7 us  [the longest x9 14 us: xor_permute(): lax.ppermute(value, axis, [(source, source ^ mask) for source in range(si...]
    ppermute x1 -> x12, starting transfers between devices: 1.66 us -> 13.5 us  [the longest x9 12 us: xor_permute(): lax.ppermute(value, axis, [(source, source ^ mask) for source in range(si...]
    reduce_scatter x1 -> x0, waiting for transfers between devices: 6.4 us -> none  [shards(): lax.psum_scatter(partials, 'context', scatter_dimension=1, tiled=True)]
    all_gather x2 -> x0, blocking collectives: 3.87 us -> none  [the longest x1 2.03 us: shards(): lax.all_gather(own_keys, 'context', axis=1, tiled=True)]
    convert_element_type x2 -> x1, other arithmetic: 1.7 us -> 0.11 us  [shards(): norm_backward(grad_qn, query_unit, query_inverse, q_gain)]
    gather x0 -> x4, local copies, waits for them, and re-layouts: none -> 1.37 us  [the longest x3 0.73 us: shards(): jnp.take(product, order, axis=0).reshape(block_rows, head_count, head_size)]
  transfers between devices with their start and end apart: 3 -> 12, of which waited for: 3 -> 9; matrix products, arithmetic and copies ran while one was open for 8% -> 13% of each run, Pallas kernels for 0% -> 0%
where the time goes in v1:
time: 44.7 us; the launch traced here: 44.4 us
  waiting for transfers between devices  16.7 us (37%)
  starting transfers between devices  13.5 us (30%)
  local copies, waits for them, and re-layouts  6.22 us (14%)
  matrix products  6.08 us (14%)
  between operations  1.01 us (2%)
  other arithmetic  0.92 us (2%)
    ppermute x9, waiting for transfers between devices, xor_permute(): lax.ppermute(value, axis, [(source, source ^ mask) for source in range(si...  14 us
    ppermute x9, starting transfers between devices, xor_permute(): lax.ppermute(value, axis, [(source, source ^ mask) for source in range(si...  12 us
    dot_general x1, matrix products, shards(): lax.dot_general(jnp.stack(cot_pieces, axis=0), out_weight, (((2,), (1,)),...  3.82 us
    ppermute x3, waiting for transfers between devices, shards(): arrived = lax.ppermute(term, ('tensor', 'context'), pairs)  2.63 us
    unnamed x11, local copies, waits for them, and re-layouts  2.19 us
    ppermute x3, starting transfers between devices, shards(): arrived = lax.ppermute(term, ('tensor', 'context'), pairs)  1.56 us
    sub x1, matrix products, shards(): exponent = jnp.exp(scores - row_max)  1.07 us
    convert_element_type x1, local copies, waits for them, and re-layouts, shards(): q_pre[0, 0].reshape(block_rows, head_count, head_size).astype(jnp.float32)  1 us
  transfers between devices with their start and end apart: 12, of which 9 were waited for; matrix products, arithmetic and copies ran while one was open for 13% of the time, Pallas kernels for 0%

profile of v1, /device:TPU:0, one launch (start us, length us, event | category | flops | bytes accessed | tf_op | source)
XLA Modules:
  0.0 44.4 jit_solution(12982978451614883536)
XLA Ops:
  0.6 4.0 %collective-permute-start.3 = (bf16[32,4096]{1,0:T(8,128)(2,1)}, bf16[32,4096]{1,0:T(8,128)(2,1)S(1)}, u32[]{:S(2)}, u32[]{:S(2)}) collective-permute-start(bf16[32,4096]{1,0:T(8,128)(2,1)} %bitcast.86), channel_id=1, source_target_pairs={{0,24},{8,16},{16,8},{24,0},{1,25},{9,17},{17,9},{25,1},{2,26},{10... | collective-permute-start | bytes 786440 | tf_op jit(solution)/shard_map/ppermute | solution.py:13
  4.6 0.5 %collective-permute-start.2 = (bf16[32,4096]{1,0:T(8,128)(2,1)}, bf16[32,4096]{1,0:T(8,128)(2,1)S(1)}, u32[]{:S(2)}, u32[]{:S(2)}) collective-permute-start(bf16[32,4096]{1,0:T(8,128)(2,1)} %bitcast.87), channel_id=1, source_target_pairs={{0,16},{8,24},{16,0},{24,8},{1,17},{9,25},{17,1},{25,9},{2,18},{10... | collective-permute-start | bytes 786440 | tf_op jit(solution)/shard_map/ppermute | solution.py:13
  5.1 0.1 collective-permute-start.1
  5.3 0.8 %dynamic-slice_bitcast_fusion = (bf16[128,128]{1,0:T(8,128)(2,1)S(1)}, bf16[128,128]{1,0:T(8,128)(2,1)S(1)}) fusion(bf16[1,1,128,256]{3,2,1,0:T(8,128)(2,1)} %param.10, s32[]{:T(128)S(6)} %select_n.85, bf16[1,1,128,256]{3,2,1,0:T(8,128)(2,1)} %param.9), kind=kLoop, calls=%fused_computation.70 | loop fusion | bytes 131076 | tf_op jit(solution)/shard_map/dynamic_slice | solution.py:46
  6.2 1.0 %copy.29 = f32[1,1,128,512]{2,3,1,0:T(8,128)S(1)} copy(bf16[1,1,128,512]{3,2,1,0:T(8,128)(2,1)} %param.8) | data formatting | bytes 393216 | tf_op jit(solution)/shard_map/convert_element_type | solution.py:72
  7.5 0.6 %gather_fusion = s32[2]{0:T(128)S(1)} fusion(s32[2]{0:T(128)S(1)} %bitcast.72, s32[1024]{0:T(1024)S(1)} %pad_clamp_fusion.1), kind=kCustom, calls=%fused_computation | custom fusion | bytes 24 | tf_op jit(solution)/shard_map/jit(_take)/gather | solution.py:66
  8.5 1.1 %fusion.59 = (f32[4,128]{1,0:T(4,128)S(1)}, f32[4,128,256]{1,2,0:T(8,128)S(1)}) fusion(pred[128,256]{0,1:T(8,128)(4,1)S(1)} %broadcast_compare_fusion, f32[128]{0:T(128)} %param.14, f32[256]{0:T(256)S(1)} %add_rsqrt_fusion.1, bf16[256,256]{1,0:T(8,128)(2,1)S(1)} %pad_maximum_fusion.2, f32[128,4,128]{0,2,1:T(8,128)S(1)} %bitcast.74, f32[128]{0:T(128)} %param.13, ...), kind=kOutput, calls=%fused_computation.108 | convolution fusion | flops 34406656 | bytes 890880 | tf_op jit(solution)/shard_map/sub | solution.py:86
  9.6 2.4 %collective-permute-done.3 = bf16[32,4096]{1,0:T(8,128)(2,1)S(1)} collective-permute-done((bf16[32,4096]{1,0:T(8,128)(2,1)}, bf16[32,4096]{1,0:T(8,128)(2,1)S(1)}, u32[]{:S(2)}, u32[]{:S(2)}) %collective-permute-start.3) | collective-permute-done | bytes 262176 | tf_op jit(solution)/shard_map/ppermute | solution.py:13
  12.0 4.7 %collective-permute-done.2 = bf16[32,4096]{1,0:T(8,128)(2,1)S(1)} collective-permute-done((bf16[32,4096]{1,0:T(8,128)(2,1)}, bf16[32,4096]{1,0:T(8,128)(2,1)S(1)}, u32[]{:S(2)}, u32[]{:S(2)}) %collective-permute-start.2) | collective-permute-done | bytes 262176 | tf_op jit(solution)/shard_map/ppermute | solution.py:13
  16.8 0.3 collective-permute-done.1
  17.1 3.8 %fusion.12 = bf16[4,32,512]{2,1,0:T(8,128)(2,1)S(1)} fusion(bf16[512,4096]{1,0:T(8,128)(2,1)} %param.12, bf16[1,32,4096]{2,1,0:T(8,128)(2,1)S(1)} %bitcast.90, bf16[1,32,4096]{2,1,0:T(8,128)(2,1)S(1)} %bitcast.91, bf16[1,32,4096]{2,1,0:T(8,128)(2,1)S(1)} %bitcast.92, bf16[1,32,4096]{2,1,0:T(8,128)(2,1)} %bitcast.89), kind=kOutput, calls=%fused_computation.17 | convolution fusion | flops 538509312 | bytes 5373952 | tf_op jit(solution)/shard_map/dot_general | solution.py:55
  20.9 0.6 %gather_fusion.1 = bf16[4,32,512]{2,1,0:T(8,128)(2,1)S(1)} fusion(bf16[4,32,512]{2,1,0:T(8,128)(2,1)S(1)} %fusion.12, s32[1024]{0:T(1024)S(1)} %pad_clamp_fusion), kind=kCustom, calls=%fused_computation.1 | custom fusion | bytes 262160 | tf_op jit(solution)/shard_map/jit(_take)/gather | solution.py:62
  21.5 0.1 copy.31
  21.6 0.2 convolution_bitcast_fusion
  21.9 0.4 multiply_reduce_fusion.1
  22.3 0.3 multiply_reduce_fusion.4
  22.7 0.2 convolution_bitcast_fusion.2
  23.1 1.0 %collective-permute-done.7 = f32[2,128]{1,0:T(2,128)S(1)} collective-permute-done((f32[2,128]{1,0:T(2,128)S(1)}, f32[2,128]{1,0:T(2,128)S(1)}, u32[]{:S(2)}, u32[]{:S(2)}) %collective-permute-start.7) | collective-permute-done | bytes 1056 | tf_op jit(solution)/shard_map/ppermute | solution.py:13
  24.2 1.6 %collective-permute-start.8 = (f32[2,128]{1,0:T(2,128)S(1)}, f32[2,128]{1,0:T(2,128)S(1)}, u32[]{:S(2)}, u32[]{:S(2)}) collective-permute-start(f32[2,128]{1,0:T(2,128)S(1)} %fusion.51), channel_id=1, source_target_pairs={{0,8},{8,0},{16,24},{24,16},{1,9},{9,1},{17,25},{25,17},{2,10},{10... | collective-permute-start | bytes 3080 | tf_op jit(solution)/shard_map/ppermute | solution.py:13
  25.8 2.0 %collective-permute-done.8 = f32[2,128]{1,0:T(2,128)S(1)} collective-permute-done((f32[2,128]{1,0:T(2,128)S(1)}, f32[2,128]{1,0:T(2,128)S(1)}, u32[]{:S(2)}, u32[]{:S(2)}) %collective-permute-start.8) | collective-permute-done | bytes 1056 | tf_op jit(solution)/shard_map/ppermute | solution.py:13
  27.8 1.5 %collective-permute-start.9 = (f32[2,128]{1,0:T(2,128)S(1)}, f32[2,128]{1,0:T(2,128)S(1)}, u32[]{:S(2)}, u32[]{:S(2)}) collective-permute-start(f32[2,128]{1,0:T(2,128)S(1)} %fusion.66), channel_id=1, source_target_pairs={{0,16},{8,24},{16,0},{24,8},{1,17},{9,25},{17,1},{25,9},{2,18},{10... | collective-permute-start | bytes 3080 | tf_op jit(solution)/shard_map/ppermute | solution.py:13
  29.3 0.8 %copy.42 = bf16[1,1,128,512]{3,2,1,0:T(8,128)(2,1)} copy(bf16[1,1,128,512]{2,3,1,0:T(8,128)(2,1)S(1)} %bitcast.78) | data formatting | bytes 262144
  30.1 1.4 %collective-permute-done.9 = f32[2,128]{1,0:T(2,128)S(1)} collective-permute-done((f32[2,128]{1,0:T(2,128)S(1)}, f32[2,128]{1,0:T(2,128)S(1)}, u32[]{:S(2)}, u32[]{:S(2)}) %collective-permute-start.9) | collective-permute-done | bytes 1056 | tf_op jit(solution)/shard_map/ppermute | solution.py:13
  31.5 1.6 %collective-permute-start.10 = (f32[2,128]{1,0:T(2,128)S(1)}, f32[2,128]{1,0:T(2,128)S(1)}, u32[]{:S(2)}, u32[]{:S(2)}) collective-permute-start(f32[2,128]{1,0:T(2,128)S(1)} %add.173), channel_id=1, source_target_pairs={{0,1},{1,0},{2,3},{3,2},{4,5},{5,4},{6,7},{7,6},{8,9},{9,8},{10,11... | collective-permute-start | bytes 3080 | tf_op jit(solution)/shard_map/ppermute | solution.py:13
  33.1 1.9 %collective-permute-done.10 = f32[2,128]{1,0:T(2,128)S(1)} collective-permute-done((f32[2,128]{1,0:T(2,128)S(1)}, f32[2,128]{1,0:T(2,128)S(1)}, u32[]{:S(2)}, u32[]{:S(2)}) %collective-permute-start.10) | collective-permute-done | bytes 1056 | tf_op jit(solution)/shard_map/ppermute | solution.py:13
  35.0 2.6 %collective-permute-start.11 = (f32[2,128]{1,0:T(2,128)S(1)}, f32[2,128]{1,0:T(2,128)S(1)}, u32[]{:S(2)}, u32[]{:S(2)}) collective-permute-start(f32[2,128]{1,0:T(2,128)S(1)} %add.174), channel_id=1, source_target_pairs={{0,2},{1,3},{2,0},{3,1},{4,6},{5,7},{6,4},{7,5},{8,10},{9,11},{10,... | collective-permute-start | bytes 3080 | tf_op jit(solution)/shard_map/ppermute | solution.py:13
  37.6 1.6 %collective-permute-start.5 = (f32[128,192]{1,0:T(8,128)S(1)}, f32[128,192]{1,0:T(8,128)S(1)}, u32[]{:S(2)}, u32[]{:S(2)}) collective-permute-start(f32[128,192]{1,0:T(8,128)S(1)} %pad_maximum_fusion.3), channel_id=1, source_target_pairs={{0,8},{4,12},{8,0},{12,4},{16,24},{20,28},{24,16},{28,20},{1,9},{5... | collective-permute-start | bytes 294920 | tf_op jit(solution)/shard_map/ppermute | solution.py:129
  39.2 0.3 collective-permute-done.11
  39.5 0.5 %slice_bitcast_fusion.2 = (f32[128]{0:T(128)}, f32[128]{0:T(128)}) fusion(f32[2,128]{1,0:T(2,128)S(1)} %add.175), kind=kLoop, calls=%fused_computation.90 | loop fusion | bytes 2048 | tf_op jit(solution)/shard_map/squeeze | solution.py:142
  40.0 2.6 %collective-permute-done.5 = f32[128,192]{1,0:T(8,128)S(1)} collective-permute-done((f32[128,192]{1,0:T(8,128)S(1)}, f32[128,192]{1,0:T(8,128)S(1)}, u32[]{:S(2)}, u32[]{:S(2)}) %collective-permute-start.5) | collective-permute-done | bytes 98336 | tf_op jit(solution)/shard_map/ppermute | solution.py:129
  43.0 0.7 %copy.43 = bf16[1,1,128,64]{2,3,1,0:T(8,128)(2,1)} copy(bf16[1,1,128,64]{3,2,1,0:T(8,128)(2,1)S(1)} %fusion.37) | data formatting | bytes 32768
  43.7 0.7 %copy.44 = bf16[1,1,128,64]{2,3,1,0:T(8,128)(2,1)} copy(bf16[1,1,128,64]{3,2,1,0:T(8,128)(2,1)S(1)} %fusion.38) | data formatting | bytes 32768
  (53 shorter events, 1.5 us)
Async XLA Ops:
  0.6 6.8 %copy-start = (s32[1,2]{1,0:T(1,128)S(1)}, s32[1,2]{1,0:T(1,128)}, u32[]{:S(2)}) copy-start(s32[1,2]{1,0:T(1,128)} %param.15) | copy-start | bytes 28
  0.6 11.4 %collective-permute-start.3 = (bf16[32,4096]{1,0:T(8,128)(2,1)}, bf16[32,4096]{1,0:T(8,128)(2,1)S(1)}, u32[]{:S(2)}, u32[]{:S(2)}) collective-permute-start(bf16[32,4096]{1,0:T(8,128)(2,1)} %bitcast.86), channel_id=1, source_target_pairs={{0,24},{8,16},{16,8},{24,0},{1,25},{9,17},{17,9},{25,1},{2,26},{10... | collective-permute-start | bytes 786440 | tf_op jit(solution)/shard_map/ppermute | solution.py:13
  4.6 12.1 %collective-permute-start.2 = (bf16[32,4096]{1,0:T(8,128)(2,1)}, bf16[32,4096]{1,0:T(8,128)(2,1)S(1)}, u32[]{:S(2)}, u32[]{:S(2)}) collective-permute-start(bf16[32,4096]{1,0:T(8,128)(2,1)} %bitcast.87), channel_id=1, source_target_pairs={{0,16},{8,24},{16,0},{24,8},{1,17},{9,25},{17,1},{25,9},{2,18},{10... | collective-permute-start | bytes 786440 | tf_op jit(solution)/shard_map/ppermute | solution.py:13
  5.1 11.9 %collective-permute-start.1 = (bf16[32,4096]{1,0:T(8,128)(2,1)}, bf16[32,4096]{1,0:T(8,128)(2,1)S(1)}, u32[]{:S(2)}, u32[]{:S(2)}) collective-permute-start(bf16[32,4096]{1,0:T(8,128)(2,1)} %bitcast.88), channel_id=1, source_target_pairs={{0,8},{8,0},{16,24},{24,16},{1,9},{9,1},{17,25},{25,17},{2,10},{10... | collective-permute-start | bytes 786440 | tf_op jit(solution)/shard_map/ppermute | solution.py:13
  6.1 2.3 %collective-permute-start = (bf16[128,256]{1,0:T(8,128)(2,1)S(1)}, bf16[128,256]{1,0:T(8,128)(2,1)S(1)}, u32[]{:S(2)}, u32[]{:S(2)}) collective-permute-start(bf16[128,256]{1,0:T(8,128)(2,1)S(1)} %pad_maximum_fusion.4), channel_id=1, source_target_pairs={{0,4},{4,0},{1,5},{5,1},{2,6},{6,2},{3,7},{7,3},{8,12},{12,8},{9,1... | collective-permute-start | bytes 196616 | tf_op jit(solution)/shard_map/ppermute | solution.py:13
  8.5 13.8 %copy-start.1 = (f32[256]{0:T(256)}, f32[256]{0:T(256)S(1)}, u32[]{:S(2)}) copy-start(f32[256]{0:T(256)S(1)} %add_rsqrt_fusion.1) | copy-start | bytes 3076
  17.1 4.8 %copy-start.2 = (f32[128]{0:T(128)S(1)}, f32[128]{0:T(128)}, u32[]{:S(2)}) copy-start(f32[128]{0:T(128)} %param.14) | copy-start | bytes 1540
  17.1 4.8 %copy-start.3 = (f32[128]{0:T(128)S(1)}, f32[128]{0:T(128)}, u32[]{:S(2)}) copy-start(f32[128]{0:T(128)} %param.13) | copy-start | bytes 1540
  22.6 20.2 %slice-start = ((f32[256]{0:T(256)}), f32[128]{0:T(128)S(1)}, s32[]{:S(2)}) async-start(f32[256]{0:T(256)} %copy-done.1), calls=%async_computation | async-start | bytes 1024 | tf_op jit(solution)/shard_map/slice | solution.py:134
  22.9 1.2 %collective-permute-start.7 = (f32[2,128]{1,0:T(2,128)S(1)}, f32[2,128]{1,0:T(2,128)S(1)}, u32[]{:S(2)}, u32[]{:S(2)}) collective-permute-start(f32[2,128]{1,0:T(2,128)S(1)} %pad_maximum_fusion.5), channel_id=1, source_target_pairs={{0,4},{4,0},{1,5},{5,1},{2,6},{6,2},{3,7},{7,3},{8,12},{12,8},{9,1... | collective-permute-start | bytes 3080 | tf_op jit(solution)/shard_map/ppermute | solution.py:13
  24.2 3.6 %collective-permute-start.8 = (f32[2,128]{1,0:T(2,128)S(1)}, f32[2,128]{1,0:T(2,128)S(1)}, u32[]{:S(2)}, u32[]{:S(2)}) collective-permute-start(f32[2,128]{1,0:T(2,128)S(1)} %fusion.51), channel_id=1, source_target_pairs={{0,8},{8,0},{16,24},{24,16},{1,9},{9,1},{17,25},{25,17},{2,10},{10... | collective-permute-start | bytes 3080 | tf_op jit(solution)/shard_map/ppermute | solution.py:13
  27.8 3.6 %collective-permute-start.9 = (f32[2,128]{1,0:T(2,128)S(1)}, f32[2,128]{1,0:T(2,128)S(1)}, u32[]{:S(2)}, u32[]{:S(2)}) collective-permute-start(f32[2,128]{1,0:T(2,128)S(1)} %fusion.66), channel_id=1, source_target_pairs={{0,16},{8,24},{16,0},{24,8},{1,17},{9,25},{17,1},{25,9},{2,18},{10... | collective-permute-start | bytes 3080 | tf_op jit(solution)/shard_map/ppermute | solution.py:13
  30.1 9.9 %collective-permute-start.6 = (f32[128,192]{1,0:T(8,128)S(1)}, f32[128,192]{1,0:T(8,128)S(1)}, u32[]{:S(2)}, u32[]{:S(2)}) collective-permute-start(f32[128,192]{1,0:T(8,128)S(1)} %get-tuple-element.29), channel_id=1, source_target_pairs={{0,12},{4,8},{8,4},{12,0},{16,28},{20,24},{24,20},{28,16},{1,13},{... | collective-permute-start | bytes 294920 | tf_op jit(solution)/shard_map/ppermute | solution.py:129
  31.5 3.6 %collective-permute-start.10 = (f32[2,128]{1,0:T(2,128)S(1)}, f32[2,128]{1,0:T(2,128)S(1)}, u32[]{:S(2)}, u32[]{:S(2)}) collective-permute-start(f32[2,128]{1,0:T(2,128)S(1)} %add.173), channel_id=1, source_target_pairs={{0,1},{1,0},{2,3},{3,2},{4,5},{5,4},{6,7},{7,6},{8,9},{9,8},{10,11... | collective-permute-start | bytes 3080 | tf_op jit(solution)/shard_map/ppermute | solution.py:13
  35.0 4.5 %collective-permute-start.11 = (f32[2,128]{1,0:T(2,128)S(1)}, f32[2,128]{1,0:T(2,128)S(1)}, u32[]{:S(2)}, u32[]{:S(2)}) collective-permute-start(f32[2,128]{1,0:T(2,128)S(1)} %add.174), channel_id=1, source_target_pairs={{0,2},{1,3},{2,0},{3,1},{4,6},{5,7},{6,4},{7,5},{8,10},{9,11},{10,... | collective-permute-start | bytes 3080 | tf_op jit(solution)/shard_map/ppermute | solution.py:13
  37.6 5.0 %collective-permute-start.5 = (f32[128,192]{1,0:T(8,128)S(1)}, f32[128,192]{1,0:T(8,128)S(1)}, u32[]{:S(2)}, u32[]{:S(2)}) collective-permute-start(f32[128,192]{1,0:T(8,128)S(1)} %pad_maximum_fusion.3), channel_id=1, source_target_pairs={{0,8},{4,12},{8,0},{12,4},{16,24},{20,28},{24,16},{28,20},{1,9},{5... | collective-permute-start | bytes 294920 | tf_op jit(solution)/shard_map/ppermute | solution.py:129
  39.2 3.5 %collective-permute-start.4 = (f32[128,192]{1,0:T(8,128)S(1)}, f32[128,192]{1,0:T(8,128)S(1)}, u32[]{:S(2)}, u32[]{:S(2)}) collective-permute-start(f32[128,192]{1,0:T(8,128)S(1)} %get-tuple-element.28), channel_id=1, source_target_pairs={{0,4},{4,0},{8,12},{12,8},{16,20},{20,16},{24,28},{28,24},{1,5},{5... | collective-permute-start | bytes 294920 | tf_op jit(solution)/shard_map/ppermute | solution.py:129

commit v2 on v1

--- a/solution.py
+++ b/solution.py
@@ -4,8 +4,13 @@
 import jax.numpy as jnp
 from jax import lax
 from jax.sharding import PartitionSpec as P
+from jax.experimental import pallas as pl
+from jax.experimental.pallas import tpu as pltpu
+from jax.experimental.layout import Layout, with_layout_constraint
 
 EPS = 1e-06
+MESH_AXES = ("tensor", "context", "dp")
+OUT_LAYOUT = Layout(major_to_minor=(0, 1, 3, 2))
 
 
 def xor_permute(value, axis, mask):
@@ -13,6 +18,61 @@
     return lax.ppermute(value, axis, [(source, source ^ mask) for source in range(size)])
 
 
+def all_sum(value):
+    count = math.prod(lax.axis_size(axis) for axis in MESH_AXES)
+    spread = jnp.broadcast_to(value[None], (count,) + value.shape)
+    pieces = lax.all_to_all(spread, MESH_AXES, 0, 0, tiled=True)
+    total = pieces[0]
+    for index in range(1, count):
+        total = total + pieces[index]
+    return total
+
+
+def grad_attn_kernel(*refs):
+    *cot_refs, weight_ref, out_ref, acc_ref = refs
+    step = pl.program_id(0)
+
+    @pl.when(step == 0)
+    def _():
+        acc_ref[...] = jnp.zeros_like(acc_ref)
+
+    weight = weight_ref[...]
+    rows = cot_refs[0].shape[0]
+    if rows % 16 == 0:
+        joined = jnp.concatenate([cot_ref[...] for cot_ref in cot_refs], axis=0)
+        acc_ref[...] += jnp.dot(joined, weight, preferred_element_type=jnp.float32)
+    else:
+        for index, cot_ref in enumerate(cot_refs):
+            acc_ref[pl.ds(index * rows, rows), :] += jnp.dot(
+                cot_ref[...], weight, preferred_element_type=jnp.float32
+            )
+
+    @pl.when(step == pl.num_programs(0) - 1)
+    def _():
+        out_ref[...] = acc_ref[...].astype(out_ref.dtype)
+
+
+def grad_attn_matmul(pieces, weight_t, depth=512):
+    count, rows = len(pieces), pieces[0].shape[0]
+    inner, width = weight_t.shape
+    depth = min(depth, inner)
+    return pl.pallas_call(
+        grad_attn_kernel,
+        out_shape=jax.ShapeDtypeStruct((count * rows, width), jnp.bfloat16),
+        grid=(inner // depth,),
+        in_specs=[pl.BlockSpec((rows, depth), lambda k: (0, k)) for _ in pieces]
+        + [pl.BlockSpec((depth, width), lambda k: (k, 0))],
+        out_specs=pl.BlockSpec((count * rows, width), lambda k: (0, 0)),
+        scratch_shapes=[pltpu.VMEM((count * rows, width), jnp.float32)],
+        compiler_params=pltpu.CompilerParams(dimension_semantics=("arbitrary",)),
+        cost_estimate=pl.CostEstimate(
+            flops=2 * count * rows * width * inner,
+            bytes_accessed=2 * (count * rows * inner + width * inner + count * rows * width),
+            transcendentals=0,
+        ),
+    )(*pieces, weight_t)
+
+
 def normalize(rows_in):
     inverse = lax.rsqrt(jnp.mean(rows_in * rows_in, axis=-1, keepdims=True) + EPS)
     return (rows_in * inverse, inverse)
@@ -23,7 +83,7 @@
     return inverse * (scaled - unit_rows * jnp.mean(scaled * unit_rows, axis=-1, keepdims=True))
 
 
-def shards(q_pre, k_pre, values, cotangent, out_weight, q_gain, k_gain, block_position):
+def shard_body(q_pre, k_pre, values, cotangent, out_weight, q_gain, k_gain, block_position):
     tensor_count = lax.axis_size("tensor")
     context_count = lax.axis_size("context")
     dp_count = lax.axis_size("dp")
@@ -52,12 +112,8 @@
     cot_own = cotangent[0, 0]
     cot_pieces = [cot_own] + [xor_permute(cot_own, "tensor", m) for m in range(1, tensor_count)]
     piece_rows = cot_own.shape[0]
-    product = lax.dot_general(
-        jnp.stack(cot_pieces, axis=0),
-        out_weight,
-        (((2,), (1,)), ((), ())),
-        preferred_element_type=jnp.float32,
-    ).astype(jnp.bfloat16)
+    weight_t = with_layout_constraint(jnp.transpose(out_weight), Layout(major_to_minor=(0, 1)))
+    product = grad_attn_matmul(cot_pieces, weight_t).reshape(tensor_count, piece_rows, -1)
     order = tensor_pos ^ jnp.arange(tensor_count, dtype=jnp.int32)
     grad_attn = jnp.take(product, order, axis=0).reshape(block_rows, head_count, head_size)
 
@@ -98,11 +154,7 @@
     gain_key_part = jnp.sum(key_part * key_unit, axis=0)
 
     gains = jnp.stack([gain_query_part, gain_key_part], axis=0)
-    for axis, size in (("context", context_count), ("tensor", tensor_count), ("dp", dp_count)):
-        bit = 1
-        while bit < size:
-            gains = gains + xor_permute(gains, axis, bit)
-            bit *= 2
+    gains = all_sum(gains)
 
     key_slots = key_part.reshape(context_count, block_rows, head_size)
     value_slots = value_part.reshape(context_count, block_rows, head_size)
@@ -134,10 +186,16 @@
     own_inverse = key_inverse[:block_rows]
     d_key_full = norm_backward(key_total, own_unit, own_inverse, k_gain)
     d_key_half = lax.dynamic_slice_in_dim(d_key_full, half_index * half_size, half_size, 1)
+    d_key_out = with_layout_constraint(
+        d_key_half.astype(jnp.bfloat16).reshape(1, 1, block_rows, half_size), OUT_LAYOUT
+    )
+    d_value_out = with_layout_constraint(
+        value_total.astype(jnp.bfloat16).reshape(1, 1, block_rows, half_size), OUT_LAYOUT
+    )
     return (
         d_query.reshape(1, 1, block_rows, head_count * head_size),
-        d_key_half.astype(jnp.bfloat16).reshape(1, 1, block_rows, half_size),
-        value_total.astype(jnp.bfloat16).reshape(1, 1, block_rows, half_size),
+        d_key_out,
+        d_value_out,
         gains[0],
         gains[1],
     )
@@ -155,7 +213,7 @@
         P("dp", None),
     )
     return jax.shard_map(
-        shards,
+        shard_body,
         mesh=mesh,
         in_specs=placed,
         out_specs=(

time: 44.7 us -> 43.1 us (0.964)
  waiting for transfers between devices: 16.7 us -> 6.55 us
  local copies, waits for them, and re-layouts: 6.22 us -> 12.8 us
  Pallas kernels: 0 us -> 6.54 us
  matrix products: 6.08 us -> 1.77 us
  starting transfers between devices: 13.5 us -> 11.8 us
  other arithmetic: 0.92 us -> 2.06 us
    ppermute x9 -> x4, waiting for transfers between devices: 14 us -> 2.5 us  [xor_permute(): lax.ppermute(value, axis, [(source, source ^ mask) for source in range(si...]
    ppermute x9 -> x4, starting transfers between devices: 12 us -> 4.65 us  [xor_permute(): lax.ppermute(value, axis, [(source, source ^ mask) for source in range(si...]
    pallas_call x0 -> x1, Pallas kernels: none -> 6.54 us  [grad_attn_matmul(): pl.pallas_call(grad_attn_kernel, out_shape=jax.ShapeDtypeStruct((count *...]
    unnamed x11 -> x18, local copies, waits for them, and re-layouts: 2.19 us -> 8.12 us
    all_to_all x0 -> x1, starting transfers between devices: none -> 4.92 us  [all_sum(): pieces = lax.all_to_all(spread, MESH_AXES, 0, 0, tiled=True)]
    all_to_all x0 -> x1, waiting for transfers between devices: none -> 4.04 us  [all_sum(): pieces = lax.all_to_all(spread, MESH_AXES, 0, 0, tiled=True)]
    dot_general x5 -> x4, matrix products: 5.01 us -> 1.33 us  [the longest x1 0.42 us: shard_body(): jnp.einsum('hqk,qhd->kd', grad_score, query_norm, preferred_element_type=...]
    ppermute x3, waiting for transfers between devices: 2.63 us -> 0.01 us  [shard_body(): arrived = lax.ppermute(term, ('tensor', 'context'), pairs)]
  transfers between devices with their start and end apart: 12 -> 8, of which waited for: 9 -> 2; matrix products, arithmetic and copies ran while one was open for 13% -> 25% of each run, Pallas kernels for 0% -> 0%
where the time goes in v2:
time: 43.1 us; the launch traced here: 42.6 us
  local copies, waits for them, and re-layouts  12.8 us (30%)
  starting transfers between devices  11.8 us (27%)
  waiting for transfers between devices  6.55 us (15%)
  Pallas kernels  6.54 us (15%)
  other arithmetic  2.06 us (5%)
  matrix products  1.77 us (4%)
  between operations  1.04 us (2%)
    unnamed x18, local copies, waits for them, and re-layouts  8.12 us
    pallas_call x1, Pallas kernels, grad_attn_matmul(): pl.pallas_call(grad_attn_kernel, out_shape=jax.ShapeDtypeStruct((count *...  6.54 us
    all_to_all x1, starting transfers between devices, all_sum(): pieces = lax.all_to_all(spread, MESH_AXES, 0, 0, tiled=True)  4.92 us
    ppermute x4, starting transfers between devices, xor_permute(): lax.ppermute(value, axis, [(source, source ^ mask) for source in range(si...  4.65 us
    all_to_all x1, waiting for transfers between devices, all_sum(): pieces = lax.all_to_all(spread, MESH_AXES, 0, 0, tiled=True)  4.04 us
    ppermute x4, waiting for transfers between devices, xor_permute(): lax.ppermute(value, axis, [(source, source ^ mask) for source in range(si...  2.5 us
    ppermute x3, starting transfers between devices, shard_body(): arrived = lax.ppermute(term, ('tensor', 'context'), pairs)  2.26 us
    gather x2, local copies, waits for them, and re-layouts, shard_body(): jnp.take(product, order, axis=0).reshape(block_rows, head_count, head_size)  1.49 us
  transfers between devices with their start and end apart: 8, of which 2 were waited for; matrix products, arithmetic and copies ran while one was open for 25% of the time, Pallas kernels for 0%

profile of v2, /device:TPU:0, one launch (start us, length us, event | category | flops | bytes accessed | tf_op | source)
XLA Modules:
  0.0 42.6 jit_solution(16871104025331208254)
XLA Ops:
  0.6 3.0 %collective-permute-start.1 = (bf16[32,4096]{1,0:T(8,128)(2,1)}, bf16[32,4096]{1,0:T(8,128)(2,1)S(1)}, u32[]{:S(2)}, u32[]{:S(2)}) collective-permute-start(bf16[32,4096]{1,0:T(8,128)(2,1)} %bitcast.167), channel_id=1, source_target_pairs={{0,8},{8,0},{16,24},{24,16},{1,9},{9,1},{17,25},{25,17},{2,10},{10... | collective-permute-start | bytes 786440 | tf_op jit(solution)/shard_map/ppermute | solution.py:18
  3.7 1.5 %collective-permute-start.2 = (bf16[32,4096]{1,0:T(8,128)(2,1)}, bf16[32,4096]{1,0:T(8,128)(2,1)S(1)}, u32[]{:S(2)}, u32[]{:S(2)}) collective-permute-start(bf16[32,4096]{1,0:T(8,128)(2,1)} %bitcast.168), channel_id=1, source_target_pairs={{0,16},{8,24},{16,0},{24,8},{1,17},{9,25},{17,1},{25,9},{2,18},{10... | collective-permute-start | bytes 786440 | tf_op jit(solution)/shard_map/ppermute | solution.py:18
  5.2 0.8 %constant_dynamic-slice_fusion.3 = (bf16[1,1,128,128]{3,2,1,0:T(8,128)(2,1)S(1)}, bf16[1,1,128,128]{3,2,1,0:T(8,128)(2,1)S(1)}) fusion(bf16[1,1,128,256]{3,2,1,0:T(8,128)(2,1)} %param.10, s32[]{:T(128)S(6)} %select_n.85, bf16[1,1,128,256]{3,2,1,0:T(8,128)(2,1)} %param.9), kind=kLoop, calls=%fused_computation.67 | loop fusion | bytes 131076 | tf_op jit(solution)/shard_map/dynamic_slice | solution.py:106
  6.0 0.1 copy.27
  6.1 0.1 copy.28
  6.4 6.5 %copy.31 = bf16[512,4096]{0,1:T(8,128)(2,1)} copy(bf16[512,4096]{1,0:T(8,128)(2,1)} %param.12) | data formatting | bytes 8388608 | tf_op args[4]
  13.1 0.6 %gather_fusion = s32[2]{0:T(128)S(1)} fusion(s32[2]{0:T(128)S(1)} %bitcast.154, s32[1024]{0:T(1024)S(1)} %pad_clamp_fusion.1), kind=kCustom, calls=%fused_computation | custom fusion | bytes 24 | tf_op jit(solution)/shard_map/jit(_take)/gather | solution.py:122
  13.9 0.1 copy.26
  14.1 0.1 broadcast_compare_fusion
  14.3 0.4 %fusion.59 = (f32[4,128]{1,0:T(4,128)S(1)}, f32[4,128,256]{1,2,0:T(8,128)S(1)}) fusion(pred[128,256]{0,1:T(8,128)(4,1)S(1)} %broadcast_compare_fusion, f32[128]{0:T(128)S(1)} %copy-done.6, f32[256]{0:T(256)S(1)} %add_rsqrt_fusion.1, bf16[256,256]{0,1:T(8,128)(2,1)S(1)} %pad_maximum_fusion, f32[128,4,128]{0,2,1:T(8,128)S(1)} %bitcast.157, ...), kind=kOutput, calls=%fused_computation.139 | convolution fusion | flops 34406656 | bytes 890880 | tf_op jit(solution)/shard_map/sub | solution.py:142
  14.8 2.5 %collective-permute-done.2.refs_2_ = bf16[32,4096]{1,0:T(8,128)(2,1)S(1)} collective-permute-done((bf16[32,4096]{1,0:T(8,128)(2,1)}, bf16[32,4096]{1,0:T(8,128)(2,1)S(1)}, u32[]{:S(2)}, u32[]{:S(2)}) %collective-permute-start.2) | collective-permute-done | bytes 262176 | tf_op jit(solution)/shard_map/ppermute | solution.py:18
  17.3 0.7 %copy-done.2 = bf16[32,4096]{1,0:T(8,128)(2,1)} copy-done((bf16[32,4096]{1,0:T(8,128)(2,1)}, bf16[32,4096]{1,0:T(8,128)(2,1)S(1)}, u32[]{:S(2)}) %copy-start.2) | copy-done | bytes 262168
  18.0 0.1 copy-done.3
  18.1 6.5 %shard_map.119 = bf16[128,512]{1,0:T(8,128)(2,1)} custom-call(bf16[32,4096]{1,0:T(8,128)(2,1)} %bitcast.170, bf16[32,4096]{1,0:T(8,128)(2,1)} %copy-done.1, bf16[32,4096]{1,0:T(8,128)(2,1)} %copy-done.2, bf16[32,4096]{1,0:T(8,128)(2,1)} %copy-done.3, bf16[4096,512]{1,0:T(8,128)(2,1)} %bitcast.155), custom_call_target="tpu_custom_call" | custom-call | flops 536870912 | bytes 5373952 | tf_op jit(solution)/shard_map/pallas_call | solution.py:59
  24.6 1.5 %gather_fusion.1 = bf16[4,32,512]{2,1,0:T(8,128)(2,1)S(1)} fusion(bf16[4,32,512]{2,1,0:T(8,128)(2,1)} %bitcast.162, s32[1024]{0:T(1024)S(1)} %pad_clamp_fusion), kind=kCustom, calls=%fused_computation.1 | custom fusion | bytes 262160 | tf_op jit(solution)/shard_map/jit(_take)/gather | solution.py:118
  26.1 0.2 broadcast_select_fusion
  26.3 0.1 copy.37
  26.5 0.2 convolution_bitcast_fusion
  26.7 0.4 multiply_reduce_fusion.4
  27.2 0.4 multiply_reduce_fusion.1
  27.6 0.2 convolution_bitcast_fusion.2
  27.9 0.6 %broadcast_in_dim.55 = f32[32,2,128]{2,1,0:T(2,128)} broadcast(f32[2,128]{1,0:T(2,128)S(1)} %pad_maximum_fusion.5), dimensions={1,2} | broadcast | bytes 33792 | tf_op jit(solution)/shard_map/broadcast_in_dim | solution.py:23
  28.5 4.9 %all-to-all-start = ((f32[32,2,128]{2,1,0:T(2,128)}), f32[32,2,128]{2,1,0:T(2,128)S(1)}, u32[]{:S(2)}, u32[]{:S(2)}) async-start(f32[32,2,128]{2,1,0:T(2,128)} %broadcast_in_dim.55), calls=%async_computation | async-start | bytes 65536 | tf_op jit(solution)/shard_map/all_to_all | solution.py:24
  33.5 1.8 %collective-permute-start.5 = (f32[128,192]{0,1:T(8,128)S(1)}, f32[128,192]{0,1:T(8,128)S(1)}, u32[]{:S(2)}, u32[]{:S(2)}) collective-permute-start(f32[128,192]{0,1:T(8,128)S(1)} %pad_maximum_fusion.3), channel_id=1, source_target_pairs={{0,8},{4,12},{8,0},{12,4},{16,24},{20,28},{24,16},{28,20},{1,9},{5... | collective-permute-start | bytes 294920 | tf_op jit(solution)/shard_map/ppermute | solution.py:181
  35.4 0.4 collective-permute-start.6
  35.8 0.1 multiply_convert_fusion
  35.9 0.8 %copy.38 = bf16[1,1,128,512]{3,2,1,0:T(8,128)(2,1)} copy(bf16[1,1,128,512]{2,3,1,0:T(8,128)(2,1)S(1)} %bitcast.161) | data formatting | bytes 262144
  36.7 4.0 %all-to-all-done = f32[32,2,128]{2,1,0:T(2,128)S(1)} async-done(((f32[32,2,128]{2,1,0:T(2,128)}), f32[32,2,128]{2,1,0:T(2,128)S(1)}, u32[]{:S(2)}, u32[]{:S(2)}) %all-to-all-start) | async-done | bytes 32800 | tf_op jit(solution)/shard_map/all_to_all | solution.py:24
  40.8 0.5 %slice_bitcast_fusion.17 = (f32[128]{0:T(128)}, f32[128]{0:T(128)}) fusion(f32[2,128]{1,0:T(2,128)S(1)} %fusion.32), kind=kLoop, calls=%fused_computation.126 | loop fusion | bytes 2048 | tf_op jit(solution)/shard_map/squeeze | solution.py:200
  41.3 0.1 multiply_reduce_fusion.5
  41.4 0.6 %fusion.23 = bf16[1,1,128,64]{2,3,1,0:T(8,128)(2,1)} fusion(f32[128,128]{0,1:T(8,128)S(1)} %get-tuple-element.23, s32[]{:T(128)S(6)} %select_n.94, f32[128,128]{0,1:T(8,128)S(1)} %get-tuple-element.18, f32[128]{0:T(128)S(1)} %slice-done, f32[128]{0:T(128)S(1)} %broadcast_multiply_fusion.1), kind=kLoop, calls=%fused_computation.56 | loop fusion | flops 32768 | bytes 82948 | tf_op jit(solution)/shard_map/reshape | solution.py:190
  42.0 0.6 %fusion.24 = bf16[1,1,128,64]{2,3,1,0:T(8,128)(2,1)} fusion(f32[128,192]{0,1:T(8,128)S(1)} %collective-permute-done.6, f32[128,192]{0,1:T(8,128)S(1)} %collective-permute-done.5, f32[128,192]{0,1:T(8,128)S(1)} %collective-permute-done.4, f32[128,128]{0,1:T(8,128)S(1)} %get-tuple-element.26, s32[]{:T(128)S(6)} %select_n.94), kind=kLoop, calls=%fused_computation.57 | loop fusion | flops 32768 | bytes 147460 | tf_op jit(solution)/shard_map/reshape | solution.py:193
  (52 shorter events, 0.8 us)
Async XLA Ops:
  0.6 12.5 %copy-start = (s32[1,2]{1,0:T(1,128)S(1)}, s32[1,2]{1,0:T(1,128)}, u32[]{:S(2)}) copy-start(s32[1,2]{1,0:T(1,128)} %param.15) | copy-start | bytes 28
  0.6 14.1 %collective-permute-start.1 = (bf16[32,4096]{1,0:T(8,128)(2,1)}, bf16[32,4096]{1,0:T(8,128)(2,1)S(1)}, u32[]{:S(2)}, u32[]{:S(2)}) collective-permute-start(bf16[32,4096]{1,0:T(8,128)(2,1)} %bitcast.167), channel_id=1, source_target_pairs={{0,8},{8,0},{16,24},{24,16},{1,9},{9,1},{17,25},{25,17},{2,10},{10... | collective-permute-start | bytes 786440 | tf_op jit(solution)/shard_map/ppermute | solution.py:18
  3.7 13.6 %collective-permute-start.2 = (bf16[32,4096]{1,0:T(8,128)(2,1)}, bf16[32,4096]{1,0:T(8,128)(2,1)S(1)}, u32[]{:S(2)}, u32[]{:S(2)}) collective-permute-start(bf16[32,4096]{1,0:T(8,128)(2,1)} %bitcast.168), channel_id=1, source_target_pairs={{0,16},{8,24},{16,0},{24,8},{1,17},{9,25},{17,1},{25,9},{2,18},{10... | collective-permute-start | bytes 786440 | tf_op jit(solution)/shard_map/ppermute | solution.py:18
  5.2 12.1 %collective-permute-start.3 = (bf16[32,4096]{1,0:T(8,128)(2,1)}, bf16[32,4096]{1,0:T(8,128)(2,1)S(1)}, u32[]{:S(2)}, u32[]{:S(2)}) collective-permute-start(bf16[32,4096]{1,0:T(8,128)(2,1)} %bitcast.169), channel_id=1, source_target_pairs={{0,24},{8,16},{16,8},{24,0},{1,25},{9,17},{17,9},{25,1},{2,26},{10... | collective-permute-start | bytes 786440 | tf_op jit(solution)/shard_map/ppermute | solution.py:18
  6.3 8.0 %collective-permute-start = (bf16[128,256]{0,1:T(8,128)(2,1)S(1)}, bf16[128,256]{0,1:T(8,128)(2,1)S(1)}, u32[]{:S(2)}, u32[]{:S(2)}) collective-permute-start(bf16[128,256]{0,1:T(8,128)(2,1)S(1)} %pad_maximum_fusion.4), channel_id=1, source_target_pairs={{0,4},{4,0},{1,5},{5,1},{2,6},{6,2},{3,7},{7,3},{8,12},{12,8},{9,1... | collective-permute-start | bytes 196616 | tf_op jit(solution)/shard_map/ppermute | solution.py:18
  6.4 7.5 %copy-start.4 = (bf16[1,1,128,512]{3,2,1,0:T(8,128)(2,1)S(1)}, bf16[1,1,128,512]{3,2,1,0:T(8,128)(2,1)}, u32[]{:S(2)}) copy-start(bf16[1,1,128,512]{3,2,1,0:T(8,128)(2,1)} %param.8) | copy-start | bytes 393220
  6.4 7.9 %copy-start.6 = (f32[128]{0:T(128)S(1)}, f32[128]{0:T(128)}, u32[]{:S(2)}) copy-start(f32[128]{0:T(128)} %param.14) | copy-start | bytes 1540
  6.4 7.9 %copy-start.7 = (f32[128]{0:T(128)S(1)}, f32[128]{0:T(128)}, u32[]{:S(2)}) copy-start(f32[128]{0:T(128)} %param.13) | copy-start | bytes 1540
  14.3 12.9 %copy-start.5 = (f32[256]{0:T(256)}, f32[256]{0:T(256)S(1)}, u32[]{:S(2)}) copy-start(f32[256]{0:T(256)S(1)} %add_rsqrt_fusion.1) | copy-start | bytes 3076
  14.8 2.5 %copy-start.1 = (bf16[32,4096]{1,0:T(8,128)(2,1)}, bf16[32,4096]{1,0:T(8,128)(2,1)S(1)}, u32[]{:S(2)}) copy-start(bf16[32,4096]{1,0:T(8,128)(2,1)S(1)} %collective-permute-done.1.refs_1_) | copy-start | bytes 786436
  17.3 0.7 %copy-start.2 = (bf16[32,4096]{1,0:T(8,128)(2,1)}, bf16[32,4096]{1,0:T(8,128)(2,1)S(1)}, u32[]{:S(2)}) copy-start(bf16[32,4096]{1,0:T(8,128)(2,1)S(1)} %collective-permute-done.2.refs_2_) | copy-start | bytes 786436
  17.3 0.8 %copy-start.3 = (bf16[32,4096]{1,0:T(8,128)(2,1)}, bf16[32,4096]{1,0:T(8,128)(2,1)S(1)}, u32[]{:S(2)}) copy-start(bf16[32,4096]{1,0:T(8,128)(2,1)S(1)} %collective-permute-done.3.refs_3_) | copy-start | bytes 786436
  27.6 13.8 %slice-start = ((f32[256]{0:T(256)}), f32[128]{0:T(128)S(1)}, s32[]{:S(2)}) async-start(f32[256]{0:T(256)} %copy-done.5), calls=%async_computation.1 | async-start | bytes 1024 | tf_op jit(solution)/shard_map/slice | solution.py:186
  28.5 12.2 %all-to-all-start = ((f32[32,2,128]{2,1,0:T(2,128)}), f32[32,2,128]{2,1,0:T(2,128)S(1)}, u32[]{:S(2)}, u32[]{:S(2)}) async-start(f32[32,2,128]{2,1,0:T(2,128)} %broadcast_in_dim.55), calls=%async_computation | async-start | bytes 65536 | tf_op jit(solution)/shard_map/all_to_all | solution.py:24
  33.5 7.8 %collective-permute-start.5 = (f32[128,192]{0,1:T(8,128)S(1)}, f32[128,192]{0,1:T(8,128)S(1)}, u32[]{:S(2)}, u32[]{:S(2)}) collective-permute-start(f32[128,192]{0,1:T(8,128)S(1)} %pad_maximum_fusion.3), channel_id=1, source_target_pairs={{0,8},{4,12},{8,0},{12,4},{16,24},{20,28},{24,16},{28,20},{1,9},{5... | collective-permute-start | bytes 294920 | tf_op jit(solution)/shard_map/ppermute | solution.py:181
  35.3 5.9 %collective-permute-start.4 = (f32[128,192]{0,1:T(8,128)S(1)}, f32[128,192]{0,1:T(8,128)S(1)}, u32[]{:S(2)}, u32[]{:S(2)}) collective-permute-start(f32[128,192]{0,1:T(8,128)S(1)} %get-tuple-element.28), channel_id=1, source_target_pairs={{0,4},{4,0},{8,12},{12,8},{16,20},{20,16},{24,28},{28,24},{1,5},{5... | collective-permute-start | bytes 294920 | tf_op jit(solution)/shard_map/ppermute | solution.py:181
  35.4 5.9 %collective-permute-start.6 = (f32[128,192]{0,1:T(8,128)S(1)}, f32[128,192]{0,1:T(8,128)S(1)}, u32[]{:S(2)}, u32[]{:S(2)}) collective-permute-start(f32[128,192]{0,1:T(8,128)S(1)} %get-tuple-element.29), channel_id=1, source_target_pairs={{0,12},{4,8},{8,4},{12,0},{16,28},{20,24},{24,20},{28,16},{1,13},{... | collective-permute-start | bytes 294920 | tf_op jit(solution)/shard_map/ppermute | solution.py:181

commit v3 on v1

--- a/solution.py
+++ b/solution.py
@@ -4,13 +4,26 @@
 import jax.numpy as jnp
 from jax import lax
 from jax.sharding import PartitionSpec as P
+from jax.experimental.layout import Layout, with_layout_constraint
 
 EPS = 1e-06
+MESH_AXES = ("tensor", "context", "dp")
+OUT_LAYOUT = Layout(major_to_minor=(0, 1, 3, 2))
 
 
 def xor_permute(value, axis, mask):
     size = lax.axis_size(axis)
     return lax.ppermute(value, axis, [(source, source ^ mask) for source in range(size)])
+
+
+def all_sum(value):
+    count = math.prod(lax.axis_size(axis) for axis in MESH_AXES)
+    spread = jnp.broadcast_to(value[None], (count,) + value.shape)
+    pieces = lax.all_to_all(spread, MESH_AXES, 0, 0, tiled=True)
+    total = pieces[0]
+    for index in range(1, count):
+        total = total + pieces[index]
+    return total
 
 
 def normalize(rows_in):
@@ -23,7 +36,7 @@
     return inverse * (scaled - unit_rows * jnp.mean(scaled * unit_rows, axis=-1, keepdims=True))
 
 
-def shards(q_pre, k_pre, values, cotangent, out_weight, q_gain, k_gain, block_position):
+def shard_body(q_pre, k_pre, values, cotangent, out_weight, q_gain, k_gain, block_position):
     tensor_count = lax.axis_size("tensor")
     context_count = lax.axis_size("context")
     dp_count = lax.axis_size("dp")
@@ -51,11 +64,11 @@
 
     cot_own = cotangent[0, 0]
     cot_pieces = [cot_own] + [xor_permute(cot_own, "tensor", m) for m in range(1, tensor_count)]
-    piece_rows = cot_own.shape[0]
+    weight_t = with_layout_constraint(jnp.transpose(out_weight), Layout(major_to_minor=(0, 1)))
     product = lax.dot_general(
         jnp.stack(cot_pieces, axis=0),
-        out_weight,
-        (((2,), (1,)), ((), ())),
+        weight_t,
+        (((2,), (0,)), ((), ())),
         preferred_element_type=jnp.float32,
     ).astype(jnp.bfloat16)
     order = tensor_pos ^ jnp.arange(tensor_count, dtype=jnp.int32)
@@ -98,11 +111,7 @@
     gain_key_part = jnp.sum(key_part * key_unit, axis=0)
 
     gains = jnp.stack([gain_query_part, gain_key_part], axis=0)
-    for axis, size in (("context", context_count), ("tensor", tensor_count), ("dp", dp_count)):
-        bit = 1
-        while bit < size:
-            gains = gains + xor_permute(gains, axis, bit)
-            bit *= 2
+    gains = all_sum(gains)
 
     key_slots = key_part.reshape(context_count, block_rows, head_size)
     value_slots = value_part.reshape(context_count, block_rows, head_size)
@@ -126,7 +135,9 @@
             for source in range(group_size):
                 st, sc = divmod(source, context_count)
                 pairs.append((source, (st ^ m) * context_count + (sc ^ k)))
-            arrived = lax.ppermute(term, ("tensor", "context"), pairs)
+            if m:
+                term = term.astype(jnp.bfloat16)
+            arrived = lax.ppermute(term, ("tensor", "context"), pairs).astype(jnp.float32)
             key_total = key_total + arrived[:, :head_size]
             value_total = value_total + arrived[:, head_size:]
 
@@ -134,10 +145,16 @@
     own_inverse = key_inverse[:block_rows]
     d_key_full = norm_backward(key_total, own_unit, own_inverse, k_gain)
     d_key_half = lax.dynamic_slice_in_dim(d_key_full, half_index * half_size, half_size, 1)
+    d_key_out = with_layout_constraint(
+        d_key_half.astype(jnp.bfloat16).reshape(1, 1, block_rows, half_size), OUT_LAYOUT
+    )
+    d_value_out = with_layout_constraint(
+        value_total.astype(jnp.bfloat16).reshape(1, 1, block_rows, half_size), OUT_LAYOUT
+    )
     return (
         d_query.reshape(1, 1, block_rows, head_count * head_size),
-        d_key_half.astype(jnp.bfloat16).reshape(1, 1, block_rows, half_size),
-        value_total.astype(jnp.bfloat16).reshape(1, 1, block_rows, half_size),
+        d_key_out,
+        d_value_out,
         gains[0],
         gains[1],
     )
@@ -155,7 +172,7 @@
         P("dp", None),
     )
     return jax.shard_map(
-        shards,
+        shard_body,
         mesh=mesh,
         in_specs=placed,
         out_specs=(

time: 44.7 us -> 37.4 us (0.84)
  waiting for transfers between devices: 16.7 us -> 6.68 us
  local copies, waits for them, and re-layouts: 6.22 us -> 11.2 us
  starting transfers between devices: 13.5 us -> 11.7 us
  matrix products: 6.08 us -> 4.61 us
  other arithmetic: 0.92 us -> 1.87 us
    ppermute x9 -> x4, waiting for transfers between devices: 14 us -> 2.48 us  [xor_permute(): lax.ppermute(value, axis, [(source, source ^ mask) for source in range(si...]
    ppermute x9 -> x4, starting transfers between devices: 12 us -> 4.65 us  [xor_permute(): lax.ppermute(value, axis, [(source, source ^ mask) for source in range(si...]
    unnamed x11 -> x14, local copies, waits for them, and re-layouts: 2.19 us -> 7.35 us
    all_to_all x0 -> x1, starting transfers between devices: none -> 4.93 us  [all_sum(): pieces = lax.all_to_all(spread, MESH_AXES, 0, 0, tiled=True)]
    all_to_all x0 -> x1, waiting for transfers between devices: none -> 1.31 us  [all_sum(): pieces = lax.all_to_all(spread, MESH_AXES, 0, 0, tiled=True)]
    reshape x2, other arithmetic: 0.22 us -> 1.24 us  [the longest x1 0.62 us: shard_body(): d_key_half.astype(jnp.bfloat16).reshape(1, 1, block_rows, half_size)]
    convert_element_type x1, local copies, waits for them, and re-layouts: 1 us -> 0.1 us  [shard_body(): q_pre[0, 0].reshape(block_rows, head_count, head_size).astype(jnp.float32)]
    dot_general x5, matrix products: 5.01 us -> 4.18 us  [the longest x1 2.91 us: shard_body(): lax.dot_general(jnp.stack(cot_pieces, axis=0), weight_t, (((2,), (0,)), (...]
  transfers between devices with their start and end apart: 12 -> 8, of which waited for: 9 -> 4; matrix products, arithmetic and copies ran while one was open for 13% -> 29% of each run, Pallas kernels for 0% -> 0%
where the time goes in v3:
time: 37.4 us; the launch traced here: 37.1 us
  starting transfers between devices  11.7 us (31%)
  local copies, waits for them, and re-layouts  11.2 us (30%)
  waiting for transfers between devices  6.68 us (18%)
  matrix products  4.61 us (12%)
  other arithmetic  1.87 us (5%)
  between operations  1.05 us (3%)
    unnamed x14, local copies, waits for them, and re-layouts  7.35 us
    all_to_all x1, starting transfers between devices, all_sum(): pieces = lax.all_to_all(spread, MESH_AXES, 0, 0, tiled=True)  4.93 us
    ppermute x4, starting transfers between devices, xor_permute(): lax.ppermute(value, axis, [(source, source ^ mask) for source in range(si...  4.65 us
    dot_general x1, matrix products, shard_body(): lax.dot_general(jnp.stack(cot_pieces, axis=0), weight_t, (((2,), (0,)), (...  2.91 us
    ppermute x3, waiting for transfers between devices, shard_body(): lax.ppermute(term, ('tensor', 'context'), pairs).astype(jnp.float32)  2.89 us
    ppermute x4, waiting for transfers between devices, xor_permute(): lax.ppermute(value, axis, [(source, source ^ mask) for source in range(si...  2.48 us
    ppermute x3, starting transfers between devices, shard_body(): lax.ppermute(term, ('tensor', 'context'), pairs).astype(jnp.float32)  2.1 us
    all_to_all x1, waiting for transfers between devices, all_sum(): pieces = lax.all_to_all(spread, MESH_AXES, 0, 0, tiled=True)  1.31 us
  transfers between devices with their start and end apart: 8, of which 4 were waited for; matrix products, arithmetic and copies ran while one was open for 29% of the time, Pallas kernels for 0%

profile of v3, /device:TPU:0, one launch (start us, length us, event | category | flops | bytes accessed | tf_op | source)
XLA Modules:
  0.0 37.1 jit_solution(18101186623259670770)
XLA Ops:
  0.6 3.0 %collective-permute-start.1 = (bf16[32,4096]{1,0:T(8,128)(2,1)}, bf16[32,4096]{1,0:T(8,128)(2,1)S(1)}, u32[]{:S(2)}, u32[]{:S(2)}) collective-permute-start(bf16[32,4096]{1,0:T(8,128)(2,1)} %bitcast.175), channel_id=1, source_target_pairs={{0,8},{8,0},{16,24},{24,16},{1,9},{9,1},{17,25},{25,17},{2,10},{10... | collective-permute-start | bytes 786440 | tf_op jit(solution)/shard_map/ppermute | solution.py:16
  3.7 1.5 %collective-permute-start.2 = (bf16[32,4096]{1,0:T(8,128)(2,1)}, bf16[32,4096]{1,0:T(8,128)(2,1)S(1)}, u32[]{:S(2)}, u32[]{:S(2)}) collective-permute-start(bf16[32,4096]{1,0:T(8,128)(2,1)} %bitcast.176), channel_id=1, source_target_pairs={{0,16},{8,24},{16,0},{24,8},{1,17},{9,25},{17,1},{25,9},{2,18},{10... | collective-permute-start | bytes 786440 | tf_op jit(solution)/shard_map/ppermute | solution.py:16
  5.2 0.8 %constant_dynamic-slice_fusion.1 = (bf16[1,1,128,128]{3,2,1,0:T(8,128)(2,1)S(1)}, bf16[1,1,128,128]{3,2,1,0:T(8,128)(2,1)S(1)}) fusion(bf16[1,1,128,256]{3,2,1,0:T(8,128)(2,1)} %param.10, s32[]{:T(128)S(6)} %select_n.85, bf16[1,1,128,256]{3,2,1,0:T(8,128)(2,1)} %param.9), kind=kLoop, calls=%fused_computation.80 | loop fusion | bytes 131076 | tf_op jit(solution)/shard_map/dynamic_slice | solution.py:59
  6.0 0.1 copy.27
  6.1 0.1 copy.28
  6.4 6.5 %copy.31 = bf16[512,4096]{0,1:T(8,128)(2,1)} copy(bf16[512,4096]{1,0:T(8,128)(2,1)} %param.12) | data formatting | bytes 8388608 | tf_op args[4]
  13.1 0.1 broadcast_in_dim.33
  13.2 0.6 %gather_fusion = s32[2]{0:T(128)S(1)} fusion(s32[2]{0:T(128)S(1)} %bitcast.161, s32[1024]{0:T(1024)S(1)} %pad_clamp_fusion.1), kind=kCustom, calls=%fused_computation | custom fusion | bytes 24 | tf_op jit(solution)/shard_map/jit(_take)/gather | solution.py:79
  14.0 0.1 copy.26
  14.1 0.1 broadcast_compare_fusion
  14.4 0.4 %fusion.76 = (f32[4,128]{1,0:T(4,128)S(1)}, f32[4,128,256]{1,2,0:T(8,128)S(1)}) fusion(pred[128,256]{0,1:T(8,128)(4,1)S(1)} %broadcast_compare_fusion, f32[128]{0:T(128)S(1)} %copy-done.3, f32[256]{0:T(256)S(1)} %add_rsqrt_fusion.1, bf16[256,256]{0,1:T(8,128)(2,1)S(1)} %pad_maximum_fusion, f32[128,4,128]{0,2,1:T(8,128)S(1)} %bitcast.163, ...), kind=kOutput, calls=%fused_computation.156 | convolution fusion | flops 34406656 | bytes 890880 | tf_op jit(solution)/shard_map/sub | solution.py:99
  14.8 2.5 %collective-permute-done.2 = bf16[32,4096]{1,0:T(8,128)(2,1)S(1)} collective-permute-done((bf16[32,4096]{1,0:T(8,128)(2,1)}, bf16[32,4096]{1,0:T(8,128)(2,1)S(1)}, u32[]{:S(2)}, u32[]{:S(2)}) %collective-permute-start.2) | collective-permute-done | bytes 262176 | tf_op jit(solution)/shard_map/ppermute | solution.py:16
  17.3 2.9 %fusion.12 = bf16[4,32,512]{2,1,0:T(8,128)(2,1)S(1)} fusion(bf16[512,4096]{0,1:T(8,128)(2,1)} %copy.31, bf16[1,32,4096]{2,1,0:T(8,128)(2,1)S(1)} %bitcast.181, bf16[1,32,4096]{2,1,0:T(8,128)(2,1)S(1)} %bitcast.180, bf16[1,32,4096]{2,1,0:T(8,128)(2,1)S(1)} %bitcast.179, bf16[1,32,4096]{2,1,0:T(8,128)(2,1)S(1)} %bitcast.178), kind=kOutput, calls=%fused_computation.17 | convolution fusion | flops 538509312 | bytes 5373952 | tf_op jit(solution)/shard_map/dot_general | solution.py:68
  20.2 0.6 %gather_fusion.1 = bf16[4,32,512]{2,1,0:T(8,128)(2,1)S(1)} fusion(bf16[4,32,512]{2,1,0:T(8,128)(2,1)S(1)} %fusion.12, s32[1024]{0:T(1024)S(1)} %pad_clamp_fusion), kind=kCustom, calls=%fused_computation.1 | custom fusion | bytes 262160 | tf_op jit(solution)/shard_map/jit(_take)/gather | solution.py:75
  20.8 0.1 copy.32
  20.9 0.2 convolution_bitcast_fusion
  21.2 0.4 %multiply_reduce_fusion.4 = (f32[128]{0:T(128)S(1)}, f32[256,128]{0,1:T(8,128)S(1)}, f32[256,128]{0,1:T(8,128)S(1)}) fusion(f32[256]{0:T(256)S(1)} %add_rsqrt_fusion.1, bf16[256,256]{0,1:T(8,128)(2,1)S(1)} %pad_maximum_fusion, f32[4,128,256]{1,2,0:T(8,128)S(1)} %convolution_bitcast_fusion, f32[4,128,256]{1,2,0:T(8,128)S(1)} %get-tuple-element.31, ...), kind=kOutput, calls=%fused_computation.43 | convolution fusion | flops 34800256 | bytes 2695168 | tf_op jit(solution)/shard_map/hqk,qhd->kd/dot_general | solution.py:106
  21.6 0.4 %multiply_reduce_fusion.1 = (f32[128]{0:T(128)S(1)}, f32[128,4]{0,1:T(4,128)S(1)}, f32[128,4,128]{0,2,1:T(8,128)S(1)}) fusion(f32[128,4,128]{0,2,1:T(8,128)S(1)} %bitcast.165, f32[128,4]{0,1:T(4,128)S(1)} %add_rsqrt_fusion, f32[128]{0:T(128)S(1)} %copy-done.4, f32[4,128,256]{1,2,0:T(8,128)S(1)} %convolution_bitcast_fusion, ...), kind=kOutput, calls=%fused_computation.30 | convolution fusion | flops 34996352 | bytes 2697728 | tf_op jit(solution)/shard_map/hqk,kd->qhd/dot_general | solution.py:105
  22.0 0.2 convolution_bitcast_fusion.2
  22.3 0.6 %broadcast_in_dim.55 = f32[32,2,128]{2,1,0:T(2,128)} broadcast(f32[2,128]{1,0:T(2,128)S(1)} %pad_maximum_fusion.5), dimensions={1,2} | broadcast | bytes 33792 | tf_op jit(solution)/shard_map/broadcast_in_dim | solution.py:21
  22.9 4.9 %all-to-all-start = ((f32[32,2,128]{2,1,0:T(2,128)}), f32[32,2,128]{2,1,0:T(2,128)S(1)}, u32[]{:S(2)}, u32[]{:S(2)}) async-start(f32[32,2,128]{2,1,0:T(2,128)} %broadcast_in_dim.55), calls=%async_computation | async-start | bytes 65536 | tf_op jit(solution)/shard_map/all_to_all | solution.py:22
  27.9 0.3 collective-permute-start.4
  28.2 1.7 %collective-permute-start.5 = (bf16[128,192]{0,1:T(8,128)(2,1)S(1)}, bf16[128,192]{0,1:T(8,128)(2,1)S(1)}, u32[]{:S(2)}, u32[]{:S(2)}) collective-permute-start(bf16[128,192]{0,1:T(8,128)(2,1)S(1)} %pad_maximum_fusion.3), channel_id=1, source_target_pairs={{0,8},{4,12},{8,0},{12,4},{16,24},{20,28},{24,16},{28,20},{1,9},{5... | collective-permute-start | bytes 147464 | tf_op jit(solution)/shard_map/ppermute | solution.py:140
  30.0 0.1 multiply_convert_fusion
  30.2 0.8 %copy.38 = bf16[1,1,128,512]{3,2,1,0:T(8,128)(2,1)} copy(bf16[1,1,128,512]{2,3,1,0:T(8,128)(2,1)S(1)} %bitcast.167) | data formatting | bytes 262144
  30.9 1.5 %collective-permute-done.5 = bf16[128,192]{0,1:T(8,128)(2,1)S(1)} collective-permute-done((bf16[128,192]{0,1:T(8,128)(2,1)S(1)}, bf16[128,192]{0,1:T(8,128)(2,1)S(1)}, u32[]{:S(2)}, u32[]{:S(2)}) %collective-permute-start.5) | collective-permute-done | bytes 49184 | tf_op jit(solution)/shard_map/ppermute | solution.py:140
  32.5 1.4 %collective-permute-done.6 = bf16[128,192]{0,1:T(8,128)(2,1)S(1)} collective-permute-done((bf16[128,192]{0,1:T(8,128)(2,1)S(1)}, bf16[128,192]{0,1:T(8,128)(2,1)S(1)}, u32[]{:S(2)}, u32[]{:S(2)}) %collective-permute-start.6) | collective-permute-done | bytes 49184 | tf_op jit(solution)/shard_map/ppermute | solution.py:140
  33.8 1.3 %all-to-all-done = f32[32,2,128]{2,1,0:T(2,128)S(1)} async-done(((f32[32,2,128]{2,1,0:T(2,128)}), f32[32,2,128]{2,1,0:T(2,128)S(1)}, u32[]{:S(2)}, u32[]{:S(2)}) %all-to-all-start) | async-done | bytes 32800 | tf_op jit(solution)/shard_map/all_to_all | solution.py:22
  35.2 0.5 %slice_bitcast_fusion.17 = (f32[128]{0:T(128)}, f32[128]{0:T(128)}) fusion(f32[2,128]{1,0:T(2,128)S(1)} %fusion.46), kind=kLoop, calls=%fused_computation.139 | loop fusion | bytes 2048 | tf_op jit(solution)/shard_map/squeeze | solution.py:159
  35.7 0.1 multiply_reduce_fusion.5
  35.8 0.6 %fusion.37 = bf16[1,1,128,64]{2,3,1,0:T(8,128)(2,1)} fusion(f32[128,128]{0,1:T(8,128)S(1)} %get-tuple-element.23, s32[]{:T(128)S(6)} %select_n.94, f32[128,128]{0,1:T(8,128)S(1)} %get-tuple-element.18, f32[128]{0:T(128)S(1)} %slice-done, f32[128]{0:T(128)S(1)} %broadcast_multiply_fusion.1), kind=kLoop, calls=%fused_computation.71 | loop fusion | flops 32768 | bytes 82948 | tf_op jit(solution)/shard_map/reshape | solution.py:149
  36.4 0.6 %fusion.38 = bf16[1,1,128,64]{2,3,1,0:T(8,128)(2,1)} fusion(f32[128,192]{0,1:T(8,128)S(1)} %convert_element_type.55, f32[128,192]{0,1:T(8,128)S(1)} %convert_element_type.54, f32[128,192]{0,1:T(8,128)S(1)} %collective-permute-done.4, f32[128,128]{0,1:T(8,128)S(1)} %get-tuple-element.26, s32[]{:T(128)S(6)} %select_n.94), kind=kLoop, calls=%fused_computation.72 | loop fusion | flops 32768 | bytes 147460 | tf_op jit(solution)/shard_map/reshape | solution.py:152
  (52 shorter events, 0.7 us)
Async XLA Ops:
  0.6 12.5 %copy-start = (s32[1,2]{1,0:T(1,128)S(1)}, s32[1,2]{1,0:T(1,128)}, u32[]{:S(2)}) copy-start(s32[1,2]{1,0:T(1,128)} %param.15) | copy-start | bytes 28
  0.6 14.2 %collective-permute-start.1 = (bf16[32,4096]{1,0:T(8,128)(2,1)}, bf16[32,4096]{1,0:T(8,128)(2,1)S(1)}, u32[]{:S(2)}, u32[]{:S(2)}) collective-permute-start(bf16[32,4096]{1,0:T(8,128)(2,1)} %bitcast.175), channel_id=1, source_target_pairs={{0,8},{8,0},{16,24},{24,16},{1,9},{9,1},{17,25},{25,17},{2,10},{10... | collective-permute-start | bytes 786440 | tf_op jit(solution)/shard_map/ppermute | solution.py:16
  3.7 13.6 %collective-permute-start.2 = (bf16[32,4096]{1,0:T(8,128)(2,1)}, bf16[32,4096]{1,0:T(8,128)(2,1)S(1)}, u32[]{:S(2)}, u32[]{:S(2)}) collective-permute-start(bf16[32,4096]{1,0:T(8,128)(2,1)} %bitcast.176), channel_id=1, source_target_pairs={{0,16},{8,24},{16,0},{24,8},{1,17},{9,25},{17,1},{25,9},{2,18},{10... | collective-permute-start | bytes 786440 | tf_op jit(solution)/shard_map/ppermute | solution.py:16
  5.2 12.1 %collective-permute-start.3 = (bf16[32,4096]{1,0:T(8,128)(2,1)}, bf16[32,4096]{1,0:T(8,128)(2,1)S(1)}, u32[]{:S(2)}, u32[]{:S(2)}) collective-permute-start(bf16[32,4096]{1,0:T(8,128)(2,1)} %bitcast.177), channel_id=1, source_target_pairs={{0,24},{8,16},{16,8},{24,0},{1,25},{9,17},{17,9},{25,1},{2,26},{10... | collective-permute-start | bytes 786440 | tf_op jit(solution)/shard_map/ppermute | solution.py:16
  6.3 8.0 %collective-permute-start = (bf16[128,256]{0,1:T(8,128)(2,1)S(1)}, bf16[128,256]{0,1:T(8,128)(2,1)S(1)}, u32[]{:S(2)}, u32[]{:S(2)}) collective-permute-start(bf16[128,256]{0,1:T(8,128)(2,1)S(1)} %pad_maximum_fusion.2), channel_id=1, source_target_pairs={{0,4},{4,0},{1,5},{5,1},{2,6},{6,2},{3,7},{7,3},{8,12},{12,8},{9,1... | collective-permute-start | bytes 196616 | tf_op jit(solution)/shard_map/ppermute | solution.py:16
  6.4 7.6 %copy-start.1 = (bf16[1,1,128,512]{3,2,1,0:T(8,128)(2,1)S(1)}, bf16[1,1,128,512]{3,2,1,0:T(8,128)(2,1)}, u32[]{:S(2)}) copy-start(bf16[1,1,128,512]{3,2,1,0:T(8,128)(2,1)} %param.8) | copy-start | bytes 393220
  6.4 7.9 %copy-start.3 = (f32[128]{0:T(128)S(1)}, f32[128]{0:T(128)}, u32[]{:S(2)}) copy-start(f32[128]{0:T(128)} %param.14) | copy-start | bytes 1540
  6.4 7.9 %copy-start.4 = (f32[128]{0:T(128)S(1)}, f32[128]{0:T(128)}, u32[]{:S(2)}) copy-start(f32[128]{0:T(128)} %param.13) | copy-start | bytes 1540
  6.4 10.8 %copy-start.5 = (bf16[1,1,32,4096]{3,2,1,0:T(8,128)(2,1)S(1)}, bf16[1,1,32,4096]{3,2,1,0:T(8,128)(2,1)}, u32[]{:S(2)}) copy-start(bf16[1,1,32,4096]{3,2,1,0:T(8,128)(2,1)} %param.11) | copy-start | bytes 786436
  14.3 7.3 %copy-start.2 = (f32[256]{0:T(256)}, f32[256]{0:T(256)S(1)}, u32[]{:S(2)}) copy-start(f32[256]{0:T(256)S(1)} %add_rsqrt_fusion.1) | copy-start | bytes 3076
  22.0 13.8 %slice-start = ((f32[256]{0:T(256)}), f32[128]{0:T(128)S(1)}, s32[]{:S(2)}) async-start(f32[256]{0:T(256)} %copy-done.2), calls=%async_computation.1 | async-start | bytes 1024 | tf_op jit(solution)/shard_map/slice | solution.py:145
  22.9 12.2 %all-to-all-start = ((f32[32,2,128]{2,1,0:T(2,128)}), f32[32,2,128]{2,1,0:T(2,128)S(1)}, u32[]{:S(2)}, u32[]{:S(2)}) async-start(f32[32,2,128]{2,1,0:T(2,128)} %broadcast_in_dim.55), calls=%async_computation | async-start | bytes 65536 | tf_op jit(solution)/shard_map/all_to_all | solution.py:22
  27.9 7.8 %collective-permute-start.4 = (f32[128,192]{0,1:T(8,128)S(1)}, f32[128,192]{0,1:T(8,128)S(1)}, u32[]{:S(2)}, u32[]{:S(2)}) collective-permute-start(f32[128,192]{0,1:T(8,128)S(1)} %pad_maximum_fusion.1), channel_id=1, source_target_pairs={{0,4},{4,0},{8,12},{12,8},{16,20},{20,16},{24,28},{28,24},{1,5},{5... | collective-permute-start | bytes 294920 | tf_op jit(solution)/shard_map/ppermute | solution.py:140
  28.2 4.2 %collective-permute-start.5 = (bf16[128,192]{0,1:T(8,128)(2,1)S(1)}, bf16[128,192]{0,1:T(8,128)(2,1)S(1)}, u32[]{:S(2)}, u32[]{:S(2)}) collective-permute-start(bf16[128,192]{0,1:T(8,128)(2,1)S(1)} %pad_maximum_fusion.3), channel_id=1, source_target_pairs={{0,8},{4,12},{8,0},{12,4},{16,24},{20,28},{24,16},{28,20},{1,9},{5... | collective-permute-start | bytes 147464 | tf_op jit(solution)/shard_map/ppermute | solution.py:140
  30.0 3.9 %collective-permute-start.6 = (bf16[128,192]{0,1:T(8,128)(2,1)S(1)}, bf16[128,192]{0,1:T(8,128)(2,1)S(1)}, u32[]{:S(2)}, u32[]{:S(2)}) collective-permute-start(bf16[128,192]{0,1:T(8,128)(2,1)S(1)} %pad_maximum_fusion.4), channel_id=1, source_target_pairs={{0,12},{4,8},{8,4},{12,0},{16,28},{20,24},{24,20},{28,16},{1,13},{... | collective-permute-start | bytes 147464 | tf_op jit(solution)/shard_map/ppermute | solution.py:140

commit v4 on v3

--- a/solution.py
+++ b/solution.py
@@ -64,6 +64,7 @@
 
     cot_own = cotangent[0, 0]
     cot_pieces = [cot_own] + [xor_permute(cot_own, "tensor", m) for m in range(1, tensor_count)]
+    piece_rows = cot_own.shape[0]
     weight_t = with_layout_constraint(jnp.transpose(out_weight), Layout(major_to_minor=(0, 1)))
     product = lax.dot_general(
         jnp.stack(cot_pieces, axis=0),
@@ -72,18 +73,20 @@
         preferred_element_type=jnp.float32,
     ).astype(jnp.bfloat16)
     order = tensor_pos ^ jnp.arange(tensor_count, dtype=jnp.int32)
-    grad_attn = jnp.take(product, order, axis=0).reshape(block_rows, head_count, head_size)
+    grad_attn = product.reshape(block_rows, head_count, head_size)
 
     offsets = jnp.arange(block_rows, dtype=jnp.int32)
     block_order = block_position[0]
     slot_blocks = jnp.take(block_order, context_pos ^ jnp.arange(context_count, dtype=jnp.int32))
-    query_positions = slot_blocks[0] * block_rows + offsets
+    query_positions = (
+        slot_blocks[0] * block_rows + order[:, None] * piece_rows + offsets[None, :piece_rows]
+    ).reshape(-1)
     key_positions = (slot_blocks[:, None] * block_rows + offsets[None, :]).reshape(-1)
     visible = key_positions[None, :] <= query_positions[:, None]
 
-    query_unit, query_inverse = normalize(
-        q_pre[0, 0].reshape(block_rows, head_count, head_size).astype(jnp.float32)
-    )
+    query_rows = q_pre[0, 0].reshape(tensor_count, piece_rows, head_count, head_size)
+    query_rows = jnp.take(query_rows, order, axis=0).reshape(block_rows, head_count, head_size)
+    query_unit, query_inverse = normalize(query_rows.astype(jnp.float32))
     query_norm = (query_unit * q_gain).astype(jnp.bfloat16)
     kv_all = jnp.concatenate(kv_slots, axis=0)
     key_unit, key_inverse = normalize(kv_all[:, :head_size].astype(jnp.float32))
@@ -107,6 +110,7 @@
     value_part = jnp.einsum("hqk,qhd->kd", prob_low, grad_attn, preferred_element_type=jnp.float32)
 
     d_query = norm_backward(grad_qn, query_unit, query_inverse, q_gain).astype(jnp.bfloat16)
+    d_query = jnp.take(d_query.reshape(tensor_count, piece_rows, -1), order, axis=0)
     gain_query_part = jnp.sum(grad_qn * query_unit, axis=(0, 1))
     gain_key_part = jnp.sum(key_part * key_unit, axis=0)
 

time: 37.4 us -> 38 us (1.016)
  waiting for transfers between devices: 6.68 us -> 3.92 us
  local copies, waits for them, and re-layouts: 11.2 us -> 12.3 us
  other arithmetic: 1.87 us -> 2.88 us
  starting transfers between devices: 11.7 us -> 12.7 us
    ppermute x4, waiting for transfers between devices: 2.48 us -> 0.48 us  [xor_permute(): lax.ppermute(value, axis, [(source, source ^ mask) for source in range(si...]
    all_to_all x1, starting transfers between devices: 4.93 us -> 5.95 us  [all_sum(): pieces = lax.all_to_all(spread, MESH_AXES, 0, 0, tiled=True)]
    another operation x2 -> x4, local copies, waits for them, and re-layouts: 0.01 us -> 0.97 us  [the longest x2 0.96 us: shard_body(): q_pre[0, 0].reshape(tensor_count, piece_rows, head_count, head_size)]
    unnamed x14 -> x11, local copies, waits for them, and re-layouts: 7.35 us -> 6.55 us
    ppermute x3, waiting for transfers between devices: 2.89 us -> 2.14 us  [shard_body(): lax.ppermute(term, ('tensor', 'context'), pairs).astype(jnp.float32)]
    select_n x1 -> x2, other arithmetic: 0.01 us -> 0.75 us  [shard_body(): jnp.take(d_query.reshape(tensor_count, piece_rows, -1), order, axis=0)]
    gather x3 -> x4, local copies, waits for them, and re-layouts: 0.73 us -> 1.27 us  [the longest x3 0.72 us: shard_body(): jnp.take(query_rows, order, axis=0)]
  transfers between devices with their start and end apart: 8 -> 8, of which waited for: 4 -> 4; matrix products, arithmetic and copies ran while one was open for 29% -> 36% of each run, Pallas kernels for 0% -> 0%
where the time goes in v4:
time: 38 us; the launch traced here: 37.6 us
  starting transfers between devices  12.7 us (33%)
  local copies, waits for them, and re-layouts  12.3 us (32%)
  matrix products  4.68 us (12%)
  waiting for transfers between devices  3.92 us (10%)
  other arithmetic  2.88 us (8%)
  between operations  1.08 us (3%)
    unnamed x11, local copies, waits for them, and re-layouts  6.55 us
    all_to_all x1, starting transfers between devices, all_sum(): pieces = lax.all_to_all(spread, MESH_AXES, 0, 0, tiled=True)  5.95 us
    ppermute x4, starting transfers between devices, xor_permute(): lax.ppermute(value, axis, [(source, source ^ mask) for source in range(si...  4.65 us
    dot_general x1, matrix products, shard_body(): lax.dot_general(jnp.stack(cot_pieces, axis=0), weight_t, (((2,), (0,)), (...  2.91 us
    ppermute x3, waiting for transfers between devices, shard_body(): lax.ppermute(term, ('tensor', 'context'), pairs).astype(jnp.float32)  2.14 us
    ppermute x3, starting transfers between devices, shard_body(): lax.ppermute(term, ('tensor', 'context'), pairs).astype(jnp.float32)  2.1 us
    all_to_all x1, waiting for transfers between devices, all_sum(): pieces = lax.all_to_all(spread, MESH_AXES, 0, 0, tiled=True)  1.31 us
    another operation x2, local copies, waits for them, and re-layouts, shard_body(): q_pre[0, 0].reshape(tensor_count, piece_rows, head_count, head_size)  0.96 us
  transfers between devices with their start and end apart: 8, of which 4 were waited for; matrix products, arithmetic and copies ran while one was open for 36% of the time, Pallas kernels for 0%

profile of v4, /device:TPU:0, one launch (start us, length us, event | category | flops | bytes accessed | tf_op | source)
XLA Modules:
  0.0 37.6 jit_solution(3815430166503850499)
XLA Ops:
  0.6 3.0 %collective-permute-start.1 = (bf16[32,4096]{1,0:T(8,128)(2,1)}, bf16[32,4096]{1,0:T(8,128)(2,1)S(1)}, u32[]{:S(2)}, u32[]{:S(2)}) collective-permute-start(bf16[32,4096]{1,0:T(8,128)(2,1)} %bitcast.179), channel_id=1, source_target_pairs={{0,8},{8,0},{16,24},{24,16},{1,9},{9,1},{17,25},{25,17},{2,10},{10... | collective-permute-start | bytes 786440 | tf_op jit(solution)/shard_map/ppermute | solution.py:16
  3.7 1.5 %collective-permute-start.2 = (bf16[32,4096]{1,0:T(8,128)(2,1)}, bf16[32,4096]{1,0:T(8,128)(2,1)S(1)}, u32[]{:S(2)}, u32[]{:S(2)}) collective-permute-start(bf16[32,4096]{1,0:T(8,128)(2,1)} %bitcast.180), channel_id=1, source_target_pairs={{0,16},{8,24},{16,0},{24,8},{1,17},{9,25},{17,1},{25,9},{2,18},{10... | collective-permute-start | bytes 786440 | tf_op jit(solution)/shard_map/ppermute | solution.py:16
  5.2 0.8 %constant_dynamic-slice_fusion.1 = (bf16[1,1,128,128]{3,2,1,0:T(8,128)(2,1)S(1)}, bf16[1,1,128,128]{3,2,1,0:T(8,128)(2,1)S(1)}) fusion(bf16[1,1,128,256]{3,2,1,0:T(8,128)(2,1)} %param.10, s32[]{:T(128)S(6)} %select_n.104, bf16[1,1,128,256]{3,2,1,0:T(8,128)(2,1)} %param.9), kind=kLoop, calls=%fused_computation.82 | loop fusion | bytes 131076 | tf_op jit(solution)/shard_map/dynamic_slice | solution.py:59
  6.1 0.1 copy.72
  6.4 0.9 %reshape_squeeze.3 = bf16[4,32,4,128]{3,2,1,0:T(4,128)(2,1)S(1)} reshape(bf16[1,1,128,512]{3,2,1,0:T(8,128)(2,1)} %param.8) | data formatting | bytes 262144 | tf_op jit(solution)/shard_map/reshape;squeeze | solution.py:87
  7.4 0.6 %gather_fusion.1 = s32[2]{0:T(128)S(1)} fusion(s32[2]{0:T(128)S(1)} %bitcast.168, s32[1024]{0:T(1024)S(1)} %pad_clamp_fusion), kind=kCustom, calls=%fused_computation.1 | custom fusion | bytes 24 | tf_op jit(solution)/shard_map/jit(_take)/gather | solution.py:80
  8.3 0.6 %gather_fusion = bf16[4,32,4,128]{3,1,2,0:T(8,128)(2,1)S(1)} fusion(bf16[4,32,4,128]{3,1,2,0:T(8,128)(2,1)S(1)} %copy.69, s32[1024]{0:T(1024)S(1)} %pad_clamp_fusion.1), kind=kCustom, calls=%fused_computation | custom fusion | bytes 262160 | tf_op jit(solution)/shard_map/jit(_take)/gather | solution.py:88
  8.9 0.2 multiply_reduce_fusion.3
  9.4 6.5 %copy.77 = bf16[512,4096]{0,1:T(8,128)(2,1)} copy(bf16[512,4096]{1,0:T(8,128)(2,1)} %param.12) | data formatting | bytes 8388608 | tf_op args[4]
  16.0 0.1 copy.74
  16.4 0.4 %fusion.72 = (f32[4,128]{1,0:T(4,128)S(1)}, f32[4,128,256]{1,2,0:T(8,128)S(1)}) fusion(pred[128,256]{0,1:T(8,128)(4,1)S(1)} %broadcast_compare_fusion, f32[128]{0:T(128)S(1)} %copy-done.2, f32[256]{0:T(256)S(1)} %add_rsqrt_fusion.1, bf16[256,256]{0,1:T(8,128)(2,1)S(1)} %pad_maximum_fusion, f32[128]{0:T(128)S(1)} %copy-done.3, f32[128,4]{0,1:T(4,128)S(1)} %rsqrt.25, ...), kind=kOutput, calls=%fused_computation.157 | convolution fusion | flops 34537728 | bytes 760320 | tf_op jit(solution)/shard_map/sub | solution.py:102
  16.8 0.5 %collective-permute-done.2 = bf16[32,4096]{1,0:T(8,128)(2,1)S(1)} collective-permute-done((bf16[32,4096]{1,0:T(8,128)(2,1)}, bf16[32,4096]{1,0:T(8,128)(2,1)S(1)}, u32[]{:S(2)}, u32[]{:S(2)}) %collective-permute-start.2) | collective-permute-done | bytes 262176 | tf_op jit(solution)/shard_map/ppermute | solution.py:16
  17.3 2.9 %fusion.12 = bf16[4,32,512]{2,1,0:T(8,128)(2,1)S(1)} fusion(bf16[512,4096]{0,1:T(8,128)(2,1)} %copy.77, bf16[1,32,4096]{2,1,0:T(8,128)(2,1)S(1)} %bitcast.185, bf16[1,32,4096]{2,1,0:T(8,128)(2,1)S(1)} %bitcast.184, bf16[1,32,4096]{2,1,0:T(8,128)(2,1)S(1)} %bitcast.183, bf16[1,32,4096]{2,1,0:T(8,128)(2,1)S(1)} %bitcast.182), kind=kOutput, calls=%fused_computation.18 | convolution fusion | flops 538509312 | bytes 5373952 | tf_op jit(solution)/shard_map/dot_general | solution.py:69
  20.2 0.1 copy.84
  20.4 0.2 convolution_bitcast_fusion
  20.6 0.4 %multiply_reduce_fusion.4 = (f32[128]{0:T(128)S(1)}, f32[256,128]{0,1:T(8,128)S(1)}, f32[256,128]{0,1:T(8,128)S(1)}) fusion(f32[256]{0:T(256)S(1)} %add_rsqrt_fusion.1, bf16[256,256]{0,1:T(8,128)(2,1)S(1)} %pad_maximum_fusion, f32[128]{0:T(128)S(1)} %copy-done.3, f32[128,4]{0,1:T(4,128)S(1)} %rsqrt.25, bf16[128,4,128]{0,2,1:T(8,128)(2,1)S(1)} %copy.74, ...), kind=kOutput, calls=%fused_computation.45 | convolution fusion | flops 34931328 | bytes 2564608 | tf_op jit(solution)/shard_map/hqk,qhd->kd/dot_general | solution.py:109
  21.1 0.4 %multiply_reduce_fusion.1 = (f32[128]{0:T(128)S(1)}, f32[128,4]{0,1:T(4,128)S(1)}, f32[128,4,128]{0,2,1:T(8,128)S(1)}) fusion(f32[128,4]{0,1:T(4,128)S(1)} %rsqrt.25, bf16[128,4,128]{0,2,1:T(8,128)(2,1)S(1)} %copy.74, pred[128]{0:T(512)(128)(4,1)S(1)} %broadcast_in_dim.65, f32[128]{0:T(128)S(1)} %copy-done.3, ...), kind=kOutput, calls=%fused_computation.31 | convolution fusion | flops 35127424 | bytes 2567168 | tf_op jit(solution)/shard_map/hqk,kd->qhd/dot_general | solution.py:108
  21.5 0.2 convolution_bitcast_fusion.2
  21.8 0.6 %broadcast_in_dim.74 = f32[32,2,128]{2,1,0:T(2,128)} broadcast(f32[2,128]{1,0:T(2,128)S(1)} %pad_maximum_fusion.5), dimensions={1,2} | broadcast | bytes 33792 | tf_op jit(solution)/shard_map/broadcast_in_dim | solution.py:21
  22.4 5.9 %all-to-all-start = ((f32[32,2,128]{2,1,0:T(2,128)}), f32[32,2,128]{2,1,0:T(2,128)S(1)}, u32[]{:S(2)}, u32[]{:S(2)}) async-start(f32[32,2,128]{2,1,0:T(2,128)} %broadcast_in_dim.74), calls=%async_computation | async-start | bytes 65536 | tf_op jit(solution)/shard_map/all_to_all | solution.py:22
  28.4 0.3 collective-permute-start.4
  28.8 1.7 %collective-permute-start.5 = (bf16[128,192]{0,1:T(8,128)(2,1)S(1)}, bf16[128,192]{0,1:T(8,128)(2,1)S(1)}, u32[]{:S(2)}, u32[]{:S(2)}) collective-permute-start(bf16[128,192]{0,1:T(8,128)(2,1)S(1)} %pad_maximum_fusion.3), channel_id=1, source_target_pairs={{0,8},{4,12},{8,0},{12,4},{16,24},{20,28},{24,16},{28,20},{1,9},{5... | collective-permute-start | bytes 147464 | tf_op jit(solution)/shard_map/ppermute | solution.py:144
  30.6 0.1 multiply_convert_fusion
  30.7 0.1 copy.81
  30.9 0.6 %gather_fusion.2 = bf16[4,32,512]{2,1,0:T(8,128)(2,1)S(1)} fusion(bf16[4,32,512]{2,1,0:T(8,128)(2,1)S(1)} %reshape.249, s32[1024]{0:T(1024)S(1)} %pad_clamp_fusion.1), kind=kCustom, calls=%fused_computation.2 | custom fusion | bytes 262160 | tf_op jit(solution)/shard_map/jit(_take)/gather | solution.py:113
  31.5 0.7 %broadcast_select_fusion = bf16[1,1,128,512]{3,2,1,0:T(8,128)(2,1)} fusion(bf16[1,1,128,512]{3,2,1,0:T(8,128)(2,1)S(1)} %bitcast.170, pred[128]{0:T(512)(128)(4,1)S(1)} %broadcast_in_dim.65), kind=kLoop, calls=%fused_computation.47 | loop fusion | flops 65536 | bytes 262272 | tf_op jit(solution)/shard_map/jit(_take)/select_n | solution.py:113
  32.2 0.8 %collective-permute-done.5 = bf16[128,192]{0,1:T(8,128)(2,1)S(1)} collective-permute-done((bf16[128,192]{0,1:T(8,128)(2,1)S(1)}, bf16[128,192]{0,1:T(8,128)(2,1)S(1)}, u32[]{:S(2)}, u32[]{:S(2)}) %collective-permute-start.5) | collective-permute-done | bytes 49184 | tf_op jit(solution)/shard_map/ppermute | solution.py:144
  33.0 1.4 %collective-permute-done.6 = bf16[128,192]{0,1:T(8,128)(2,1)S(1)} collective-permute-done((bf16[128,192]{0,1:T(8,128)(2,1)S(1)}, bf16[128,192]{0,1:T(8,128)(2,1)S(1)}, u32[]{:S(2)}, u32[]{:S(2)}) %collective-permute-start.6) | collective-permute-done | bytes 49184 | tf_op jit(solution)/shard_map/ppermute | solution.py:144
  34.4 1.3 %all-to-all-done = f32[32,2,128]{2,1,0:T(2,128)S(1)} async-done(((f32[32,2,128]{2,1,0:T(2,128)}), f32[32,2,128]{2,1,0:T(2,128)S(1)}, u32[]{:S(2)}, u32[]{:S(2)}) %all-to-all-start) | async-done | bytes 32800 | tf_op jit(solution)/shard_map/all_to_all | solution.py:22
  35.7 0.5 %slice_bitcast_fusion.17 = (f32[128]{0:T(128)}, f32[128]{0:T(128)}) fusion(f32[2,128]{1,0:T(2,128)S(1)} %fusion.44), kind=kLoop, calls=%fused_computation.141 | loop fusion | bytes 2048 | tf_op jit(solution)/shard_map/squeeze | solution.py:163
  36.4 0.6 %fusion.35 = bf16[1,1,128,64]{2,3,1,0:T(8,128)(2,1)} fusion(f32[128,128]{0,1:T(8,128)S(1)} %get-tuple-element.13, s32[]{:T(128)S(6)} %select_n.112, f32[128,128]{0,1:T(8,128)S(1)} %get-tuple-element.8, f32[128]{0:T(128)S(1)} %slice-done, f32[128]{0:T(128)S(1)} %broadcast_multiply_fusion.1), kind=kLoop, calls=%fused_computation.72 | loop fusion | flops 32768 | bytes 82948 | tf_op jit(solution)/shard_map/reshape | solution.py:153
  37.0 0.6 %fusion.36 = bf16[1,1,128,64]{2,3,1,0:T(8,128)(2,1)} fusion(f32[128,192]{0,1:T(8,128)S(1)} %convert_element_type.51, f32[128,192]{0,1:T(8,128)S(1)} %convert_element_type.50, f32[128,192]{0,1:T(8,128)S(1)} %collective-permute-done.4, f32[128,128]{0,1:T(8,128)S(1)} %get-tuple-element.16, s32[]{:T(128)S(6)} %select_n.112), kind=kLoop, calls=%fused_computation.73 | loop fusion | flops 32768 | bytes 147460 | tf_op jit(solution)/shard_map/reshape | solution.py:156
  (61 shorter events, 1.4 us)
Async XLA Ops:
  0.6 6.8 %copy-start = (s32[1,2]{1,0:T(1,128)S(1)}, s32[1,2]{1,0:T(1,128)}, u32[]{:S(2)}) copy-start(s32[1,2]{1,0:T(1,128)} %param.15) | copy-start | bytes 28
  0.6 16.2 %collective-permute-start.1 = (bf16[32,4096]{1,0:T(8,128)(2,1)}, bf16[32,4096]{1,0:T(8,128)(2,1)S(1)}, u32[]{:S(2)}, u32[]{:S(2)}) collective-permute-start(bf16[32,4096]{1,0:T(8,128)(2,1)} %bitcast.179), channel_id=1, source_target_pairs={{0,8},{8,0},{16,24},{24,16},{1,9},{9,1},{17,25},{25,17},{2,10},{10... | collective-permute-start | bytes 786440 | tf_op jit(solution)/shard_map/ppermute | solution.py:16
  3.7 13.6 %collective-permute-start.2 = (bf16[32,4096]{1,0:T(8,128)(2,1)}, bf16[32,4096]{1,0:T(8,128)(2,1)S(1)}, u32[]{:S(2)}, u32[]{:S(2)}) collective-permute-start(bf16[32,4096]{1,0:T(8,128)(2,1)} %bitcast.180), channel_id=1, source_target_pairs={{0,16},{8,24},{16,0},{24,8},{1,17},{9,25},{17,1},{25,9},{2,18},{10... | collective-permute-start | bytes 786440 | tf_op jit(solution)/shard_map/ppermute | solution.py:16
  5.2 12.1 %collective-permute-start.3 = (bf16[32,4096]{1,0:T(8,128)(2,1)}, bf16[32,4096]{1,0:T(8,128)(2,1)S(1)}, u32[]{:S(2)}, u32[]{:S(2)}) collective-permute-start(bf16[32,4096]{1,0:T(8,128)(2,1)} %bitcast.181), channel_id=1, source_target_pairs={{0,24},{8,16},{16,8},{24,0},{1,25},{9,17},{17,9},{25,1},{2,26},{10... | collective-permute-start | bytes 786440 | tf_op jit(solution)/shard_map/ppermute | solution.py:16
  6.3 10.0 %collective-permute-start = (bf16[128,256]{0,1:T(8,128)(2,1)S(1)}, bf16[128,256]{0,1:T(8,128)(2,1)S(1)}, u32[]{:S(2)}, u32[]{:S(2)}) collective-permute-start(bf16[128,256]{0,1:T(8,128)(2,1)S(1)} %pad_maximum_fusion.2), channel_id=1, source_target_pairs={{0,4},{4,0},{1,5},{5,1},{2,6},{6,2},{3,7},{7,3},{8,12},{12,8},{9,1... | collective-permute-start | bytes 196616 | tf_op jit(solution)/shard_map/ppermute | solution.py:16
  9.3 7.0 %copy-start.2 = (f32[128]{0:T(128)S(1)}, f32[128]{0:T(128)}, u32[]{:S(2)}) copy-start(f32[128]{0:T(128)} %param.14) | copy-start | bytes 1540
  9.3 7.0 %copy-start.3 = (f32[128]{0:T(128)S(1)}, f32[128]{0:T(128)}, u32[]{:S(2)}) copy-start(f32[128]{0:T(128)} %param.13) | copy-start | bytes 1540
  9.3 7.9 %copy-start.4 = (bf16[1,1,32,4096]{3,2,1,0:T(8,128)(2,1)S(1)}, bf16[1,1,32,4096]{3,2,1,0:T(8,128)(2,1)}, u32[]{:S(2)}) copy-start(bf16[1,1,32,4096]{3,2,1,0:T(8,128)(2,1)} %param.11) | copy-start | bytes 786436
  16.3 4.7 %copy-start.1 = (f32[256]{0:T(256)}, f32[256]{0:T(256)S(1)}, u32[]{:S(2)}) copy-start(f32[256]{0:T(256)S(1)} %add_rsqrt_fusion.1) | copy-start | bytes 3076
  21.5 14.8 %slice-start = ((f32[256]{0:T(256)}), f32[128]{0:T(128)S(1)}, s32[]{:S(2)}) async-start(f32[256]{0:T(256)} %copy-done.1), calls=%async_computation.1 | async-start | bytes 1024 | tf_op jit(solution)/shard_map/slice | solution.py:149
  22.4 13.3 %all-to-all-start = ((f32[32,2,128]{2,1,0:T(2,128)}), f32[32,2,128]{2,1,0:T(2,128)S(1)}, u32[]{:S(2)}, u32[]{:S(2)}) async-start(f32[32,2,128]{2,1,0:T(2,128)} %broadcast_in_dim.74), calls=%async_computation | async-start | bytes 65536 | tf_op jit(solution)/shard_map/all_to_all | solution.py:22
  28.4 7.8 %collective-permute-start.4 = (f32[128,192]{0,1:T(8,128)S(1)}, f32[128,192]{0,1:T(8,128)S(1)}, u32[]{:S(2)}, u32[]{:S(2)}) collective-permute-start(f32[128,192]{0,1:T(8,128)S(1)} %pad_maximum_fusion.1), channel_id=1, source_target_pairs={{0,4},{4,0},{8,12},{12,8},{16,20},{20,16},{24,28},{28,24},{1,5},{5... | collective-permute-start | bytes 294920 | tf_op jit(solution)/shard_map/ppermute | solution.py:144
  28.8 4.2 %collective-permute-start.5 = (bf16[128,192]{0,1:T(8,128)(2,1)S(1)}, bf16[128,192]{0,1:T(8,128)(2,1)S(1)}, u32[]{:S(2)}, u32[]{:S(2)}) collective-permute-start(bf16[128,192]{0,1:T(8,128)(2,1)S(1)} %pad_maximum_fusion.3), channel_id=1, source_target_pairs={{0,8},{4,12},{8,0},{12,4},{16,24},{20,28},{24,16},{28,20},{1,9},{5... | collective-permute-start | bytes 147464 | tf_op jit(solution)/shard_map/ppermute | solution.py:144
  30.5 3.9 %collective-permute-start.6 = (bf16[128,192]{0,1:T(8,128)(2,1)S(1)}, bf16[128,192]{0,1:T(8,128)(2,1)S(1)}, u32[]{:S(2)}, u32[]{:S(2)}) collective-permute-start(bf16[128,192]{0,1:T(8,128)(2,1)S(1)} %pad_maximum_fusion.4), channel_id=1, source_target_pairs={{0,12},{4,8},{8,4},{12,0},{16,28},{20,24},{24,20},{28,16},{1,13},{... | collective-permute-start | bytes 147464 | tf_op jit(solution)/shard_map/ppermute | solution.py:144

commit v5 on v3

--- a/solution.py
+++ b/solution.py
@@ -63,14 +63,24 @@
     kv_slots = [own_kv] + [xor_permute(own_kv, "context", k) for k in range(1, context_count)]
 
     cot_own = cotangent[0, 0]
-    cot_pieces = [cot_own] + [xor_permute(cot_own, "tensor", m) for m in range(1, tensor_count)]
+    _, features = cot_own.shape
+    split = features // 2
     weight_t = with_layout_constraint(jnp.transpose(out_weight), Layout(major_to_minor=(0, 1)))
-    product = lax.dot_general(
-        jnp.stack(cot_pieces, axis=0),
-        weight_t,
-        (((2,), (0,)), ((), ())),
-        preferred_element_type=jnp.float32,
-    ).astype(jnp.bfloat16)
+    product = None
+    for lo, hi in ((0, split), (split, features)):
+        cot_half = cot_own[:, lo:hi]
+        pieces = [cot_half] + [xor_permute(cot_half, "tensor", m) for m in range(1, tensor_count)]
+        partial = lax.dot_general(
+            jnp.stack(pieces, axis=0),
+            weight_t[lo:hi],
+            (((2,), (0,)), ((), ())),
+            preferred_element_type=jnp.float32,
+        )
+        if product is None:
+            product = lax.optimization_barrier(partial)
+        else:
+            product = product + partial
+    product = product.astype(jnp.bfloat16)
     order = tensor_pos ^ jnp.arange(tensor_count, dtype=jnp.int32)
     grad_attn = jnp.take(product, order, axis=0).reshape(block_rows, head_count, head_size)
 

time: 37.4 us -> 44.6 us (1.19)
  starting transfers between devices: 11.7 us -> 16.3 us
  waiting for transfers between devices: 6.68 us -> 8.62 us
  local copies, waits for them, and re-layouts: 11.2 us -> 12.2 us
    ppermute x4 -> x7, starting transfers between devices: 4.65 us -> 8.27 us  [xor_permute(): lax.ppermute(value, axis, [(source, source ^ mask) for source in range(si...]
    ppermute x4 -> x7, waiting for transfers between devices: 2.48 us -> 4.42 us  [xor_permute(): lax.ppermute(value, axis, [(source, source ^ mask) for source in range(si...]
    another operation x2 -> x3, local copies, waits for them, and re-layouts: 0.01 us -> 1.03 us  [the longest x1 1.02 us: shard_body(): jnp.stack(pieces, axis=0)]
    all_to_all x1, starting transfers between devices: 4.93 us -> 5.88 us  [all_sum(): pieces = lax.all_to_all(spread, MESH_AXES, 0, 0, tiled=True)]
    dot_general x1 -> x2, matrix products: 2.91 us -> 2.48 us  [shard_body(): lax.dot_general(jnp.stack(pieces, axis=0), weight_t[lo:hi], (((2,), (0,))...]
  transfers between devices with their start and end apart: 8 -> 11, of which waited for: 4 -> 5; matrix products, arithmetic and copies ran while one was open for 29% -> 29% of each run, Pallas kernels for 0% -> 0%
where the time goes in v5:
time: 44.6 us; the launch traced here: 44.2 us
  starting transfers between devices  16.3 us (37%)
  local copies, waits for them, and re-layouts  12.2 us (27%)
  waiting for transfers between devices  8.62 us (19%)
  matrix products  4.18 us (9%)
  other arithmetic  1.91 us (4%)
  between operations  1.08 us (2%)
    ppermute x7, starting transfers between devices, xor_permute(): lax.ppermute(value, axis, [(source, source ^ mask) for source in range(si...  8.27 us
    unnamed x14, local copies, waits for them, and re-layouts  7.32 us
    all_to_all x1, starting transfers between devices, all_sum(): pieces = lax.all_to_all(spread, MESH_AXES, 0, 0, tiled=True)  5.88 us
    ppermute x7, waiting for transfers between devices, xor_permute(): lax.ppermute(value, axis, [(source, source ^ mask) for source in range(si...  4.42 us
    ppermute x3, waiting for transfers between devices, shard_body(): lax.ppermute(term, ('tensor', 'context'), pairs).astype(jnp.float32)  2.89 us
    dot_general x2, matrix products, shard_body(): lax.dot_general(jnp.stack(pieces, axis=0), weight_t[lo:hi], (((2,), (0,))...  2.48 us
    ppermute x3, starting transfers between devices, shard_body(): lax.ppermute(term, ('tensor', 'context'), pairs).astype(jnp.float32)  2.1 us
    all_to_all x1, waiting for transfers between devices, all_sum(): pieces = lax.all_to_all(spread, MESH_AXES, 0, 0, tiled=True)  1.31 us
  transfers between devices with their start and end apart: 11, of which 5 were waited for; matrix products, arithmetic and copies ran while one was open for 29% of the time, Pallas kernels for 0%

profile of v5, /device:TPU:0, one launch (start us, length us, event | category | flops | bytes accessed | tf_op | source)
XLA Modules:
  0.0 44.2 jit_solution(3963605535828320134)
XLA Ops:
  0.6 1.0 %slice_bitcast_fusion.23 = (bf16[1,32,2048]{2,1,0:T(8,128)(2,1)S(1)}, bf16[1,32,2048]{2,1,0:T(8,128)(2,1)S(1)}, bf16[32,2048]{1,0:T(8,128)(2,1)S(1)}, bf16[32,2048]{1,0:T(8,128)(2,1)S(1)}) fusion(bf16[32,4096]{1,0:T(8,128)(2,1)} %bitcast.180), kind=kLoop, calls=%fused_computation.164 | loop fusion | bytes 786432 | tf_op jit(solution)/shard_map/stack | solution.py:74
  1.7 3.0 %collective-permute-start.4 = (bf16[32,2048]{1,0:T(8,128)(2,1)S(1)}, bf16[32,2048]{1,0:T(8,128)(2,1)S(1)}, u32[]{:S(2)}, u32[]{:S(2)}) collective-permute-start(bf16[32,2048]{1,0:T(8,128)(2,1)S(1)} %get-tuple-element.23), channel_id=1, source_target_pairs={{0,8},{8,0},{16,24},{24,16},{1,9},{9,1},{17,25},{25,17},{2,10},{10... | collective-permute-start | bytes 393224 | tf_op jit(solution)/shard_map/ppermute | solution.py:16
  4.7 1.5 %collective-permute-start.5 = (bf16[32,2048]{1,0:T(8,128)(2,1)S(1)}, bf16[32,2048]{1,0:T(8,128)(2,1)S(1)}, u32[]{:S(2)}, u32[]{:S(2)}) collective-permute-start(bf16[32,2048]{1,0:T(8,128)(2,1)S(1)} %get-tuple-element.23), channel_id=1, source_target_pairs={{0,16},{8,24},{16,0},{24,8},{1,17},{9,25},{17,1},{25,9},{2,18},{10... | collective-permute-start | bytes 393224 | tf_op jit(solution)/shard_map/ppermute | solution.py:16
  6.2 0.5 %collective-permute-start.1 = (bf16[32,2048]{1,0:T(8,128)(2,1)S(1)}, bf16[32,2048]{1,0:T(8,128)(2,1)S(1)}, u32[]{:S(2)}, u32[]{:S(2)}) collective-permute-start(bf16[32,2048]{1,0:T(8,128)(2,1)S(1)} %get-tuple-element.24), channel_id=1, source_target_pairs={{0,8},{8,0},{16,24},{24,16},{1,9},{9,1},{17,25},{25,17},{2,10},{10... | collective-permute-start | bytes 393224 | tf_op jit(solution)/shard_map/ppermute | solution.py:16
  6.8 0.8 %constant_dynamic-slice_fusion.1 = (bf16[1,1,128,128]{3,2,1,0:T(8,128)(2,1)S(1)}, bf16[1,1,128,128]{3,2,1,0:T(8,128)(2,1)S(1)}) fusion(bf16[1,1,128,256]{3,2,1,0:T(8,128)(2,1)} %param.10, s32[]{:T(128)S(6)} %select_n.85, bf16[1,1,128,256]{3,2,1,0:T(8,128)(2,1)} %param.9), kind=kLoop, calls=%fused_computation.89 | loop fusion | bytes 131076 | tf_op jit(solution)/shard_map/dynamic_slice | solution.py:59
  7.7 0.1 copy.28
  8.0 6.5 %copy.31 = bf16[512,4096]{0,1:T(8,128)(2,1)} copy(bf16[512,4096]{1,0:T(8,128)(2,1)} %param.12) | data formatting | bytes 8388608 | tf_op args[4]
  14.7 0.6 %gather_fusion = s32[2]{0:T(128)S(1)} fusion(s32[2]{0:T(128)S(1)} %bitcast.167, s32[1024]{0:T(1024)S(1)} %pad_clamp_fusion.1), kind=kCustom, calls=%fused_computation | custom fusion | bytes 24 | tf_op jit(solution)/shard_map/jit(_take)/gather | solution.py:89
  15.8 3.0 %collective-permute-start.3 = (bf16[32,2048]{1,0:T(8,128)(2,1)S(1)}, bf16[32,2048]{1,0:T(8,128)(2,1)S(1)}, u32[]{:S(2)}, u32[]{:S(2)}) collective-permute-start(bf16[32,2048]{1,0:T(8,128)(2,1)S(1)} %get-tuple-element.24), channel_id=1, source_target_pairs={{0,24},{8,16},{16,8},{24,0},{1,25},{9,17},{17,9},{25,1},{2,26},{10... | collective-permute-start | bytes 393224 | tf_op jit(solution)/shard_map/ppermute | solution.py:16
  18.9 0.4 fusion.81
  19.4 3.5 %collective-permute-done.3 = bf16[32,2048]{1,0:T(8,128)(2,1)S(1)} collective-permute-done((bf16[32,2048]{1,0:T(8,128)(2,1)S(1)}, bf16[32,2048]{1,0:T(8,128)(2,1)S(1)}, u32[]{:S(2)}, u32[]{:S(2)}) %collective-permute-start.3) | collective-permute-done | bytes 131104 | tf_op jit(solution)/shard_map/ppermute | solution.py:16
  22.9 2.0 %fusion.3 = f32[4,32,512]{2,1,0:T(8,128)S(1)} fusion(bf16[4096,512]{1,0:T(8,128)(2,1)} %bitcast.168, bf16[1,32,2048]{2,1,0:T(8,128)(2,1)S(1)} %bitcast.188, bf16[1,32,2048]{2,1,0:T(8,128)(2,1)S(1)} %bitcast.187, bf16[1,32,2048]{2,1,0:T(8,128)(2,1)S(1)} %bitcast.186, bf16[1,32,2048]{2,1,0:T(8,128)(2,1)S(1)} %get-tuple-element.22), kind=kOutput, calls=%fused_computation.7 | convolution fusion | flops 269221888 | bytes 2883584 | tf_op jit(solution)/shard_map/dot_general | solution.py:73
  25.0 0.9 %collective-permute-done.6 = bf16[32,2048]{1,0:T(8,128)(2,1)S(1)} collective-permute-done((bf16[32,2048]{1,0:T(8,128)(2,1)S(1)}, bf16[32,2048]{1,0:T(8,128)(2,1)S(1)}, u32[]{:S(2)}, u32[]{:S(2)}) %collective-permute-start.6) | collective-permute-done | bytes 131104 | tf_op jit(solution)/shard_map/ppermute | solution.py:16
  25.9 0.4 %fusion.2 = f32[4,32,512]{2,1,0:T(8,128)S(1)} fusion(bf16[4096,512]{1,0:T(8,128)(2,1)S(1)} %bitcast.169, bf16[1,32,2048]{2,1,0:T(8,128)(2,1)S(1)} %bitcast.189, bf16[1,32,2048]{2,1,0:T(8,128)(2,1)S(1)} %bitcast.185, bf16[1,32,2048]{2,1,0:T(8,128)(2,1)S(1)} %bitcast.184, bf16[1,32,2048]{2,1,0:T(8,128)(2,1)S(1)} %get-tuple-element.21), kind=kOutput, calls=%fused_computation.5 | convolution fusion | flops 269221888 | bytes 2883584 | tf_op jit(solution)/shard_map/dot_general | solution.py:73
  26.4 0.6 %gather_fusion.1 = bf16[4,32,512]{2,1,0:T(8,128)(2,1)S(1)} fusion(bf16[4,32,512]{2,1,0:T(8,128)(2,1)S(1)} %add_convert_fusion, s32[1024]{0:T(1024)S(1)} %pad_clamp_fusion), kind=kCustom, calls=%fused_computation.1 | custom fusion | bytes 262160 | tf_op jit(solution)/shard_map/jit(_take)/gather | solution.py:85
  27.0 0.1 copy.32
  27.1 0.2 convolution_bitcast_fusion
  27.4 0.4 multiply_reduce_fusion.4
  27.8 0.4 multiply_reduce_fusion.1
  28.2 0.2 convolution_bitcast_fusion.2
  28.5 0.6 %broadcast_in_dim.55 = f32[32,2,128]{2,1,0:T(2,128)} broadcast(f32[2,128]{1,0:T(2,128)S(1)} %pad_maximum_fusion.5), dimensions={1,2} | broadcast | bytes 33792 | tf_op jit(solution)/shard_map/broadcast_in_dim | solution.py:21
  29.1 5.9 %all-to-all-start = ((f32[32,2,128]{2,1,0:T(2,128)}), f32[32,2,128]{2,1,0:T(2,128)S(1)}, u32[]{:S(2)}, u32[]{:S(2)}) async-start(f32[32,2,128]{2,1,0:T(2,128)} %broadcast_in_dim.55), calls=%async_computation | async-start | bytes 65536 | tf_op jit(solution)/shard_map/all_to_all | solution.py:22
  35.1 0.3 collective-permute-start.7
  35.4 1.7 %collective-permute-start.8 = (bf16[128,192]{0,1:T(8,128)(2,1)S(1)}, bf16[128,192]{0,1:T(8,128)(2,1)S(1)}, u32[]{:S(2)}, u32[]{:S(2)}) collective-permute-start(bf16[128,192]{0,1:T(8,128)(2,1)S(1)} %pad_maximum_fusion.3), channel_id=1, source_target_pairs={{0,8},{4,12},{8,0},{12,4},{16,24},{20,28},{24,16},{28,20},{1,9},{5... | collective-permute-start | bytes 147464 | tf_op jit(solution)/shard_map/ppermute | solution.py:150
  37.2 0.1 multiply_convert_fusion
  37.3 0.8 %copy.38 = bf16[1,1,128,512]{3,2,1,0:T(8,128)(2,1)} copy(bf16[1,1,128,512]{2,3,1,0:T(8,128)(2,1)S(1)} %bitcast.175) | data formatting | bytes 262144
  38.1 1.5 %collective-permute-done.8 = bf16[128,192]{0,1:T(8,128)(2,1)S(1)} collective-permute-done((bf16[128,192]{0,1:T(8,128)(2,1)S(1)}, bf16[128,192]{0,1:T(8,128)(2,1)S(1)}, u32[]{:S(2)}, u32[]{:S(2)}) %collective-permute-start.8) | collective-permute-done | bytes 49184 | tf_op jit(solution)/shard_map/ppermute | solution.py:150
  39.6 1.4 %collective-permute-done.9 = bf16[128,192]{0,1:T(8,128)(2,1)S(1)} collective-permute-done((bf16[128,192]{0,1:T(8,128)(2,1)S(1)}, bf16[128,192]{0,1:T(8,128)(2,1)S(1)}, u32[]{:S(2)}, u32[]{:S(2)}) %collective-permute-start.9) | collective-permute-done | bytes 49184 | tf_op jit(solution)/shard_map/ppermute | solution.py:150
  41.0 1.3 %all-to-all-done = f32[32,2,128]{2,1,0:T(2,128)S(1)} async-done(((f32[32,2,128]{2,1,0:T(2,128)}), f32[32,2,128]{2,1,0:T(2,128)S(1)}, u32[]{:S(2)}, u32[]{:S(2)}) %all-to-all-start) | async-done | bytes 32800 | tf_op jit(solution)/shard_map/all_to_all | solution.py:22
  42.4 0.5 %slice_bitcast_fusion.21 = (f32[128]{0:T(128)}, f32[128]{0:T(128)}) fusion(f32[2,128]{1,0:T(2,128)S(1)} %fusion.50), kind=kLoop, calls=%fused_computation.148 | loop fusion | bytes 2048 | tf_op jit(solution)/shard_map/squeeze | solution.py:169
  43.0 0.6 %fusion.41 = bf16[1,1,128,64]{2,3,1,0:T(8,128)(2,1)} fusion(f32[128,128]{0,1:T(8,128)S(1)} %get-tuple-element.27, s32[]{:T(128)S(6)} %select_n.94, f32[128,128]{0,1:T(8,128)S(1)} %get-tuple-element.18, f32[128]{0:T(128)S(1)} %slice-done, f32[128]{0:T(128)S(1)} %broadcast_multiply_fusion.1), kind=kLoop, calls=%fused_computation.80 | loop fusion | flops 32768 | bytes 82948 | tf_op jit(solution)/shard_map/reshape | solution.py:159
  43.6 0.6 %fusion.42 = bf16[1,1,128,64]{2,3,1,0:T(8,128)(2,1)} fusion(f32[128,192]{0,1:T(8,128)S(1)} %convert_element_type.55, f32[128,192]{0,1:T(8,128)S(1)} %convert_element_type.54, f32[128,192]{0,1:T(8,128)S(1)} %collective-permute-done.7, f32[128,128]{0,1:T(8,128)S(1)} %get-tuple-element.30, s32[]{:T(128)S(6)} %select_n.94), kind=kLoop, calls=%fused_computation.81 | loop fusion | flops 32768 | bytes 147460 | tf_op jit(solution)/shard_map/reshape | solution.py:162
  (61 shorter events, 1.4 us)
Async XLA Ops:
  0.6 14.1 %copy-start = (s32[1,2]{1,0:T(1,128)S(1)}, s32[1,2]{1,0:T(1,128)}, u32[]{:S(2)}) copy-start(s32[1,2]{1,0:T(1,128)} %param.15) | copy-start | bytes 28
  1.7 23.3 %collective-permute-start.4 = (bf16[32,2048]{1,0:T(8,128)(2,1)S(1)}, bf16[32,2048]{1,0:T(8,128)(2,1)S(1)}, u32[]{:S(2)}, u32[]{:S(2)}) collective-permute-start(bf16[32,2048]{1,0:T(8,128)(2,1)S(1)} %get-tuple-element.23), channel_id=1, source_target_pairs={{0,8},{8,0},{16,24},{24,16},{1,9},{9,1},{17,25},{25,17},{2,10},{10... | collective-permute-start | bytes 393224 | tf_op jit(solution)/shard_map/ppermute | solution.py:16
  4.7 20.3 %collective-permute-start.5 = (bf16[32,2048]{1,0:T(8,128)(2,1)S(1)}, bf16[32,2048]{1,0:T(8,128)(2,1)S(1)}, u32[]{:S(2)}, u32[]{:S(2)}) collective-permute-start(bf16[32,2048]{1,0:T(8,128)(2,1)S(1)} %get-tuple-element.23), channel_id=1, source_target_pairs={{0,16},{8,24},{16,0},{24,8},{1,17},{9,25},{17,1},{25,9},{2,18},{10... | collective-permute-start | bytes 393224 | tf_op jit(solution)/shard_map/ppermute | solution.py:16
  6.2 13.1 %collective-permute-start.1 = (bf16[32,2048]{1,0:T(8,128)(2,1)S(1)}, bf16[32,2048]{1,0:T(8,128)(2,1)S(1)}, u32[]{:S(2)}, u32[]{:S(2)}) collective-permute-start(bf16[32,2048]{1,0:T(8,128)(2,1)S(1)} %get-tuple-element.24), channel_id=1, source_target_pairs={{0,8},{8,0},{16,24},{24,16},{1,9},{9,1},{17,25},{25,17},{2,10},{10... | collective-permute-start | bytes 393224 | tf_op jit(solution)/shard_map/ppermute | solution.py:16
  6.8 12.7 %collective-permute-start.2 = (bf16[32,2048]{1,0:T(8,128)(2,1)S(1)}, bf16[32,2048]{1,0:T(8,128)(2,1)S(1)}, u32[]{:S(2)}, u32[]{:S(2)}) collective-permute-start(bf16[32,2048]{1,0:T(8,128)(2,1)S(1)} %get-tuple-element.24), channel_id=1, source_target_pairs={{0,16},{8,24},{16,0},{24,8},{1,17},{9,25},{17,1},{25,9},{2,18},{10... | collective-permute-start | bytes 393224 | tf_op jit(solution)/shard_map/ppermute | solution.py:16
  7.8 8.0 %collective-permute-start = (bf16[128,256]{0,1:T(8,128)(2,1)S(1)}, bf16[128,256]{0,1:T(8,128)(2,1)S(1)}, u32[]{:S(2)}, u32[]{:S(2)}) collective-permute-start(bf16[128,256]{0,1:T(8,128)(2,1)S(1)} %pad_maximum_fusion.2), channel_id=1, source_target_pairs={{0,4},{4,0},{1,5},{5,1},{2,6},{6,2},{3,7},{7,3},{8,12},{12,8},{9,1... | collective-permute-start | bytes 196616 | tf_op jit(solution)/shard_map/ppermute | solution.py:16
  8.0 7.5 %copy-start.2 = (bf16[1,1,128,512]{3,2,1,0:T(8,128)(2,1)S(1)}, bf16[1,1,128,512]{3,2,1,0:T(8,128)(2,1)}, u32[]{:S(2)}) copy-start(bf16[1,1,128,512]{3,2,1,0:T(8,128)(2,1)} %param.8) | copy-start | bytes 393220
  8.0 10.9 %copy-start.4 = (f32[128]{0:T(128)S(1)}, f32[128]{0:T(128)}, u32[]{:S(2)}) copy-start(f32[128]{0:T(128)} %param.14) | copy-start | bytes 1540
  8.0 10.9 %copy-start.5 = (f32[128]{0:T(128)S(1)}, f32[128]{0:T(128)}, u32[]{:S(2)}) copy-start(f32[128]{0:T(128)} %param.13) | copy-start | bytes 1540
  15.8 7.1 %collective-permute-start.3 = (bf16[32,2048]{1,0:T(8,128)(2,1)S(1)}, bf16[32,2048]{1,0:T(8,128)(2,1)S(1)}, u32[]{:S(2)}, u32[]{:S(2)}) collective-permute-start(bf16[32,2048]{1,0:T(8,128)(2,1)S(1)} %get-tuple-element.24), channel_id=1, source_target_pairs={{0,24},{8,16},{16,8},{24,0},{1,25},{9,17},{17,9},{25,1},{2,26},{10... | collective-permute-start | bytes 393224 | tf_op jit(solution)/shard_map/ppermute | solution.py:16
  18.8 8.9 %copy-start.3 = (f32[256]{0:T(256)}, f32[256]{0:T(256)S(1)}, u32[]{:S(2)}) copy-start(f32[256]{0:T(256)S(1)} %add_rsqrt_fusion.1) | copy-start | bytes 3076
  19.3 6.6 %copy-start.1 = (bf16[512,4096]{0,1:T(8,128)(2,1)S(1)}, bf16[512,4096]{0,1:T(8,128)(2,1)}, u32[]{:S(2)}) copy-start(bf16[512,4096]{0,1:T(8,128)(2,1)} %copy.31) | copy-start | bytes 12582916
  19.3 6.6 %collective-permute-start.6 = (bf16[32,2048]{1,0:T(8,128)(2,1)S(1)}, bf16[32,2048]{1,0:T(8,128)(2,1)S(1)}, u32[]{:S(2)}, u32[]{:S(2)}) collective-permute-start(bf16[32,2048]{1,0:T(8,128)(2,1)S(1)} %get-tuple-element.23), channel_id=1, source_target_pairs={{0,24},{8,16},{16,8},{24,0},{1,25},{9,17},{17,9},{25,1},{2,26},{10... | collective-permute-start | bytes 393224 | tf_op jit(solution)/shard_map/ppermute | solution.py:16
  28.2 14.8 %slice-start = ((f32[256]{0:T(256)}), f32[128]{0:T(128)S(1)}, s32[]{:S(2)}) async-start(f32[256]{0:T(256)} %copy-done.3), calls=%async_computation.1 | async-start | bytes 1024 | tf_op jit(solution)/shard_map/slice | solution.py:155
  29.1 13.2 %all-to-all-start = ((f32[32,2,128]{2,1,0:T(2,128)}), f32[32,2,128]{2,1,0:T(2,128)S(1)}, u32[]{:S(2)}, u32[]{:S(2)}) async-start(f32[32,2,128]{2,1,0:T(2,128)} %broadcast_in_dim.55), calls=%async_computation | async-start | bytes 65536 | tf_op jit(solution)/shard_map/all_to_all | solution.py:22
  35.1 7.8 %collective-permute-start.7 = (f32[128,192]{0,1:T(8,128)S(1)}, f32[128,192]{0,1:T(8,128)S(1)}, u32[]{:S(2)}, u32[]{:S(2)}) collective-permute-start(f32[128,192]{0,1:T(8,128)S(1)} %pad_maximum_fusion.1), channel_id=1, source_target_pairs={{0,4},{4,0},{8,12},{12,8},{16,20},{20,16},{24,28},{28,24},{1,5},{5... | collective-permute-start | bytes 294920 | tf_op jit(solution)/shard_map/ppermute | solution.py:150
  35.4 4.2 %collective-permute-start.8 = (bf16[128,192]{0,1:T(8,128)(2,1)S(1)}, bf16[128,192]{0,1:T(8,128)(2,1)S(1)}, u32[]{:S(2)}, u32[]{:S(2)}) collective-permute-start(bf16[128,192]{0,1:T(8,128)(2,1)S(1)} %pad_maximum_fusion.3), channel_id=1, source_target_pairs={{0,8},{4,12},{8,0},{12,4},{16,24},{20,28},{24,16},{28,20},{1,9},{5... | collective-permute-start | bytes 147464 | tf_op jit(solution)/shard_map/ppermute | solution.py:150
  37.1 3.9 %collective-permute-start.9 = (bf16[128,192]{0,1:T(8,128)(2,1)S(1)}, bf16[128,192]{0,1:T(8,128)(2,1)S(1)}, u32[]{:S(2)}, u32[]{:S(2)}) collective-permute-start(bf16[128,192]{0,1:T(8,128)(2,1)S(1)} %pad_maximum_fusion.4), channel_id=1, source_target_pairs={{0,12},{4,8},{8,4},{12,0},{16,28},{20,24},{24,20},{28,16},{1,13},{... | collective-permute-start | bytes 147464 | tf_op jit(solution)/shard_map/ppermute | solution.py:150

commit v6 on v5

--- a/solution.py
+++ b/solution.py
@@ -63,23 +63,20 @@
     kv_slots = [own_kv] + [xor_permute(own_kv, "context", k) for k in range(1, context_count)]
 
     cot_own = cotangent[0, 0]
-    _, features = cot_own.shape
+    cot_pieces = [cot_own] + [xor_permute(cot_own, "tensor", m) for m in range(1, tensor_count)]
+    weight_t = with_layout_constraint(jnp.transpose(out_weight), Layout(major_to_minor=(0, 1)))
+    stacked = jnp.stack(cot_pieces, axis=0)
+    features = stacked.shape[2]
     split = features // 2
-    weight_t = with_layout_constraint(jnp.transpose(out_weight), Layout(major_to_minor=(0, 1)))
     product = None
     for lo, hi in ((0, split), (split, features)):
-        cot_half = cot_own[:, lo:hi]
-        pieces = [cot_half] + [xor_permute(cot_half, "tensor", m) for m in range(1, tensor_count)]
         partial = lax.dot_general(
-            jnp.stack(pieces, axis=0),
+            stacked[:, :, lo:hi],
             weight_t[lo:hi],
             (((2,), (0,)), ((), ())),
             preferred_element_type=jnp.float32,
         )
-        if product is None:
-            product = lax.optimization_barrier(partial)
-        else:
-            product = product + partial
+        product = lax.optimization_barrier(partial) if product is None else product + partial
     product = product.astype(jnp.bfloat16)
     order = tensor_pos ^ jnp.arange(tensor_count, dtype=jnp.int32)
     grad_attn = jnp.take(product, order, axis=0).reshape(block_rows, head_count, head_size)

time: 44.6 us -> 37.3 us (0.84)
  starting transfers between devices: 16.3 us -> 11.7 us
  waiting for transfers between devices: 8.62 us -> 6.67 us
  local copies, waits for them, and re-layouts: 12.2 us -> 11.2 us
    ppermute x7 -> x4, starting transfers between devices: 8.27 us -> 4.65 us  [xor_permute(): lax.ppermute(value, axis, [(source, source ^ mask) for source in range(si...]
    ppermute x7 -> x4, waiting for transfers between devices: 4.42 us -> 2.47 us  [xor_permute(): lax.ppermute(value, axis, [(source, source ^ mask) for source in range(si...]
    another operation x3 -> x2, local copies, waits for them, and re-layouts: 1.03 us -> 0.01 us  [the longest x1 1.02 us: shard_body(): jnp.stack(pieces, axis=0)]
    all_to_all x1, starting transfers between devices: 5.88 us -> 4.94 us  [all_sum(): pieces = lax.all_to_all(spread, MESH_AXES, 0, 0, tiled=True)]
    unnamed x14 -> x16, local copies, waits for them, and re-layouts: 7.32 us -> 7.36 us
  transfers between devices with their start and end apart: 11 -> 8, of which waited for: 5 -> 4; matrix products, arithmetic and copies ran while one was open for 29% -> 29% of each run, Pallas kernels for 0% -> 0%
where the time goes in v6:
time: 37.3 us; the launch traced here: 36.9 us
  starting transfers between devices  11.7 us (31%)
  local copies, waits for them, and re-layouts  11.2 us (30%)
  waiting for transfers between devices  6.67 us (18%)
  matrix products  4.28 us (11%)
  other arithmetic  2 us (5%)
  between operations  1.08 us (3%)
    unnamed x16, local copies, waits for them, and re-layouts  7.36 us
    all_to_all x1, starting transfers between devices, all_sum(): pieces = lax.all_to_all(spread, MESH_AXES, 0, 0, tiled=True)  4.94 us
    ppermute x4, starting transfers between devices, xor_permute(): lax.ppermute(value, axis, [(source, source ^ mask) for source in range(si...  4.65 us
    ppermute x3, waiting for transfers between devices, shard_body(): lax.ppermute(term, ('tensor', 'context'), pairs).astype(jnp.float32)  2.89 us
    dot_general x2, matrix products, shard_body(): lax.dot_general(stacked[:, :, lo:hi], weight_t[lo:hi], (((2,), (0,)), (()...  2.51 us
    ppermute x4, waiting for transfers between devices, xor_permute(): lax.ppermute(value, axis, [(source, source ^ mask) for source in range(si...  2.47 us
    ppermute x3, starting transfers between devices, shard_body(): lax.ppermute(term, ('tensor', 'context'), pairs).astype(jnp.float32)  2.1 us
    all_to_all x1, waiting for transfers between devices, all_sum(): pieces = lax.all_to_all(spread, MESH_AXES, 0, 0, tiled=True)  1.31 us
  transfers between devices with their start and end apart: 8, of which 4 were waited for; matrix products, arithmetic and copies ran while one was open for 29% of the time, Pallas kernels for 0%

profile of v6, /device:TPU:0, one launch (start us, length us, event | category | flops | bytes accessed | tf_op | source)
XLA Modules:
  0.0 36.9 jit_solution(17024654965963405042)
XLA Ops:
  0.6 3.0 %collective-permute-start.1 = (bf16[32,4096]{1,0:T(8,128)(2,1)}, bf16[32,4096]{1,0:T(8,128)(2,1)S(1)}, u32[]{:S(2)}, u32[]{:S(2)}) collective-permute-start(bf16[32,4096]{1,0:T(8,128)(2,1)} %bitcast.178), channel_id=1, source_target_pairs={{0,8},{8,0},{16,24},{24,16},{1,9},{9,1},{17,25},{25,17},{2,10},{10... | collective-permute-start | bytes 786440 | tf_op jit(solution)/shard_map/ppermute | solution.py:16
  3.7 1.5 %collective-permute-start.2 = (bf16[32,4096]{1,0:T(8,128)(2,1)}, bf16[32,4096]{1,0:T(8,128)(2,1)S(1)}, u32[]{:S(2)}, u32[]{:S(2)}) collective-permute-start(bf16[32,4096]{1,0:T(8,128)(2,1)} %bitcast.179), channel_id=1, source_target_pairs={{0,16},{8,24},{16,0},{24,8},{1,17},{9,25},{17,1},{25,9},{2,18},{10... | collective-permute-start | bytes 786440 | tf_op jit(solution)/shard_map/ppermute | solution.py:16
  5.2 0.8 %constant_dynamic-slice_fusion.1 = (bf16[1,1,128,128]{3,2,1,0:T(8,128)(2,1)S(1)}, bf16[1,1,128,128]{3,2,1,0:T(8,128)(2,1)S(1)}) fusion(bf16[1,1,128,256]{3,2,1,0:T(8,128)(2,1)} %param.10, s32[]{:T(128)S(6)} %select_n.85, bf16[1,1,128,256]{3,2,1,0:T(8,128)(2,1)} %param.9), kind=kLoop, calls=%fused_computation.79 | loop fusion | bytes 131076 | tf_op jit(solution)/shard_map/dynamic_slice | solution.py:59
  6.0 0.1 copy.27
  6.1 0.1 copy.28
  6.4 6.5 %copy.31 = bf16[512,4096]{0,1:T(8,128)(2,1)} copy(bf16[512,4096]{1,0:T(8,128)(2,1)} %param.12) | data formatting | bytes 8388608 | tf_op args[4]
  13.2 0.6 %gather_fusion = s32[2]{0:T(128)S(1)} fusion(s32[2]{0:T(128)S(1)} %bitcast.165, s32[1024]{0:T(1024)S(1)} %pad_clamp_fusion.1), kind=kCustom, calls=%fused_computation | custom fusion | bytes 24 | tf_op jit(solution)/shard_map/jit(_take)/gather | solution.py:86
  14.1 0.1 broadcast_compare_fusion
  14.4 0.4 %fusion.69 = (f32[4,128]{1,0:T(4,128)S(1)}, f32[4,128,256]{1,2,0:T(8,128)S(1)}) fusion(pred[128,256]{0,1:T(8,128)(4,1)S(1)} %broadcast_compare_fusion, f32[128]{0:T(128)S(1)} %copy-done.5, f32[256]{0:T(256)S(1)} %add_rsqrt_fusion.1, bf16[256,256]{0,1:T(8,128)(2,1)S(1)} %pad_maximum_fusion.1, f32[128,4,128]{0,2,1:T(8,128)S(1)} %bitcast.169, ...), kind=kOutput, calls=%fused_computation.154 | convolution fusion | flops 34406656 | bytes 890880 | tf_op jit(solution)/shard_map/sub | solution.py:106
  14.8 2.5 %collective-permute-done.2 = bf16[32,4096]{1,0:T(8,128)(2,1)S(1)} collective-permute-done((bf16[32,4096]{1,0:T(8,128)(2,1)}, bf16[32,4096]{1,0:T(8,128)(2,1)S(1)}, u32[]{:S(2)}, u32[]{:S(2)}) %collective-permute-start.2) | collective-permute-done | bytes 262176 | tf_op jit(solution)/shard_map/ppermute | solution.py:16
  17.3 0.1 pad_maximum_fusion
  17.4 2.1 %fusion.3 = f32[4,32,512]{2,1,0:T(8,128)S(1)} fusion(bf16[4096,512]{1,0:T(8,128)(2,1)} %bitcast.166, bf16[4,32,4096]{2,1,0:T(8,128)(2,1)S(1)} %pad_maximum_fusion), kind=kOutput, calls=%fused_computation.7 | convolution fusion | flops 268435456 | bytes 2883584 | tf_op jit(solution)/shard_map/dot_general | solution.py:73
  19.5 0.5 %fusion.13 = bf16[4,32,512]{2,1,0:T(8,128)(2,1)S(1)} fusion(f32[4,32,512]{2,1,0:T(8,128)S(1)} %fusion.3, bf16[4096,512]{1,0:T(8,128)(2,1)S(1)} %bitcast.167, bf16[4,32,4096]{2,1,0:T(8,128)(2,1)S(1)} %pad_maximum_fusion), kind=kOutput, calls=%fused_computation.20 | convolution fusion | flops 268566528 | bytes 3014656 | tf_op jit(solution)/shard_map/dot_general | solution.py:73
  20.0 0.6 %gather_fusion.1 = bf16[4,32,512]{2,1,0:T(8,128)(2,1)S(1)} fusion(bf16[4,32,512]{2,1,0:T(8,128)(2,1)S(1)} %fusion.13, s32[1024]{0:T(1024)S(1)} %pad_clamp_fusion), kind=kCustom, calls=%fused_computation.1 | custom fusion | bytes 262160 | tf_op jit(solution)/shard_map/jit(_take)/gather | solution.py:82
  20.6 0.1 copy.32
  20.7 0.3 convolution_bitcast_fusion
  21.0 0.4 %multiply_reduce_fusion.4 = (f32[128]{0:T(128)S(1)}, f32[256,128]{0,1:T(8,128)S(1)}, f32[256,128]{0,1:T(8,128)S(1)}) fusion(f32[256]{0:T(256)S(1)} %add_rsqrt_fusion.1, bf16[256,256]{0,1:T(8,128)(2,1)S(1)} %pad_maximum_fusion.1, f32[4,128,256]{1,2,0:T(8,128)S(1)} %convolution_bitcast_fusion, f32[4,128,256]{1,2,0:T(8,128)S(1)} %get-tuple-element.31, ...), kind=kOutput, calls=%fused_computation.42 | convolution fusion | flops 34800256 | bytes 2695168 | tf_op jit(solution)/shard_map/hqk,qhd->kd/dot_general | solution.py:113
  21.4 0.4 %multiply_reduce_fusion.1 = (f32[128]{0:T(128)S(1)}, f32[128,4]{0,1:T(4,128)S(1)}, f32[128,4,128]{0,2,1:T(8,128)S(1)}) fusion(f32[128,4,128]{0,2,1:T(8,128)S(1)} %bitcast.171, f32[128,4]{0,1:T(4,128)S(1)} %add_rsqrt_fusion, f32[128]{0:T(128)S(1)} %copy-done.6, f32[4,128,256]{1,2,0:T(8,128)S(1)} %convolution_bitcast_fusion, ...), kind=kOutput, calls=%fused_computation.29 | convolution fusion | flops 34996352 | bytes 2697728 | tf_op jit(solution)/shard_map/hqk,kd->qhd/dot_general | solution.py:112
  21.8 0.2 convolution_bitcast_fusion.2
  22.1 0.6 %broadcast_in_dim.55 = f32[32,2,128]{2,1,0:T(2,128)} broadcast(f32[2,128]{1,0:T(2,128)S(1)} %pad_maximum_fusion.6), dimensions={1,2} | broadcast | bytes 33792 | tf_op jit(solution)/shard_map/broadcast_in_dim | solution.py:21
  22.7 4.9 %all-to-all-start = ((f32[32,2,128]{2,1,0:T(2,128)}), f32[32,2,128]{2,1,0:T(2,128)S(1)}, u32[]{:S(2)}, u32[]{:S(2)}) async-start(f32[32,2,128]{2,1,0:T(2,128)} %broadcast_in_dim.55), calls=%async_computation | async-start | bytes 65536 | tf_op jit(solution)/shard_map/all_to_all | solution.py:22
  27.7 0.3 collective-permute-start.4
  28.1 1.7 %collective-permute-start.5 = (bf16[128,192]{0,1:T(8,128)(2,1)S(1)}, bf16[128,192]{0,1:T(8,128)(2,1)S(1)}, u32[]{:S(2)}, u32[]{:S(2)}) collective-permute-start(bf16[128,192]{0,1:T(8,128)(2,1)S(1)} %pad_maximum_fusion.4), channel_id=1, source_target_pairs={{0,8},{4,12},{8,0},{12,4},{16,24},{20,28},{24,16},{28,20},{1,9},{5... | collective-permute-start | bytes 147464 | tf_op jit(solution)/shard_map/ppermute | solution.py:147
  29.9 0.1 multiply_convert_fusion
  30.0 0.8 %copy.38 = bf16[1,1,128,512]{3,2,1,0:T(8,128)(2,1)} copy(bf16[1,1,128,512]{2,3,1,0:T(8,128)(2,1)S(1)} %bitcast.173) | data formatting | bytes 262144
  30.8 1.5 %collective-permute-done.5 = bf16[128,192]{0,1:T(8,128)(2,1)S(1)} collective-permute-done((bf16[128,192]{0,1:T(8,128)(2,1)S(1)}, bf16[128,192]{0,1:T(8,128)(2,1)S(1)}, u32[]{:S(2)}, u32[]{:S(2)}) %collective-permute-start.5) | collective-permute-done | bytes 49184 | tf_op jit(solution)/shard_map/ppermute | solution.py:147
  32.3 1.4 %collective-permute-done.6 = bf16[128,192]{0,1:T(8,128)(2,1)S(1)} collective-permute-done((bf16[128,192]{0,1:T(8,128)(2,1)S(1)}, bf16[128,192]{0,1:T(8,128)(2,1)S(1)}, u32[]{:S(2)}, u32[]{:S(2)}) %collective-permute-start.6) | collective-permute-done | bytes 49184 | tf_op jit(solution)/shard_map/ppermute | solution.py:147
  33.7 1.3 %all-to-all-done = f32[32,2,128]{2,1,0:T(2,128)S(1)} async-done(((f32[32,2,128]{2,1,0:T(2,128)}), f32[32,2,128]{2,1,0:T(2,128)S(1)}, u32[]{:S(2)}, u32[]{:S(2)}) %all-to-all-start) | async-done | bytes 32800 | tf_op jit(solution)/shard_map/all_to_all | solution.py:22
  35.0 0.5 %slice_bitcast_fusion.25 = (f32[128]{0:T(128)}, f32[128]{0:T(128)}) fusion(f32[2,128]{1,0:T(2,128)S(1)} %fusion.40), kind=kLoop, calls=%fused_computation.138 | loop fusion | bytes 2048 | tf_op jit(solution)/shard_map/squeeze | solution.py:166
  35.5 0.1 multiply_reduce_fusion.5
  35.7 0.6 %fusion.31 = bf16[1,1,128,64]{2,3,1,0:T(8,128)(2,1)} fusion(f32[128,128]{0,1:T(8,128)S(1)} %get-tuple-element.23, s32[]{:T(128)S(6)} %select_n.94, f32[128,128]{0,1:T(8,128)S(1)} %get-tuple-element.18, f32[128]{0:T(128)S(1)} %slice-done, f32[128]{0:T(128)S(1)} %broadcast_multiply_fusion.1), kind=kLoop, calls=%fused_computation.70 | loop fusion | flops 32768 | bytes 82948 | tf_op jit(solution)/shard_map/reshape | solution.py:156
  36.3 0.6 %fusion.32 = bf16[1,1,128,64]{2,3,1,0:T(8,128)(2,1)} fusion(f32[128,192]{0,1:T(8,128)S(1)} %convert_element_type.55, f32[128,192]{0,1:T(8,128)S(1)} %convert_element_type.54, f32[128,192]{0,1:T(8,128)S(1)} %collective-permute-done.4, f32[128,128]{0,1:T(8,128)S(1)} %get-tuple-element.26, s32[]{:T(128)S(6)} %select_n.94), kind=kLoop, calls=%fused_computation.71 | loop fusion | flops 32768 | bytes 147460 | tf_op jit(solution)/shard_map/reshape | solution.py:159
  (56 shorter events, 0.9 us)
Async XLA Ops:
  0.6 12.5 %copy-start = (s32[1,2]{1,0:T(1,128)S(1)}, s32[1,2]{1,0:T(1,128)}, u32[]{:S(2)}) copy-start(s32[1,2]{1,0:T(1,128)} %param.15) | copy-start | bytes 28
  0.6 14.2 %collective-permute-start.1 = (bf16[32,4096]{1,0:T(8,128)(2,1)}, bf16[32,4096]{1,0:T(8,128)(2,1)S(1)}, u32[]{:S(2)}, u32[]{:S(2)}) collective-permute-start(bf16[32,4096]{1,0:T(8,128)(2,1)} %bitcast.178), channel_id=1, source_target_pairs={{0,8},{8,0},{16,24},{24,16},{1,9},{9,1},{17,25},{25,17},{2,10},{10... | collective-permute-start | bytes 786440 | tf_op jit(solution)/shard_map/ppermute | solution.py:16
  3.7 13.6 %collective-permute-start.2 = (bf16[32,4096]{1,0:T(8,128)(2,1)}, bf16[32,4096]{1,0:T(8,128)(2,1)S(1)}, u32[]{:S(2)}, u32[]{:S(2)}) collective-permute-start(bf16[32,4096]{1,0:T(8,128)(2,1)} %bitcast.179), channel_id=1, source_target_pairs={{0,16},{8,24},{16,0},{24,8},{1,17},{9,25},{17,1},{25,9},{2,18},{10... | collective-permute-start | bytes 786440 | tf_op jit(solution)/shard_map/ppermute | solution.py:16
  5.2 12.1 %collective-permute-start.3 = (bf16[32,4096]{1,0:T(8,128)(2,1)}, bf16[32,4096]{1,0:T(8,128)(2,1)S(1)}, u32[]{:S(2)}, u32[]{:S(2)}) collective-permute-start(bf16[32,4096]{1,0:T(8,128)(2,1)} %bitcast.180), channel_id=1, source_target_pairs={{0,24},{8,16},{16,8},{24,0},{1,25},{9,17},{17,9},{25,1},{2,26},{10... | collective-permute-start | bytes 786440 | tf_op jit(solution)/shard_map/ppermute | solution.py:16
  6.3 8.0 %collective-permute-start = (bf16[128,256]{0,1:T(8,128)(2,1)S(1)}, bf16[128,256]{0,1:T(8,128)(2,1)S(1)}, u32[]{:S(2)}, u32[]{:S(2)}) collective-permute-start(bf16[128,256]{0,1:T(8,128)(2,1)S(1)} %pad_maximum_fusion.3), channel_id=1, source_target_pairs={{0,4},{4,0},{1,5},{5,1},{2,6},{6,2},{3,7},{7,3},{8,12},{12,8},{9,1... | collective-permute-start | bytes 196616 | tf_op jit(solution)/shard_map/ppermute | solution.py:16
  6.4 7.6 %copy-start.3 = (bf16[1,1,128,512]{3,2,1,0:T(8,128)(2,1)S(1)}, bf16[1,1,128,512]{3,2,1,0:T(8,128)(2,1)}, u32[]{:S(2)}) copy-start(bf16[1,1,128,512]{3,2,1,0:T(8,128)(2,1)} %param.8) | copy-start | bytes 393220
  6.4 7.9 %copy-start.5 = (f32[128]{0:T(128)S(1)}, f32[128]{0:T(128)}, u32[]{:S(2)}) copy-start(f32[128]{0:T(128)} %param.14) | copy-start | bytes 1540
  6.4 7.9 %copy-start.6 = (f32[128]{0:T(128)S(1)}, f32[128]{0:T(128)}, u32[]{:S(2)}) copy-start(f32[128]{0:T(128)} %param.13) | copy-start | bytes 1540
  6.4 10.8 %copy-start.2 = (bf16[1,1,32,4096]{3,2,1,0:T(8,128)(2,1)S(1)}, bf16[1,1,32,4096]{3,2,1,0:T(8,128)(2,1)}, u32[]{:S(2)}) copy-start(bf16[1,1,32,4096]{3,2,1,0:T(8,128)(2,1)} %param.11) | copy-start | bytes 786436
  14.3 7.1 %copy-start.4 = (f32[256]{0:T(256)}, f32[256]{0:T(256)S(1)}, u32[]{:S(2)}) copy-start(f32[256]{0:T(256)S(1)} %add_rsqrt_fusion.1) | copy-start | bytes 3076
  14.8 4.7 %copy-start.1 = (bf16[512,4096]{0,1:T(8,128)(2,1)S(1)}, bf16[512,4096]{0,1:T(8,128)(2,1)}, u32[]{:S(2)}) copy-start(bf16[512,4096]{0,1:T(8,128)(2,1)} %copy.31) | copy-start | bytes 12582916
  21.8 13.8 %slice-start = ((f32[256]{0:T(256)}), f32[128]{0:T(128)S(1)}, s32[]{:S(2)}) async-start(f32[256]{0:T(256)} %copy-done.4), calls=%async_computation.1 | async-start | bytes 1024 | tf_op jit(solution)/shard_map/slice | solution.py:152
  22.7 12.2 %all-to-all-start = ((f32[32,2,128]{2,1,0:T(2,128)}), f32[32,2,128]{2,1,0:T(2,128)S(1)}, u32[]{:S(2)}, u32[]{:S(2)}) async-start(f32[32,2,128]{2,1,0:T(2,128)} %broadcast_in_dim.55), calls=%async_computation | async-start | bytes 65536 | tf_op jit(solution)/shard_map/all_to_all | solution.py:22
  27.7 7.8 %collective-permute-start.4 = (f32[128,192]{0,1:T(8,128)S(1)}, f32[128,192]{0,1:T(8,128)S(1)}, u32[]{:S(2)}, u32[]{:S(2)}) collective-permute-start(f32[128,192]{0,1:T(8,128)S(1)} %pad_maximum_fusion.2), channel_id=1, source_target_pairs={{0,4},{4,0},{8,12},{12,8},{16,20},{20,16},{24,28},{28,24},{1,5},{5... | collective-permute-start | bytes 294920 | tf_op jit(solution)/shard_map/ppermute | solution.py:147
  28.1 4.2 %collective-permute-start.5 = (bf16[128,192]{0,1:T(8,128)(2,1)S(1)}, bf16[128,192]{0,1:T(8,128)(2,1)S(1)}, u32[]{:S(2)}, u32[]{:S(2)}) collective-permute-start(bf16[128,192]{0,1:T(8,128)(2,1)S(1)} %pad_maximum_fusion.4), channel_id=1, source_target_pairs={{0,8},{4,12},{8,0},{12,4},{16,24},{20,28},{24,16},{28,20},{1,9},{5... | collective-permute-start | bytes 147464 | tf_op jit(solution)/shard_map/ppermute | solution.py:147
  29.8 3.9 %collective-permute-start.6 = (bf16[128,192]{0,1:T(8,128)(2,1)S(1)}, bf16[128,192]{0,1:T(8,128)(2,1)S(1)}, u32[]{:S(2)}, u32[]{:S(2)}) collective-permute-start(bf16[128,192]{0,1:T(8,128)(2,1)S(1)} %pad_maximum_fusion.5), channel_id=1, source_target_pairs={{0,12},{4,8},{8,4},{12,0},{16,28},{20,24},{24,20},{28,16},{1,13},{... | collective-permute-start | bytes 147464 | tf_op jit(solution)/shard_map/ppermute | solution.py:147

commit v7 on v6

--- a/solution.py
+++ b/solution.py
@@ -64,6 +64,7 @@
 
     cot_own = cotangent[0, 0]
     cot_pieces = [cot_own] + [xor_permute(cot_own, "tensor", m) for m in range(1, tensor_count)]
+    piece_rows = cot_own.shape[0]
     weight_t = with_layout_constraint(jnp.transpose(out_weight), Layout(major_to_minor=(0, 1)))
     stacked = jnp.stack(cot_pieces, axis=0)
     features = stacked.shape[2]
@@ -79,18 +80,20 @@
         product = lax.optimization_barrier(partial) if product is None else product + partial
     product = product.astype(jnp.bfloat16)
     order = tensor_pos ^ jnp.arange(tensor_count, dtype=jnp.int32)
-    grad_attn = jnp.take(product, order, axis=0).reshape(block_rows, head_count, head_size)
+    grad_attn = product.reshape(block_rows, head_count, head_size)
 
     offsets = jnp.arange(block_rows, dtype=jnp.int32)
     block_order = block_position[0]
     slot_blocks = jnp.take(block_order, context_pos ^ jnp.arange(context_count, dtype=jnp.int32))
-    query_positions = slot_blocks[0] * block_rows + offsets
+    query_positions = (
+        slot_blocks[0] * block_rows + order[:, None] * piece_rows + offsets[None, :piece_rows]
+    ).reshape(-1)
     key_positions = (slot_blocks[:, None] * block_rows + offsets[None, :]).reshape(-1)
     visible = key_positions[None, :] <= query_positions[:, None]
 
-    query_unit, query_inverse = normalize(
-        q_pre[0, 0].reshape(block_rows, head_count, head_size).astype(jnp.float32)
-    )
+    query_rows = q_pre[0, 0].reshape(tensor_count, piece_rows, head_count, head_size)
+    query_rows = jnp.take(query_rows, order, axis=0).reshape(block_rows, head_count, head_size)
+    query_unit, query_inverse = normalize(query_rows.astype(jnp.float32))
     query_norm = (query_unit * q_gain).astype(jnp.bfloat16)
     kv_all = jnp.concatenate(kv_slots, axis=0)
     key_unit, key_inverse = normalize(kv_all[:, :head_size].astype(jnp.float32))
@@ -114,6 +117,7 @@
     value_part = jnp.einsum("hqk,qhd->kd", prob_low, grad_attn, preferred_element_type=jnp.float32)
 
     d_query = norm_backward(grad_qn, query_unit, query_inverse, q_gain).astype(jnp.bfloat16)
+    d_query = jnp.take(d_query.reshape(tensor_count, piece_rows, -1), order, axis=0)
     gain_query_part = jnp.sum(grad_qn * query_unit, axis=(0, 1))
     gain_key_part = jnp.sum(key_part * key_unit, axis=0)
 

time: 37.3 us -> 38.3 us (1.027)
  waiting for transfers between devices: 6.67 us -> 3.91 us
  starting transfers between devices: 11.7 us -> 13 us
  local copies, waits for them, and re-layouts: 11.2 us -> 12.3 us
  other arithmetic: 2 us -> 3.01 us
    ppermute x4, waiting for transfers between devices: 2.47 us -> 0.46 us  [xor_permute(): lax.ppermute(value, axis, [(source, source ^ mask) for source in range(si...]
    all_to_all x1, starting transfers between devices: 4.94 us -> 6.22 us  [all_sum(): pieces = lax.all_to_all(spread, MESH_AXES, 0, 0, tiled=True)]
    another operation x2 -> x4, local copies, waits for them, and re-layouts: 0.01 us -> 0.97 us  [the longest x2 0.96 us: shard_body(): q_pre[0, 0].reshape(tensor_count, piece_rows, head_count, head_size)]
    unnamed x16 -> x13, local copies, waits for them, and re-layouts: 7.36 us -> 6.55 us
    ppermute x3, waiting for transfers between devices: 2.89 us -> 2.14 us  [shard_body(): lax.ppermute(term, ('tensor', 'context'), pairs).astype(jnp.float32)]
    select_n x1 -> x2, other arithmetic: 0.01 us -> 0.75 us  [shard_body(): jnp.take(d_query.reshape(tensor_count, piece_rows, -1), order, axis=0)]
    gather x3 -> x4, local copies, waits for them, and re-layouts: 0.73 us -> 1.27 us  [the longest x3 0.72 us: shard_body(): jnp.take(query_rows, order, axis=0)]
  transfers between devices with their start and end apart: 8 -> 8, of which waited for: 4 -> 4; matrix products, arithmetic and copies ran while one was open for 29% -> 35% of each run, Pallas kernels for 0% -> 0%
where the time goes in v7:
time: 38.3 us; the launch traced here: 37.9 us
  starting transfers between devices  13 us (34%)
  local copies, waits for them, and re-layouts  12.3 us (32%)
  matrix products  4.58 us (12%)
  waiting for transfers between devices  3.91 us (10%)
  other arithmetic  3.01 us (8%)
  between operations  1.11 us (3%)
    unnamed x13, local copies, waits for them, and re-layouts  6.55 us
    all_to_all x1, starting transfers between devices, all_sum(): pieces = lax.all_to_all(spread, MESH_AXES, 0, 0, tiled=True)  6.22 us
    ppermute x4, starting transfers between devices, xor_permute(): lax.ppermute(value, axis, [(source, source ^ mask) for source in range(si...  4.65 us
    dot_general x2, matrix products, shard_body(): lax.dot_general(stacked[:, :, lo:hi], weight_t[lo:hi], (((2,), (0,)), (()...  2.81 us
    ppermute x3, waiting for transfers between devices, shard_body(): lax.ppermute(term, ('tensor', 'context'), pairs).astype(jnp.float32)  2.14 us
    ppermute x3, starting transfers between devices, shard_body(): lax.ppermute(term, ('tensor', 'context'), pairs).astype(jnp.float32)  2.1 us
    all_to_all x1, waiting for transfers between devices, all_sum(): pieces = lax.all_to_all(spread, MESH_AXES, 0, 0, tiled=True)  1.31 us
    another operation x2, local copies, waits for them, and re-layouts, shard_body(): q_pre[0, 0].reshape(tensor_count, piece_rows, head_count, head_size)  0.96 us
  transfers between devices with their start and end apart: 8, of which 4 were waited for; matrix products, arithmetic and copies ran while one was open for 35% of the time, Pallas kernels for 0%

profile of v7, /device:TPU:0, one launch (start us, length us, event | category | flops | bytes accessed | tf_op | source)
XLA Modules:
  0.0 37.9 jit_solution(2522954453764804831)
XLA Ops:
  0.6 3.0 %collective-permute-start.1 = (bf16[32,4096]{1,0:T(8,128)(2,1)}, bf16[32,4096]{1,0:T(8,128)(2,1)S(1)}, u32[]{:S(2)}, u32[]{:S(2)}) collective-permute-start(bf16[32,4096]{1,0:T(8,128)(2,1)} %bitcast.181), channel_id=1, source_target_pairs={{0,8},{8,0},{16,24},{24,16},{1,9},{9,1},{17,25},{25,17},{2,10},{10... | collective-permute-start | bytes 786440 | tf_op jit(solution)/shard_map/ppermute | solution.py:16
  3.7 1.5 %collective-permute-start.2 = (bf16[32,4096]{1,0:T(8,128)(2,1)}, bf16[32,4096]{1,0:T(8,128)(2,1)S(1)}, u32[]{:S(2)}, u32[]{:S(2)}) collective-permute-start(bf16[32,4096]{1,0:T(8,128)(2,1)} %bitcast.182), channel_id=1, source_target_pairs={{0,16},{8,24},{16,0},{24,8},{1,17},{9,25},{17,1},{25,9},{2,18},{10... | collective-permute-start | bytes 786440 | tf_op jit(solution)/shard_map/ppermute | solution.py:16
  5.2 0.8 %constant_dynamic-slice_fusion.1 = (bf16[1,1,128,128]{3,2,1,0:T(8,128)(2,1)S(1)}, bf16[1,1,128,128]{3,2,1,0:T(8,128)(2,1)S(1)}) fusion(bf16[1,1,128,256]{3,2,1,0:T(8,128)(2,1)} %param.10, s32[]{:T(128)S(6)} %select_n.104, bf16[1,1,128,256]{3,2,1,0:T(8,128)(2,1)} %param.9), kind=kLoop, calls=%fused_computation.81 | loop fusion | bytes 131076 | tf_op jit(solution)/shard_map/dynamic_slice | solution.py:59
  6.4 0.9 %reshape_squeeze.3 = bf16[4,32,4,128]{3,2,1,0:T(4,128)(2,1)S(1)} reshape(bf16[1,1,128,512]{3,2,1,0:T(8,128)(2,1)} %param.8) | data formatting | bytes 262144 | tf_op jit(solution)/shard_map/reshape;squeeze | solution.py:94
  7.4 0.6 %gather_fusion.1 = s32[2]{0:T(128)S(1)} fusion(s32[2]{0:T(128)S(1)} %bitcast.172, s32[1024]{0:T(1024)S(1)} %pad_clamp_fusion), kind=kCustom, calls=%fused_computation.1 | custom fusion | bytes 24 | tf_op jit(solution)/shard_map/jit(_take)/gather | solution.py:87
  8.3 0.6 %gather_fusion = bf16[4,32,4,128]{3,1,2,0:T(8,128)(2,1)S(1)} fusion(bf16[4,32,4,128]{3,1,2,0:T(8,128)(2,1)S(1)} %copy.69, s32[1024]{0:T(1024)S(1)} %pad_clamp_fusion.1), kind=kCustom, calls=%fused_computation | custom fusion | bytes 262160 | tf_op jit(solution)/shard_map/jit(_take)/gather | solution.py:95
  8.9 0.2 multiply_reduce_fusion.3
  9.4 6.5 %copy.77 = bf16[512,4096]{0,1:T(8,128)(2,1)} copy(bf16[512,4096]{1,0:T(8,128)(2,1)} %param.12) | data formatting | bytes 8388608 | tf_op args[4]
  16.0 0.1 copy.74
  16.4 0.4 %fusion.65 = (f32[4,128]{1,0:T(4,128)S(1)}, f32[4,128,256]{1,2,0:T(8,128)S(1)}) fusion(pred[128,256]{0,1:T(8,128)(4,1)S(1)} %broadcast_compare_fusion, f32[128]{0:T(128)S(1)} %copy-done.4, f32[256]{0:T(256)S(1)} %add_rsqrt_fusion.1, bf16[256,256]{0,1:T(8,128)(2,1)S(1)} %pad_maximum_fusion.1, f32[128]{0:T(128)S(1)} %copy-done.5, f32[128,4]{0,1:T(4,128)S(1)} %rsqrt.25, ...), kind=kOutput, calls=%fused_computation.155 | convolution fusion | flops 34537728 | bytes 760320 | tf_op jit(solution)/shard_map/sub | solution.py:109
  16.8 0.4 %collective-permute-done.2 = bf16[32,4096]{1,0:T(8,128)(2,1)S(1)} collective-permute-done((bf16[32,4096]{1,0:T(8,128)(2,1)}, bf16[32,4096]{1,0:T(8,128)(2,1)S(1)}, u32[]{:S(2)}, u32[]{:S(2)}) %collective-permute-start.2) | collective-permute-done | bytes 262176 | tf_op jit(solution)/shard_map/ppermute | solution.py:16
  17.3 0.1 pad_maximum_fusion
  17.4 2.4 %fusion.3 = f32[4,32,512]{2,1,0:T(8,128)S(1)} fusion(bf16[4096,512]{1,0:T(8,128)(2,1)} %bitcast.173, bf16[4,32,4096]{2,1,0:T(8,128)(2,1)S(1)} %pad_maximum_fusion), kind=kOutput, calls=%fused_computation.8 | convolution fusion | flops 268435456 | bytes 2883584 | tf_op jit(solution)/shard_map/dot_general | solution.py:74
  19.8 0.5 %fusion.13 = bf16[4,32,512]{2,1,0:T(8,128)(2,1)S(1)} fusion(f32[4,32,512]{2,1,0:T(8,128)S(1)} %fusion.3, bf16[4096,512]{1,0:T(8,128)(2,1)S(1)} %bitcast.174, bf16[4,32,4096]{2,1,0:T(8,128)(2,1)S(1)} %pad_maximum_fusion), kind=kOutput, calls=%fused_computation.21 | convolution fusion | flops 268566528 | bytes 3014656 | tf_op jit(solution)/shard_map/dot_general | solution.py:74
  20.3 0.1 copy.84
  20.4 0.2 convolution_bitcast_fusion
  20.7 0.4 %multiply_reduce_fusion.4 = (f32[128]{0:T(128)S(1)}, f32[256,128]{0,1:T(8,128)S(1)}, f32[256,128]{0,1:T(8,128)S(1)}) fusion(f32[256]{0:T(256)S(1)} %add_rsqrt_fusion.1, bf16[256,256]{0,1:T(8,128)(2,1)S(1)} %pad_maximum_fusion.1, f32[128]{0:T(128)S(1)} %copy-done.5, f32[128,4]{0,1:T(4,128)S(1)} %rsqrt.25, bf16[128,4,128]{0,2,1:T(8,128)(2,1)S(1)} %copy.74, ...), kind=kOutput, calls=%fused_computation.44 | convolution fusion | flops 34931328 | bytes 2564608 | tf_op jit(solution)/shard_map/hqk,qhd->kd/dot_general | solution.py:116
  21.1 0.4 %multiply_reduce_fusion.1 = (f32[128]{0:T(128)S(1)}, f32[128,4]{0,1:T(4,128)S(1)}, f32[128,4,128]{0,2,1:T(8,128)S(1)}) fusion(f32[128,4]{0,1:T(4,128)S(1)} %rsqrt.25, bf16[128,4,128]{0,2,1:T(8,128)(2,1)S(1)} %copy.74, pred[128]{0:T(512)(128)(4,1)S(1)} %broadcast_in_dim.65, f32[128]{0:T(128)S(1)} %copy-done.5, ...), kind=kOutput, calls=%fused_computation.30 | convolution fusion | flops 35127424 | bytes 2567168 | tf_op jit(solution)/shard_map/hqk,kd->qhd/dot_general | solution.py:115
  21.6 0.2 convolution_bitcast_fusion.2
  21.9 0.6 %broadcast_in_dim.74 = f32[32,2,128]{2,1,0:T(2,128)} broadcast(f32[2,128]{1,0:T(2,128)S(1)} %pad_maximum_fusion.6), dimensions={1,2} | broadcast | bytes 33792 | tf_op jit(solution)/shard_map/broadcast_in_dim | solution.py:21
  22.5 6.2 %all-to-all-start = ((f32[32,2,128]{2,1,0:T(2,128)}), f32[32,2,128]{2,1,0:T(2,128)S(1)}, u32[]{:S(2)}, u32[]{:S(2)}) async-start(f32[32,2,128]{2,1,0:T(2,128)} %broadcast_in_dim.74), calls=%async_computation | async-start | bytes 65536 | tf_op jit(solution)/shard_map/all_to_all | solution.py:22
  28.7 0.3 collective-permute-start.4
  29.1 1.7 %collective-permute-start.5 = (bf16[128,192]{0,1:T(8,128)(2,1)S(1)}, bf16[128,192]{0,1:T(8,128)(2,1)S(1)}, u32[]{:S(2)}, u32[]{:S(2)}) collective-permute-start(bf16[128,192]{0,1:T(8,128)(2,1)S(1)} %pad_maximum_fusion.4), channel_id=1, source_target_pairs={{0,8},{4,12},{8,0},{12,4},{16,24},{20,28},{24,16},{28,20},{1,9},{5... | collective-permute-start | bytes 147464 | tf_op jit(solution)/shard_map/ppermute | solution.py:151
  31.0 0.1 copy.81
  31.2 0.6 %gather_fusion.2 = bf16[4,32,512]{2,1,0:T(8,128)(2,1)S(1)} fusion(bf16[4,32,512]{2,1,0:T(8,128)(2,1)S(1)} %reshape.249, s32[1024]{0:T(1024)S(1)} %pad_clamp_fusion.1), kind=kCustom, calls=%fused_computation.2 | custom fusion | bytes 262160 | tf_op jit(solution)/shard_map/jit(_take)/gather | solution.py:120
  31.8 0.7 %broadcast_select_fusion = bf16[1,1,128,512]{3,2,1,0:T(8,128)(2,1)} fusion(bf16[1,1,128,512]{3,2,1,0:T(8,128)(2,1)S(1)} %bitcast.176, pred[128]{0:T(512)(128)(4,1)S(1)} %broadcast_in_dim.65), kind=kLoop, calls=%fused_computation.46 | loop fusion | flops 65536 | bytes 262272 | tf_op jit(solution)/shard_map/jit(_take)/select_n | solution.py:120
  32.5 0.8 %collective-permute-done.5 = bf16[128,192]{0,1:T(8,128)(2,1)S(1)} collective-permute-done((bf16[128,192]{0,1:T(8,128)(2,1)S(1)}, bf16[128,192]{0,1:T(8,128)(2,1)S(1)}, u32[]{:S(2)}, u32[]{:S(2)}) %collective-permute-start.5) | collective-permute-done | bytes 49184 | tf_op jit(solution)/shard_map/ppermute | solution.py:151
  33.3 1.4 %collective-permute-done.6 = bf16[128,192]{0,1:T(8,128)(2,1)S(1)} collective-permute-done((bf16[128,192]{0,1:T(8,128)(2,1)S(1)}, bf16[128,192]{0,1:T(8,128)(2,1)S(1)}, u32[]{:S(2)}, u32[]{:S(2)}) %collective-permute-start.6) | collective-permute-done | bytes 49184 | tf_op jit(solution)/shard_map/ppermute | solution.py:151
  34.7 1.3 %all-to-all-done = f32[32,2,128]{2,1,0:T(2,128)S(1)} async-done(((f32[32,2,128]{2,1,0:T(2,128)}), f32[32,2,128]{2,1,0:T(2,128)S(1)}, u32[]{:S(2)}, u32[]{:S(2)}) %all-to-all-start) | async-done | bytes 32800 | tf_op jit(solution)/shard_map/all_to_all | solution.py:22
  36.0 0.5 %slice_bitcast_fusion.25 = (f32[128]{0:T(128)}, f32[128]{0:T(128)}) fusion(f32[2,128]{1,0:T(2,128)S(1)} %fusion.38), kind=kLoop, calls=%fused_computation.140 | loop fusion | bytes 2048 | tf_op jit(solution)/shard_map/squeeze | solution.py:170
  36.7 0.6 %fusion.29 = bf16[1,1,128,64]{2,3,1,0:T(8,128)(2,1)} fusion(f32[128,128]{0,1:T(8,128)S(1)} %get-tuple-element.13, s32[]{:T(128)S(6)} %select_n.112, f32[128,128]{0,1:T(8,128)S(1)} %get-tuple-element.8, f32[128]{0:T(128)S(1)} %slice-done, f32[128]{0:T(128)S(1)} %broadcast_multiply_fusion.1), kind=kLoop, calls=%fused_computation.71 | loop fusion | flops 32768 | bytes 82948 | tf_op jit(solution)/shard_map/reshape | solution.py:160
  37.3 0.6 %fusion.30 = bf16[1,1,128,64]{2,3,1,0:T(8,128)(2,1)} fusion(f32[128,192]{0,1:T(8,128)S(1)} %convert_element_type.51, f32[128,192]{0,1:T(8,128)S(1)} %convert_element_type.50, f32[128,192]{0,1:T(8,128)S(1)} %collective-permute-done.4, f32[128,128]{0,1:T(8,128)S(1)} %get-tuple-element.16, s32[]{:T(128)S(6)} %select_n.112), kind=kLoop, calls=%fused_computation.72 | loop fusion | flops 32768 | bytes 147460 | tf_op jit(solution)/shard_map/reshape | solution.py:163
  (65 shorter events, 1.7 us)
Async XLA Ops:
  0.6 6.8 %copy-start = (s32[1,2]{1,0:T(1,128)S(1)}, s32[1,2]{1,0:T(1,128)}, u32[]{:S(2)}) copy-start(s32[1,2]{1,0:T(1,128)} %param.15) | copy-start | bytes 28
  0.6 16.2 %collective-permute-start.1 = (bf16[32,4096]{1,0:T(8,128)(2,1)}, bf16[32,4096]{1,0:T(8,128)(2,1)S(1)}, u32[]{:S(2)}, u32[]{:S(2)}) collective-permute-start(bf16[32,4096]{1,0:T(8,128)(2,1)} %bitcast.181), channel_id=1, source_target_pairs={{0,8},{8,0},{16,24},{24,16},{1,9},{9,1},{17,25},{25,17},{2,10},{10... | collective-permute-start | bytes 786440 | tf_op jit(solution)/shard_map/ppermute | solution.py:16
  3.7 13.6 %collective-permute-start.2 = (bf16[32,4096]{1,0:T(8,128)(2,1)}, bf16[32,4096]{1,0:T(8,128)(2,1)S(1)}, u32[]{:S(2)}, u32[]{:S(2)}) collective-permute-start(bf16[32,4096]{1,0:T(8,128)(2,1)} %bitcast.182), channel_id=1, source_target_pairs={{0,16},{8,24},{16,0},{24,8},{1,17},{9,25},{17,1},{25,9},{2,18},{10... | collective-permute-start | bytes 786440 | tf_op jit(solution)/shard_map/ppermute | solution.py:16
  5.2 12.1 %collective-permute-start.3 = (bf16[32,4096]{1,0:T(8,128)(2,1)}, bf16[32,4096]{1,0:T(8,128)(2,1)S(1)}, u32[]{:S(2)}, u32[]{:S(2)}) collective-permute-start(bf16[32,4096]{1,0:T(8,128)(2,1)} %bitcast.183), channel_id=1, source_target_pairs={{0,24},{8,16},{16,8},{24,0},{1,25},{9,17},{17,9},{25,1},{2,26},{10... | collective-permute-start | bytes 786440 | tf_op jit(solution)/shard_map/ppermute | solution.py:16
  6.3 10.0 %collective-permute-start = (bf16[128,256]{0,1:T(8,128)(2,1)S(1)}, bf16[128,256]{0,1:T(8,128)(2,1)S(1)}, u32[]{:S(2)}, u32[]{:S(2)}) collective-permute-start(bf16[128,256]{0,1:T(8,128)(2,1)S(1)} %pad_maximum_fusion.3), channel_id=1, source_target_pairs={{0,4},{4,0},{1,5},{5,1},{2,6},{6,2},{3,7},{7,3},{8,12},{12,8},{9,1... | collective-permute-start | bytes 196616 | tf_op jit(solution)/shard_map/ppermute | solution.py:16
  9.3 7.0 %copy-start.4 = (f32[128]{0:T(128)S(1)}, f32[128]{0:T(128)}, u32[]{:S(2)}) copy-start(f32[128]{0:T(128)} %param.14) | copy-start | bytes 1540
  9.3 7.0 %copy-start.5 = (f32[128]{0:T(128)S(1)}, f32[128]{0:T(128)}, u32[]{:S(2)}) copy-start(f32[128]{0:T(128)} %param.13) | copy-start | bytes 1540
  9.3 7.9 %copy-start.2 = (bf16[1,1,32,4096]{3,2,1,0:T(8,128)(2,1)S(1)}, bf16[1,1,32,4096]{3,2,1,0:T(8,128)(2,1)}, u32[]{:S(2)}) copy-start(bf16[1,1,32,4096]{3,2,1,0:T(8,128)(2,1)} %param.11) | copy-start | bytes 786436
  16.3 4.8 %copy-start.3 = (f32[256]{0:T(256)}, f32[256]{0:T(256)S(1)}, u32[]{:S(2)}) copy-start(f32[256]{0:T(256)S(1)} %add_rsqrt_fusion.1) | copy-start | bytes 3076
  16.8 3.0 %copy-start.1 = (bf16[512,4096]{0,1:T(8,128)(2,1)S(1)}, bf16[512,4096]{0,1:T(8,128)(2,1)}, u32[]{:S(2)}) copy-start(bf16[512,4096]{0,1:T(8,128)(2,1)} %copy.77) | copy-start | bytes 12582916
  21.6 15.1 %slice-start = ((f32[256]{0:T(256)}), f32[128]{0:T(128)S(1)}, s32[]{:S(2)}) async-start(f32[256]{0:T(256)} %copy-done.3), calls=%async_computation.1 | async-start | bytes 1024 | tf_op jit(solution)/shard_map/slice | solution.py:156
  22.5 13.5 %all-to-all-start = ((f32[32,2,128]{2,1,0:T(2,128)}), f32[32,2,128]{2,1,0:T(2,128)S(1)}, u32[]{:S(2)}, u32[]{:S(2)}) async-start(f32[32,2,128]{2,1,0:T(2,128)} %broadcast_in_dim.74), calls=%async_computation | async-start | bytes 65536 | tf_op jit(solution)/shard_map/all_to_all | solution.py:22
  28.7 7.8 %collective-permute-start.4 = (f32[128,192]{0,1:T(8,128)S(1)}, f32[128,192]{0,1:T(8,128)S(1)}, u32[]{:S(2)}, u32[]{:S(2)}) collective-permute-start(f32[128,192]{0,1:T(8,128)S(1)} %pad_maximum_fusion.2), channel_id=1, source_target_pairs={{0,4},{4,0},{8,12},{12,8},{16,20},{20,16},{24,28},{28,24},{1,5},{5... | collective-permute-start | bytes 294920 | tf_op jit(solution)/shard_map/ppermute | solution.py:151
  29.1 4.2 %collective-permute-start.5 = (bf16[128,192]{0,1:T(8,128)(2,1)S(1)}, bf16[128,192]{0,1:T(8,128)(2,1)S(1)}, u32[]{:S(2)}, u32[]{:S(2)}) collective-permute-start(bf16[128,192]{0,1:T(8,128)(2,1)S(1)} %pad_maximum_fusion.4), channel_id=1, source_target_pairs={{0,8},{4,12},{8,0},{12,4},{16,24},{20,28},{24,16},{28,20},{1,9},{5... | collective-permute-start | bytes 147464 | tf_op jit(solution)/shard_map/ppermute | solution.py:151
  30.8 3.9 %collective-permute-start.6 = (bf16[128,192]{0,1:T(8,128)(2,1)S(1)}, bf16[128,192]{0,1:T(8,128)(2,1)S(1)}, u32[]{:S(2)}, u32[]{:S(2)}) collective-permute-start(bf16[128,192]{0,1:T(8,128)(2,1)S(1)} %pad_maximum_fusion.5), channel_id=1, source_target_pairs={{0,12},{4,8},{8,4},{12,0},{16,28},{20,24},{24,20},{28,16},{1,13},{... | collective-permute-start | bytes 147464 | tf_op jit(solution)/shard_map/ppermute | solution.py:151

commit v8 on v6

--- a/solution.py
+++ b/solution.py
@@ -20,10 +20,7 @@
     count = math.prod(lax.axis_size(axis) for axis in MESH_AXES)
     spread = jnp.broadcast_to(value[None], (count,) + value.shape)
     pieces = lax.all_to_all(spread, MESH_AXES, 0, 0, tiled=True)
-    total = pieces[0]
-    for index in range(1, count):
-        total = total + pieces[index]
-    return total
+    return jnp.sum(pieces, axis=0)
 
 
 def normalize(rows_in):

time: 37.3 us -> 37.3 us (level)
  no operation moved by 1% of the time
where the time goes in v8:
time: 37.3 us; the launch traced here: 36.9 us
  starting transfers between devices  11.7 us (31%)
  local copies, waits for them, and re-layouts  11.2 us (30%)
  waiting for transfers between devices  6.67 us (18%)
  matrix products  4.28 us (11%)
  other arithmetic  2.01 us (5%)
  between operations  1.08 us (3%)
    unnamed x16, local copies, waits for them, and re-layouts  7.36 us
    all_to_all x1, starting transfers between devices, all_sum(): pieces = lax.all_to_all(spread, MESH_AXES, 0, 0, tiled=True)  4.94 us
    ppermute x4, starting transfers between devices, xor_permute(): lax.ppermute(value, axis, [(source, source ^ mask) for source in range(si...  4.65 us
    ppermute x3, waiting for transfers between devices, shard_body(): lax.ppermute(term, ('tensor', 'context'), pairs).astype(jnp.float32)  2.89 us
    dot_general x2, matrix products, shard_body(): lax.dot_general(stacked[:, :, lo:hi], weight_t[lo:hi], (((2,), (0,)), (()...  2.51 us
    ppermute x4, waiting for transfers between devices, xor_permute(): lax.ppermute(value, axis, [(source, source ^ mask) for source in range(si...  2.47 us
    ppermute x3, starting transfers between devices, shard_body(): lax.ppermute(term, ('tensor', 'context'), pairs).astype(jnp.float32)  2.1 us
    all_to_all x1, waiting for transfers between devices, all_sum(): pieces = lax.all_to_all(spread, MESH_AXES, 0, 0, tiled=True)  1.31 us
  transfers between devices with their start and end apart: 8, of which 4 were waited for; matrix products, arithmetic and copies ran while one was open for 29% of the time, Pallas kernels for 0%

profile of v8, /device:TPU:0, one launch (start us, length us, event | category | flops | bytes accessed | tf_op | source)
XLA Modules:
  0.0 36.9 jit_solution(6521488808370808296)
XLA Ops:
  0.6 3.0 %collective-permute-start.1 = (bf16[32,4096]{1,0:T(8,128)(2,1)}, bf16[32,4096]{1,0:T(8,128)(2,1)S(1)}, u32[]{:S(2)}, u32[]{:S(2)}) collective-permute-start(bf16[32,4096]{1,0:T(8,128)(2,1)} %bitcast.86), channel_id=1, source_target_pairs={{0,8},{8,0},{16,24},{24,16},{1,9},{9,1},{17,25},{25,17},{2,10},{10... | collective-permute-start | bytes 786440 | tf_op jit(solution)/shard_map/ppermute | solution.py:16
  3.7 1.5 %collective-permute-start.2 = (bf16[32,4096]{1,0:T(8,128)(2,1)}, bf16[32,4096]{1,0:T(8,128)(2,1)S(1)}, u32[]{:S(2)}, u32[]{:S(2)}) collective-permute-start(bf16[32,4096]{1,0:T(8,128)(2,1)} %bitcast.87), channel_id=1, source_target_pairs={{0,16},{8,24},{16,0},{24,8},{1,17},{9,25},{17,1},{25,9},{2,18},{10... | collective-permute-start | bytes 786440 | tf_op jit(solution)/shard_map/ppermute | solution.py:16
  5.2 0.8 %constant_dynamic-slice_fusion.1 = (bf16[1,1,128,128]{3,2,1,0:T(8,128)(2,1)S(1)}, bf16[1,1,128,128]{3,2,1,0:T(8,128)(2,1)S(1)}) fusion(bf16[1,1,128,256]{3,2,1,0:T(8,128)(2,1)} %param.10, s32[]{:T(128)S(6)} %select_n.85, bf16[1,1,128,256]{3,2,1,0:T(8,128)(2,1)} %param.9), kind=kLoop, calls=%fused_computation.79 | loop fusion | bytes 131076 | tf_op jit(solution)/shard_map/dynamic_slice | solution.py:56
  6.0 0.1 copy.53
  6.1 0.1 copy.54
  6.4 6.5 %copy.57 = bf16[512,4096]{0,1:T(8,128)(2,1)} copy(bf16[512,4096]{1,0:T(8,128)(2,1)} %param.12) | data formatting | bytes 8388608 | tf_op args[4]
  13.2 0.6 %gather_fusion = s32[2]{0:T(128)S(1)} fusion(s32[2]{0:T(128)S(1)} %bitcast.73, s32[1024]{0:T(1024)S(1)} %pad_clamp_fusion.1), kind=kCustom, calls=%fused_computation | custom fusion | bytes 24 | tf_op jit(solution)/shard_map/jit(_take)/gather | solution.py:83
  14.1 0.1 broadcast_compare_fusion
  14.4 0.4 %fusion.53 = (f32[4,128]{1,0:T(4,128)S(1)}, f32[4,128,256]{1,2,0:T(8,128)S(1)}) fusion(pred[128,256]{0,1:T(8,128)(4,1)S(1)} %broadcast_compare_fusion, f32[128]{0:T(128)S(1)} %copy-done.5, f32[256]{0:T(256)S(1)} %add_rsqrt_fusion.1, bf16[256,256]{0,1:T(8,128)(2,1)S(1)} %pad_maximum_fusion.1, f32[128,4,128]{0,2,1:T(8,128)S(1)} %bitcast.77, ...), kind=kOutput, calls=%fused_computation.107 | convolution fusion | flops 34406656 | bytes 890880 | tf_op jit(solution)/shard_map/sub | solution.py:103
  14.8 2.5 %collective-permute-done.2 = bf16[32,4096]{1,0:T(8,128)(2,1)S(1)} collective-permute-done((bf16[32,4096]{1,0:T(8,128)(2,1)}, bf16[32,4096]{1,0:T(8,128)(2,1)S(1)}, u32[]{:S(2)}, u32[]{:S(2)}) %collective-permute-start.2) | collective-permute-done | bytes 262176 | tf_op jit(solution)/shard_map/ppermute | solution.py:16
  17.3 0.1 pad_maximum_fusion
  17.4 2.1 %fusion.3 = f32[4,32,512]{2,1,0:T(8,128)S(1)} fusion(bf16[4096,512]{1,0:T(8,128)(2,1)} %bitcast.74, bf16[4,32,4096]{2,1,0:T(8,128)(2,1)S(1)} %pad_maximum_fusion), kind=kOutput, calls=%fused_computation.7 | convolution fusion | flops 268435456 | bytes 2883584 | tf_op jit(solution)/shard_map/dot_general | solution.py:70
  19.5 0.5 %fusion.13 = bf16[4,32,512]{2,1,0:T(8,128)(2,1)S(1)} fusion(f32[4,32,512]{2,1,0:T(8,128)S(1)} %fusion.3, bf16[4096,512]{1,0:T(8,128)(2,1)S(1)} %bitcast.75, bf16[4,32,4096]{2,1,0:T(8,128)(2,1)S(1)} %pad_maximum_fusion), kind=kOutput, calls=%fused_computation.20 | convolution fusion | flops 268566528 | bytes 3014656 | tf_op jit(solution)/shard_map/dot_general | solution.py:70
  20.0 0.6 %gather_fusion.1 = bf16[4,32,512]{2,1,0:T(8,128)(2,1)S(1)} fusion(bf16[4,32,512]{2,1,0:T(8,128)(2,1)S(1)} %fusion.13, s32[1024]{0:T(1024)S(1)} %pad_clamp_fusion), kind=kCustom, calls=%fused_computation.1 | custom fusion | bytes 262160 | tf_op jit(solution)/shard_map/jit(_take)/gather | solution.py:79
  20.6 0.1 copy.58
  20.7 0.3 convolution_bitcast_fusion
  21.0 0.4 %multiply_reduce_fusion.4 = (f32[128]{0:T(128)S(1)}, f32[256,128]{0,1:T(8,128)S(1)}, f32[256,128]{0,1:T(8,128)S(1)}) fusion(f32[256]{0:T(256)S(1)} %add_rsqrt_fusion.1, bf16[256,256]{0,1:T(8,128)(2,1)S(1)} %pad_maximum_fusion.1, f32[4,128,256]{1,2,0:T(8,128)S(1)} %convolution_bitcast_fusion, f32[4,128,256]{1,2,0:T(8,128)S(1)} %get-tuple-element.41, ...), kind=kOutput, calls=%fused_computation.42 | convolution fusion | flops 34800256 | bytes 2695168 | tf_op jit(solution)/shard_map/hqk,qhd->kd/dot_general | solution.py:110
  21.4 0.4 %multiply_reduce_fusion.1 = (f32[128]{0:T(128)S(1)}, f32[128,4]{0,1:T(4,128)S(1)}, f32[128,4,128]{0,2,1:T(8,128)S(1)}) fusion(f32[128,4,128]{0,2,1:T(8,128)S(1)} %bitcast.79, f32[128,4]{0,1:T(4,128)S(1)} %add_rsqrt_fusion, f32[128]{0:T(128)S(1)} %copy-done.6, f32[4,128,256]{1,2,0:T(8,128)S(1)} %convolution_bitcast_fusion, ...), kind=kOutput, calls=%fused_computation.29 | convolution fusion | flops 34996352 | bytes 2697728 | tf_op jit(solution)/shard_map/hqk,kd->qhd/dot_general | solution.py:109
  21.8 0.2 convolution_bitcast_fusion.2
  22.1 0.6 %broadcast_in_dim.55 = f32[32,2,128]{2,1,0:T(2,128)} broadcast(f32[2,128]{1,0:T(2,128)S(1)} %pad_maximum_fusion.6), dimensions={1,2} | broadcast | bytes 33792 | tf_op jit(solution)/shard_map/broadcast_in_dim | solution.py:21
  22.7 4.9 %all-to-all-start = ((f32[32,2,128]{2,1,0:T(2,128)}), f32[32,2,128]{2,1,0:T(2,128)S(1)}, u32[]{:S(2)}, u32[]{:S(2)}) async-start(f32[32,2,128]{2,1,0:T(2,128)} %broadcast_in_dim.55), calls=%async_computation | async-start | bytes 65536 | tf_op jit(solution)/shard_map/all_to_all | solution.py:22
  27.7 0.3 collective-permute-start.4
  28.1 1.7 %collective-permute-start.5 = (bf16[128,192]{0,1:T(8,128)(2,1)S(1)}, bf16[128,192]{0,1:T(8,128)(2,1)S(1)}, u32[]{:S(2)}, u32[]{:S(2)}) collective-permute-start(bf16[128,192]{0,1:T(8,128)(2,1)S(1)} %pad_maximum_fusion.4), channel_id=1, source_target_pairs={{0,8},{4,12},{8,0},{12,4},{16,24},{20,28},{24,16},{28,20},{1,9},{5... | collective-permute-start | bytes 147464 | tf_op jit(solution)/shard_map/ppermute | solution.py:144
  29.9 0.1 multiply_convert_fusion
  30.0 0.8 %copy.65 = bf16[1,1,128,512]{3,2,1,0:T(8,128)(2,1)} copy(bf16[1,1,128,512]{2,3,1,0:T(8,128)(2,1)S(1)} %bitcast.81) | data formatting | bytes 262144
  30.8 1.5 %collective-permute-done.5 = bf16[128,192]{0,1:T(8,128)(2,1)S(1)} collective-permute-done((bf16[128,192]{0,1:T(8,128)(2,1)S(1)}, bf16[128,192]{0,1:T(8,128)(2,1)S(1)}, u32[]{:S(2)}, u32[]{:S(2)}) %collective-permute-start.5) | collective-permute-done | bytes 49184 | tf_op jit(solution)/shard_map/ppermute | solution.py:144
  32.3 1.4 %collective-permute-done.6 = bf16[128,192]{0,1:T(8,128)(2,1)S(1)} collective-permute-done((bf16[128,192]{0,1:T(8,128)(2,1)S(1)}, bf16[128,192]{0,1:T(8,128)(2,1)S(1)}, u32[]{:S(2)}, u32[]{:S(2)}) %collective-permute-start.6) | collective-permute-done | bytes 49184 | tf_op jit(solution)/shard_map/ppermute | solution.py:144
  33.7 1.3 %all-to-all-done = f32[32,2,128]{2,1,0:T(2,128)S(1)} async-done(((f32[32,2,128]{2,1,0:T(2,128)}), f32[32,2,128]{2,1,0:T(2,128)S(1)}, u32[]{:S(2)}, u32[]{:S(2)}) %all-to-all-start) | async-done | bytes 32800 | tf_op jit(solution)/shard_map/all_to_all | solution.py:22
  35.0 0.5 %slice_bitcast_fusion.10 = (f32[128]{0:T(128)}, f32[128]{0:T(128)}) fusion(f32[2,128]{1,0:T(2,128)S(1)} %reduce_sum.89), kind=kLoop, calls=%fused_computation.91 | loop fusion | bytes 2048 | tf_op jit(solution)/shard_map/squeeze | solution.py:163
  35.5 0.1 multiply_reduce_fusion.5
  35.7 0.6 %fusion.31 = bf16[1,1,128,64]{2,3,1,0:T(8,128)(2,1)} fusion(f32[128,128]{0,1:T(8,128)S(1)} %get-tuple-element.33, s32[]{:T(128)S(6)} %select_n.94, f32[128,128]{0,1:T(8,128)S(1)} %get-tuple-element.28, f32[128]{0:T(128)S(1)} %slice-done, f32[128]{0:T(128)S(1)} %broadcast_multiply_fusion.1), kind=kLoop, calls=%fused_computation.70 | loop fusion | flops 32768 | bytes 82948 | tf_op jit(solution)/shard_map/reshape | solution.py:153
  36.3 0.6 %fusion.32 = bf16[1,1,128,64]{2,3,1,0:T(8,128)(2,1)} fusion(f32[128,192]{0,1:T(8,128)S(1)} %convert_element_type.55, f32[128,192]{0,1:T(8,128)S(1)} %convert_element_type.54, f32[128,192]{0,1:T(8,128)S(1)} %collective-permute-done.4, f32[128,128]{0,1:T(8,128)S(1)} %get-tuple-element.36, s32[]{:T(128)S(6)} %select_n.94), kind=kLoop, calls=%fused_computation.71 | loop fusion | flops 32768 | bytes 147460 | tf_op jit(solution)/shard_map/reshape | solution.py:156
  (56 shorter events, 0.9 us)
Async XLA Ops:
  0.6 12.5 %copy-start = (s32[1,2]{1,0:T(1,128)S(1)}, s32[1,2]{1,0:T(1,128)}, u32[]{:S(2)}) copy-start(s32[1,2]{1,0:T(1,128)} %param.15) | copy-start | bytes 28
  0.6 14.2 %collective-permute-start.1 = (bf16[32,4096]{1,0:T(8,128)(2,1)}, bf16[32,4096]{1,0:T(8,128)(2,1)S(1)}, u32[]{:S(2)}, u32[]{:S(2)}) collective-permute-start(bf16[32,4096]{1,0:T(8,128)(2,1)} %bitcast.86), channel_id=1, source_target_pairs={{0,8},{8,0},{16,24},{24,16},{1,9},{9,1},{17,25},{25,17},{2,10},{10... | collective-permute-start | bytes 786440 | tf_op jit(solution)/shard_map/ppermute | solution.py:16
  3.7 13.6 %collective-permute-start.2 = (bf16[32,4096]{1,0:T(8,128)(2,1)}, bf16[32,4096]{1,0:T(8,128)(2,1)S(1)}, u32[]{:S(2)}, u32[]{:S(2)}) collective-permute-start(bf16[32,4096]{1,0:T(8,128)(2,1)} %bitcast.87), channel_id=1, source_target_pairs={{0,16},{8,24},{16,0},{24,8},{1,17},{9,25},{17,1},{25,9},{2,18},{10... | collective-permute-start | bytes 786440 | tf_op jit(solution)/shard_map/ppermute | solution.py:16
  5.2 12.1 %collective-permute-start.3 = (bf16[32,4096]{1,0:T(8,128)(2,1)}, bf16[32,4096]{1,0:T(8,128)(2,1)S(1)}, u32[]{:S(2)}, u32[]{:S(2)}) collective-permute-start(bf16[32,4096]{1,0:T(8,128)(2,1)} %bitcast.88), channel_id=1, source_target_pairs={{0,24},{8,16},{16,8},{24,0},{1,25},{9,17},{17,9},{25,1},{2,26},{10... | collective-permute-start | bytes 786440 | tf_op jit(solution)/shard_map/ppermute | solution.py:16
  6.3 8.0 %collective-permute-start = (bf16[128,256]{0,1:T(8,128)(2,1)S(1)}, bf16[128,256]{0,1:T(8,128)(2,1)S(1)}, u32[]{:S(2)}, u32[]{:S(2)}) collective-permute-start(bf16[128,256]{0,1:T(8,128)(2,1)S(1)} %pad_maximum_fusion.3), channel_id=1, source_target_pairs={{0,4},{4,0},{1,5},{5,1},{2,6},{6,2},{3,7},{7,3},{8,12},{12,8},{9,1... | collective-permute-start | bytes 196616 | tf_op jit(solution)/shard_map/ppermute | solution.py:16
  6.4 7.6 %copy-start.3 = (bf16[1,1,128,512]{3,2,1,0:T(8,128)(2,1)S(1)}, bf16[1,1,128,512]{3,2,1,0:T(8,128)(2,1)}, u32[]{:S(2)}) copy-start(bf16[1,1,128,512]{3,2,1,0:T(8,128)(2,1)} %param.8) | copy-start | bytes 393220
  6.4 7.9 %copy-start.5 = (f32[128]{0:T(128)S(1)}, f32[128]{0:T(128)}, u32[]{:S(2)}) copy-start(f32[128]{0:T(128)} %param.14) | copy-start | bytes 1540
  6.4 7.9 %copy-start.6 = (f32[128]{0:T(128)S(1)}, f32[128]{0:T(128)}, u32[]{:S(2)}) copy-start(f32[128]{0:T(128)} %param.13) | copy-start | bytes 1540
  6.4 10.8 %copy-start.2 = (bf16[1,1,32,4096]{3,2,1,0:T(8,128)(2,1)S(1)}, bf16[1,1,32,4096]{3,2,1,0:T(8,128)(2,1)}, u32[]{:S(2)}) copy-start(bf16[1,1,32,4096]{3,2,1,0:T(8,128)(2,1)} %param.11) | copy-start | bytes 786436
  14.3 7.1 %copy-start.4 = (f32[256]{0:T(256)}, f32[256]{0:T(256)S(1)}, u32[]{:S(2)}) copy-start(f32[256]{0:T(256)S(1)} %add_rsqrt_fusion.1) | copy-start | bytes 3076
  14.8 4.7 %copy-start.1 = (bf16[512,4096]{0,1:T(8,128)(2,1)S(1)}, bf16[512,4096]{0,1:T(8,128)(2,1)}, u32[]{:S(2)}) copy-start(bf16[512,4096]{0,1:T(8,128)(2,1)} %copy.57) | copy-start | bytes 12582916
  21.8 13.8 %slice-start = ((f32[256]{0:T(256)}), f32[128]{0:T(128)S(1)}, s32[]{:S(2)}) async-start(f32[256]{0:T(256)} %copy-done.4), calls=%async_computation.1 | async-start | bytes 1024 | tf_op jit(solution)/shard_map/slice | solution.py:149
  22.7 12.2 %all-to-all-start = ((f32[32,2,128]{2,1,0:T(2,128)}), f32[32,2,128]{2,1,0:T(2,128)S(1)}, u32[]{:S(2)}, u32[]{:S(2)}) async-start(f32[32,2,128]{2,1,0:T(2,128)} %broadcast_in_dim.55), calls=%async_computation | async-start | bytes 65536 | tf_op jit(solution)/shard_map/all_to_all | solution.py:22
  27.7 7.8 %collective-permute-start.4 = (f32[128,192]{0,1:T(8,128)S(1)}, f32[128,192]{0,1:T(8,128)S(1)}, u32[]{:S(2)}, u32[]{:S(2)}) collective-permute-start(f32[128,192]{0,1:T(8,128)S(1)} %pad_maximum_fusion.2), channel_id=1, source_target_pairs={{0,4},{4,0},{8,12},{12,8},{16,20},{20,16},{24,28},{28,24},{1,5},{5... | collective-permute-start | bytes 294920 | tf_op jit(solution)/shard_map/ppermute | solution.py:144
  28.1 4.2 %collective-permute-start.5 = (bf16[128,192]{0,1:T(8,128)(2,1)S(1)}, bf16[128,192]{0,1:T(8,128)(2,1)S(1)}, u32[]{:S(2)}, u32[]{:S(2)}) collective-permute-start(bf16[128,192]{0,1:T(8,128)(2,1)S(1)} %pad_maximum_fusion.4), channel_id=1, source_target_pairs={{0,8},{4,12},{8,0},{12,4},{16,24},{20,28},{24,16},{28,20},{1,9},{5... | collective-permute-start | bytes 147464 | tf_op jit(solution)/shard_map/ppermute | solution.py:144
  29.8 3.9 %collective-permute-start.6 = (bf16[128,192]{0,1:T(8,128)(2,1)S(1)}, bf16[128,192]{0,1:T(8,128)(2,1)S(1)}, u32[]{:S(2)}, u32[]{:S(2)}) collective-permute-start(bf16[128,192]{0,1:T(8,128)(2,1)S(1)} %pad_maximum_fusion.5), channel_id=1, source_target_pairs={{0,12},{4,8},{8,4},{12,0},{16,28},{20,24},{24,20},{28,16},{1,13},{... | collective-permute-start | bytes 147464 | tf_op jit(solution)/shard_map/ppermute | solution.py:144
